TPU v7x, 256 devices: a whole 4x4x8 slice. The times are simulated.
256 devices in a mesh: ctx: 64 (over z, x_hi, y), hd: 4 (over x_lo, core).
Axes of the slice: x: 4 (x_hi: 2, x_lo: 2; x = x_hi * 2 + x_lo), y: 4, z: 8, core: 2. Of those that a mesh axis runs over, the one named last changes fastest.
Arguments:
- tokens: bfloat16 [32768, 4096], P('ctx'), may hold values from -6 to 6
- w_query: bfloat16 [4096, 2048], P('ctx', 'hd'), may hold values from -0.09375 to 0.09375
- w_key: bfloat16 [4096, 2048], P('ctx', 'hd'), may hold values from -0.09375 to 0.09375
- w_value: bfloat16 [4096, 2048], P('ctx', 'hd'), may hold values from -0.09375 to 0.09375
Outputs:
- attended: bfloat16 [32768, 2048], P('ctx', 'hd')
All inputs are finite; a program needn't handle non-finite values.
Results may differ from a plain program's by a relative error of at most 0.0065.
Values may be sent and summed in bfloat16 or wider, within the bound.
No kernel may reach another device: no remote copies, remote signals or barrier semaphores. Data moves between devices by JAX's collectives and lax.ppermute only.
A program may use at most 64 MiB of HBM per device.

v0:
```python
import jax
import jax.numpy as jnp
from jax import lax
from jax.sharding import PartitionSpec as P

DH = 128
BLOCK = 512


epsilon = 1e-06


def carried_in(part, axis, combine, identity):
    place = lax.axis_index(axis)
    gathered = lax.all_gather(part, axis)
    state = jnp.zeros_like(part) + jnp.asarray(identity, part.dtype)

    def one(hop, state):
        return combine(state, lax.dynamic_index_in_dim(gathered, hop, 0, False))

    return lax.fori_loop(0, place, one, state)


def local(tokens, w_query, w_key, w_value):
    tok_rows = tokens.shape[0]
    width_group = w_query.shape[1]
    head_count = width_group // DH
    block_count = tok_rows // BLOCK
    query_full = jnp.dot(
        tokens,
        lax.all_gather(w_query, "ctx", axis=0, tiled=True),
        preferred_element_type=jnp.float32,
    )
    key_full = jnp.dot(
        tokens, lax.all_gather(w_key, "ctx", axis=0, tiled=True), preferred_element_type=jnp.float32
    )
    value_full = jnp.dot(
        tokens,
        lax.all_gather(w_value, "ctx", axis=0, tiled=True),
        preferred_element_type=jnp.float32,
    )
    query_rows = query_full.astype(jnp.bfloat16).reshape(block_count, BLOCK, head_count, DH)
    key_rows = key_full.astype(jnp.bfloat16).reshape(block_count, BLOCK, head_count, DH)
    value_rows = value_full.astype(jnp.bfloat16).reshape(block_count, BLOCK, head_count, DH)
    causal_mask = jnp.tril(jnp.ones((BLOCK, BLOCK), dtype=bool))
    scores = jnp.einsum("bqhd,bkhd->bhqk", query_rows, key_rows, preferred_element_type=jnp.float32)
    scores = jnp.where(causal_mask[None, None], scores, 0.0).astype(jnp.bfloat16)
    local_term = jnp.einsum(
        "bhqk,bkhd->bqhd", scores, value_rows, preferred_element_type=jnp.float32
    )
    block_states = jnp.einsum(
        "bkhd,bkhe->bhde", key_rows, value_rows, preferred_element_type=jnp.float32
    )
    own_total = jnp.sum(block_states, axis=0)

    def add_states(earlier, later_part):
        return earlier + later_part

    prefix_state = carried_in(own_total, "ctx", add_states, jnp.zeros_like(own_total))
    before_blocks = jnp.concatenate([jnp.zeros_like(block_states), block_states[:-1]], axis=0)
    start_states = prefix_state[None] + jnp.cumsum(before_blocks, axis=0)
    carried = jnp.einsum(
        "bqhd,bhde->bqhe",
        query_rows.astype(jnp.float32),
        start_states,
        precision=lax.Precision.HIGHEST,
    )
    attended_raw = carried + local_term
    scale_inv = lax.rsqrt(jnp.mean(attended_raw * attended_raw, axis=-1, keepdims=True) + epsilon)
    return (attended_raw * scale_inv).astype(jnp.bfloat16).reshape(tok_rows, width_group)


def solution(mesh):
    return jax.shard_map(
        local,
        mesh=mesh,
        in_specs=(P("ctx", None), P("ctx", "hd"), P("ctx", "hd"), P("ctx", "hd")),
        out_specs=P("ctx", "hd"),
        check_vma=False,
    )
```

profile of v0, /device:TPU:254, one launch (start us, length us, event | category | flops | bytes accessed | tf_op | source)
XLA Modules:
  0.0 674.8 jit_solution(13655943641388664750)
XLA Ops:
  8.8 126.3 %all-gather.6.cloned.1.call-done = bf16[4096,512]{1,0:T(8,128)(2,1)} async-done(((bf16[64,512]{1,0:T(8,128)(2,1)}), bf16[4096,512]{1,0:T(8,128)(2,1)}) %all-gather.6.cloned.1.call-update) | async-done | bytes 4194320 | tf_op jit(solution)/shard_map/all_gather | solution.py:35
  135.0 5.8 convolution_convert_fusion.2
  140.9 121.8 %all-gather.8.cloned.1.call-done = bf16[4096,512]{1,0:T(8,128)(2,1)} async-done(((bf16[64,512]{1,0:T(8,128)(2,1)}), bf16[4096,512]{1,0:T(8,128)(2,1)}) %all-gather.8.cloned.1.call-update) | async-done | bytes 4194320 | tf_op jit(solution)/shard_map/all_gather | solution.py:39
  262.7 5.8 convolution_convert_fusion.1
  270.5 119.9 %all-gather.10.cloned.1.call-done = bf16[4096,512]{1,0:T(8,128)(2,1)} async-done(((bf16[64,512]{1,0:T(8,128)(2,1)}), bf16[4096,512]{1,0:T(8,128)(2,1)}) %all-gather.10.cloned.1.call-update) | async-done | bytes 4194320 | tf_op jit(solution)/shard_map/all_gather | solution.py:31
  390.4 5.8 convolution_convert_fusion
  396.2 202.4 %all-gather.12.cloned.1.call-done = f32[256,128,128]{2,1,0:T(8,128)} async-done(((f32[4,128,128]{2,1,0:T(8,128)}), f32[256,128,128]{2,1,0:T(8,128)}) %all-gather.12.cloned.1.call-update) | async-done | bytes 16777232 | tf_op jit(solution)/shard_map/all_gather | solution.py:15
  598.6 65.4 %while.10 = (s32[]{:T(128)}, f32[4,128,128]{2,1,0:T(8,128)S(1)}, s32[]{:T(128)}, f32[64,4,128,128]{3,2,1,0:T(8,128)}, s32[]{:T(128)}, /*index=5*/s32[]{:T(128)}, s32[]{:T(128)}) while((s32[]{:T(128)}, f32[4,128,128]{2,1,0:T(8,128)S(1)}, s32[]{:T(128)}, f32[64,4,128,128]{3,2,1,0:T(8,128)}, s32[]{:T(128)}, /*index=5*/s32[]{:T(128)}, ...), condition=%wide.region_1.2_spmd, body=%wide.region_0.1_spmd.sunk | while | flops 65541 | bytes 786547 | solution.py:21
  598.6 1.0 bitcast_add_fusion.2
  599.6 1.0 bitcast_add_fusion.2
  600.7 1.0 bitcast_add_fusion.2
  601.7 1.0 bitcast_add_fusion.2
  602.7 1.0 bitcast_add_fusion.2
  603.8 1.0 bitcast_add_fusion.2
  604.8 1.0 bitcast_add_fusion.2
  605.9 1.0 bitcast_add_fusion.2
  606.9 1.0 bitcast_add_fusion.2
  607.9 1.0 bitcast_add_fusion.2
  609.0 1.0 bitcast_add_fusion.2
  610.0 1.0 bitcast_add_fusion.2
  611.1 1.0 bitcast_add_fusion.2
  612.1 1.0 bitcast_add_fusion.2
  613.1 1.0 bitcast_add_fusion.2
  614.2 1.0 bitcast_add_fusion.2
  615.2 1.0 bitcast_add_fusion.2
  616.2 1.0 bitcast_add_fusion.2
  617.3 1.0 bitcast_add_fusion.2
  618.3 1.0 bitcast_add_fusion.2
  619.4 1.0 bitcast_add_fusion.2
  620.4 1.0 bitcast_add_fusion.2
  621.4 1.0 bitcast_add_fusion.2
  622.5 1.0 bitcast_add_fusion.2
  623.5 1.0 bitcast_add_fusion.2
  624.5 1.0 bitcast_add_fusion.2
  625.6 1.0 bitcast_add_fusion.2
  626.6 1.0 bitcast_add_fusion.2
  627.7 1.0 bitcast_add_fusion.2
  628.7 1.0 bitcast_add_fusion.2
  629.7 1.0 bitcast_add_fusion.2
  630.8 1.0 bitcast_add_fusion.2
  631.8 1.0 bitcast_add_fusion.2
  632.8 1.0 bitcast_add_fusion.2
  633.9 1.0 bitcast_add_fusion.2
  634.9 1.0 bitcast_add_fusion.2
  636.0 1.0 bitcast_add_fusion.2
  637.0 1.0 bitcast_add_fusion.2
  638.0 1.0 bitcast_add_fusion.2
  639.1 1.0 bitcast_add_fusion.2
  640.1 1.0 bitcast_add_fusion.2
  641.1 1.0 bitcast_add_fusion.2
  642.2 1.0 bitcast_add_fusion.2
  643.2 1.0 bitcast_add_fusion.2
  644.3 1.0 bitcast_add_fusion.2
  645.3 1.0 bitcast_add_fusion.2
  646.3 1.0 bitcast_add_fusion.2
  647.4 1.0 bitcast_add_fusion.2
  648.4 1.0 bitcast_add_fusion.2
  649.5 1.0 bitcast_add_fusion.2
  650.5 1.0 bitcast_add_fusion.2
  654.6 1.0 bitcast_add_fusion.2
  657.8 1.0 bitcast_add_fusion.2
  658.8 1.0 bitcast_add_fusion.2
  661.9 1.0 bitcast_add_fusion.2
  664.6 2.5 multiply_reduce_fusion
  (25 shorter events, 14.0 us)
Async XLA Ops:
  6.5 128.5 %all-gather.6.cloned.1.call-start = ((), (), s32[]{:S(2)}) async-start(), calls=%async_computation | async-start | bytes 4259840 | tf_op jit(solution)/shard_map/all_gather | solution.py:35
  7.3 255.4 %all-gather.8.cloned.1.call-start = ((), (), s32[]{:S(2)}) async-start(), calls=%async_computation.1 | async-start | bytes 4259840 | tf_op jit(solution)/shard_map/all_gather | solution.py:39
  8.0 382.4 %all-gather.10.cloned.1.call-start = ((), (), s32[]{:S(2)}) async-start(), calls=%async_computation.2 | async-start | bytes 4259840 | tf_op jit(solution)/shard_map/all_gather | solution.py:31
  8.7 589.8 %all-gather.12.cloned.1.call-start = ((), (), s32[]{:S(2)}) async-start(), calls=%async_computation.3 | async-start | bytes 17039360 | tf_op jit(solution)/shard_map/all_gather | solution.py:15
  268.5 0.8 copy-start
Sparse Core Ops, SparseCore 0:
  10.8 124.1 all-gather.5
  138.5 124.1 all-gather.7
  266.2 124.1 all-gather.9
  393.7 204.8 all-gather.11
where the time goes:
time: 677 us; the launch traced here: 675 us
  waiting for transfers between devices  572 us (84%)
  other arithmetic  63.9 us (9%)
  matrix products  21.6 us (3%)
  between operations  13.2 us (2%)
    all_gather x1, waiting for transfers between devices, carried_in(): gathered = lax.all_gather(part, axis)  202 us
    all_gather x1, waiting for transfers between devices, local(): lax.all_gather(w_key, 'ctx', axis=0, tiled=True)  126 us
    all_gather x1, waiting for transfers between devices, local(): lax.all_gather(w_value, 'ctx', axis=0, tiled=True)  122 us
    all_gather x1, waiting for transfers between devices, local(): lax.all_gather(w_query, 'ctx', axis=0, tiled=True)  120 us
    add x63, other arithmetic, add_states(): return earlier + later_part  63.7 us
  transfers between devices with their start and end apart: 4, of which 4 were waited for; matrix products, arithmetic and copies ran while one was open for 3% of the time, Pallas kernels for 0%

commit v1 on v0

v1 whole, which is shorter than its diff:
```python
import jax
import jax.numpy as jnp
from jax import lax
from jax.sharding import Mesh
from jax.sharding import PartitionSpec as P

DH = 128
BLOCK = 512
epsilon = 1e-06

FINE = (("z", 8), ("xh", 2), ("y", 4))
CTX = tuple(name for name, _ in FINE)
W_ORDER = ("xh", "y", "z")
KV_MODE = "hier"


def fine_mesh(mesh):
    sizes = [n for _, n in FINE]
    devices = mesh.devices.reshape(*sizes, mesh.devices.shape[1])
    return Mesh(devices, (*CTX, "hd"))


def gather_weights(w3):
    g = w3
    for name in W_ORDER:
        g = lax.all_gather(g, name, axis=1, tiled=False)
    got = list(reversed(W_ORDER))
    perm = [0] + [1 + got.index(name) for name in CTX] + [4, 5]
    return g, got


def prefix_over_ctx(state):
    def exclusive(g, name):
        idx = lax.axis_index(name)
        n = g.shape[0]
        mask = (jnp.arange(n) < idx).reshape(n, *([1] * (g.ndim - 1)))
        return jnp.sum(jnp.where(mask, g, 0.0), axis=0), jnp.sum(g, axis=0)

    if KV_MODE == "hier":
        total = state
        out = jnp.zeros_like(state)
        for name in reversed(CTX):
            g = lax.all_gather(total, name)
            before, total = exclusive(g, name)
            out = out + before
        return out
    else:
        g = lax.all_gather(state, CTX)
        return exclusive(g, CTX)[0]


def local(tokens, w_query, w_key, w_value):
    tok_rows, width = tokens.shape
    width_group = w_query.shape[1]
    head_count = width_group // DH
    w3 = jnp.stack([w_query, w_key, w_value])
    g, got = gather_weights(w3)
    sizes = dict(FINE)
    tok = tokens.reshape(tok_rows, *[sizes[n] for n in CTX], w3.shape[1])
    t_labels = "t" + "".join({"z": "a", "xh": "b", "y": "c"}[n] for n in CTX) + "k"
    g_labels = "w" + "".join({"z": "a", "xh": "b", "y": "c"}[n] for n in got) + "kn"
    qkv = jnp.einsum(f"{t_labels},{g_labels}->wtn", tok, g, preferred_element_type=jnp.float32)
    qkv = qkv.astype(jnp.bfloat16).reshape(3, tok_rows, head_count, DH)
    query_rows, key_rows, value_rows = qkv[0], qkv[1], qkv[2]
    causal_mask = jnp.tril(jnp.ones((BLOCK, BLOCK), dtype=bool))
    scores = jnp.einsum("qhd,khd->hqk", query_rows, key_rows, preferred_element_type=jnp.float32)
    scores = jnp.where(causal_mask[None], scores, 0.0).astype(jnp.bfloat16)
    local_term = jnp.einsum("hqk,khd->qhd", scores, value_rows, preferred_element_type=jnp.float32)
    own_total = jnp.einsum("khd,khe->hde", key_rows, value_rows, preferred_element_type=jnp.float32)
    start_state = prefix_over_ctx(own_total)
    carried = jnp.einsum(
        "qhd,hde->qhe",
        query_rows.astype(jnp.float32),
        start_state,
        precision=lax.Precision.HIGHEST,
    )
    attended_raw = carried + local_term
    scale_inv = lax.rsqrt(jnp.mean(attended_raw * attended_raw, axis=-1, keepdims=True) + epsilon)
    return (attended_raw * scale_inv).astype(jnp.bfloat16).reshape(tok_rows, width_group)


def solution(mesh):
    fine = fine_mesh(mesh)
    return jax.shard_map(
        local,
        mesh=fine,
        in_specs=(P(CTX, None), P(CTX, "hd"), P(CTX, "hd"), P(CTX, "hd")),
        out_specs=P(CTX, "hd"),
        check_vma=False,
    )
```

time: 677 us -> 288 us (0.43)
  the two profiles are of different devices: /device:TPU:254 before, /device:TPU:62 now
where the time goes in v1:
time: 288 us; the launch traced here: 286 us
  waiting for transfers between devices  227 us (79%)
  blocking collectives  17.5 us (6%)
  matrix products  16.2 us (6%)
  between operations  13.2 us (5%)
  local copies, waits for them, and re-layouts  7.6 us (3%)
  other arithmetic  5.21 us (2%)
    all_gather x2, waiting for transfers between devices, gather_weights(): g = lax.all_gather(g, name, axis=1, tiled=False)  158 us
    all_gather x2, waiting for transfers between devices, prefix_over_ctx(): g = lax.all_gather(total, name)  68.2 us
    dot_general x1, matrix products, local(): jnp.einsum(f'{t_labels},{g_labels}->wtn', tok, g, preferred_element_type=...  10.9 us
    all_gather x1, blocking collectives, gather_weights(): g = lax.all_gather(g, name, axis=1, tiled=False)  8.92 us
    all_gather x1, blocking collectives, prefix_over_ctx(): g = lax.all_gather(total, name)  8.61 us
    unnamed x1, local copies, waits for them, and re-layouts  6.49 us
  transfers between devices with their start and end apart: 4, of which 4 were waited for; matrix products, arithmetic and copies ran while one was open for 2% of the time, Pallas kernels for 0%

profile of v1, /device:TPU:62, one launch (start us, length us, event | category | flops | bytes accessed | tf_op | source)
XLA Modules:
  0.0 286.4 jit_solution(14048436524449105806)
XLA Ops:
  6.5 0.0 all-gather.11.cloned.1.call-start
  6.5 0.9 pad_maximum_fusion
  7.5 8.9 %all-gather = bf16[3,128,512]{2,1,0:T(8,128)(2,1)} all-gather(bf16[3,64,512]{2,1,0:T(8,128)(2,1)S(1)} %pad_maximum_fusion), channel_id=2, replica_groups=mesh['z'=8,'xh'=2,'y'=4,'hd'=4] {'xh'}, dimensions={1}, use_global_device_ids=true | all-gather | bytes 589824 | tf_op jit(solution)/shard_map/all_gather | solution.py:26
  16.4 0.0 all-gather.11.cloned.1.call-update
  16.4 0.0 all-gather.13.cloned.1.call-start
  16.5 30.4 %all-gather.11.cloned.1.call-done = bf16[3,8,64,512]{3,2,1,0:T(8,128)(2,1)} async-done(((bf16[3,2,64,512]{3,2,1,0:T(8,128)(2,1)}), bf16[3,8,64,512]{3,2,1,0:T(8,128)(2,1)}) %all-gather.11.cloned.1.call-update) | async-done | bytes 1572880 | tf_op jit(solution)/shard_map/all_gather | solution.py:26
  46.8 0.0 all-gather.13.cloned.1.call-update
  46.8 0.0 all-gather.15.cloned.1.call-start
  46.9 6.5 %copy.14 = bf16[512,4096]{0,1:T(8,128)(2,1)} copy(bf16[512,4096]{1,0:T(8,128)(2,1)} %param.4) | data formatting | bytes 8388608 | tf_op args[0]
  53.4 127.9 %all-gather.13.cloned.1.call-done = bf16[3,32,2,64,512]{4,3,2,1,0:T(8,128)(2,1)} async-done(((bf16[3,4,2,64,512]{4,3,2,1,0:T(8,128)(2,1)}), bf16[3,32,2,64,512]{4,3,2,1,0:T(8,128)(2,1)}) %all-gather.13.cloned.1.call-update) | async-done | bytes 12582928 | tf_op jit(solution)/shard_map/all_gather | solution.py:26
  181.3 10.9 %fusion.6 = bf16[3,512,512]{1,2,0:T(8,128)(2,1)S(1)} fusion(bf16[3,8,4,2,64,512]{5,4,3,2,1,0:T(8,128)(2,1)} %bitcast.58, bf16[512,8,2,4,64,1]{0,4,3,2,1,5:T(8,128)(2,1)} %bitcast.42), kind=kOutput, calls=%fused_computation.7 | convolution fusion | flops 6443237376 | bytes 18350080 | tf_op jit(solution)/shard_map/tabck,wacbkn->wtn/dot_general | solution.py:62
  192.2 0.1 fusion.15
  192.3 1.0 fusion.16
  193.3 0.0 all-gather.15.cloned.1.call-update
  193.3 0.0 all-gather.17.cloned.1.call-start
  193.4 25.9 %all-gather.15.cloned.1.call-done = f32[16,128,128]{2,1,0:T(8,128)} async-done(((f32[4,128,128]{2,1,0:T(8,128)}), f32[16,128,128]{2,1,0:T(8,128)}) %all-gather.15.cloned.1.call-update) | async-done | bytes 1048592 | tf_op jit(solution)/shard_map/all_gather | solution.py:43
  219.3 1.4 select_reduce_fusion.1
  220.8 8.6 %all-gather.4 = f32[8,128,128]{2,1,0:T(8,128)S(1)} all-gather(f32[4,128,128]{2,1,0:T(8,128)S(1)} %get-tuple-element.6), channel_id=6, replica_groups=mesh['z'=8,'xh'=2,'y'=4,'hd'=4] {'xh'}, dimensions={0}, use_global_device_ids=true | all-gather | bytes 786432 | tf_op jit(solution)/shard_map/all_gather | solution.py:43
  229.4 0.8 select_reduce_fusion.2
  230.1 0.0 all-gather.17.cloned.1.call-update
  230.2 0.1 iota_compare_fusion
  230.3 42.3 %all-gather.17.cloned.1.call-done = f32[32,128,128]{2,1,0:T(8,128)} async-done(((f32[4,128,128]{2,1,0:T(8,128)}), f32[32,128,128]{2,1,0:T(8,128)}) %all-gather.17.cloned.1.call-update) | async-done | bytes 2097168 | tf_op jit(solution)/shard_map/all_gather | solution.py:43
  272.6 1.9 select_reduce_fusion
  274.4 1.6 fusion.11
  276.0 2.6 multiply_reduce_fusion
  278.7 0.1 multiply_convert_fusion
  278.8 1.0 copy.22
  (4 shorter events, 0.0 us)
Async XLA Ops:
  6.5 40.3 %all-gather.11.cloned.1.call-start = ((), (), s32[]{:S(2)}) async-start(), calls=%async_computation | async-start | bytes 1966080 | tf_op jit(solution)/shard_map/all_gather | solution.py:26
  16.4 164.9 %all-gather.13.cloned.1.call-start = ((), (), s32[]{:S(2)}) async-start(), calls=%async_computation.1 | async-start | bytes 14155776 | tf_op jit(solution)/shard_map/all_gather | solution.py:26
  46.8 172.5 %all-gather.15.cloned.1.call-start = ((), (), s32[]{:S(2)}) async-start(), calls=%async_computation.2 | async-start | bytes 1310720 | tf_op jit(solution)/shard_map/all_gather | solution.py:43
  193.3 79.2 %all-gather.17.cloned.1.call-start = ((), (), s32[]{:S(2)}) async-start(), calls=%async_computation.3 | async-start | bytes 2359296 | tf_op jit(solution)/shard_map/all_gather | solution.py:43
Sparse Core Ops, SparseCore 0:
  16.5 30.2 all-gather.10
  48.6 132.6 all-gather.12
  193.4 25.8 all-gather.14
  230.3 42.2 all-gather.16

commit v2 on v1

v2 whole, which is shorter than its diff:
```python
import jax
import jax.numpy as jnp
from jax import lax
from jax.sharding import Mesh
from jax.sharding import PartitionSpec as P

DH = 128
BLOCK = 512
epsilon = 1e-06

FINE = (("z", 8), ("xh", 2), ("y", 4))
CTX = tuple(name for name, _ in FINE)
SIZES = dict(FINE)


def fine_mesh(mesh):
    devices = mesh.devices.reshape(*SIZES.values(), mesh.devices.shape[1])
    return Mesh(devices, (*CTX, "hd"))


def ring_values(x, name, n):
    right = [(j, (j + 1) % n) for j in range(n)]
    left = [(j, (j - 1) % n) for j in range(n)]
    got = []
    r = l = x
    for k in range(1, n // 2 + 1):
        r = lax.ppermute(r, name, right)
        got.append((k, r))
        if k < n - k:
            l = lax.ppermute(l, name, left)
            got.append((n - k, l))
    return got


def ring_gather(x, name, axis):
    n = SIZES[name]
    by_ahead = {0: x}
    for k, v in ring_values(x, name, n):
        by_ahead[(n - k) % n] = v
    stacked = jnp.stack([by_ahead[m] for m in range(n)], axis=axis)
    return jnp.roll(stacked, lax.axis_index(name), axis=axis)


def exclusive_and_total(x, name):
    n = SIZES[name]
    idx = lax.axis_index(name)
    before = jnp.zeros_like(x)
    total = x
    for k, v in ring_values(x, name, n):
        before = before + jnp.where(k <= idx, v, 0.0)
        total = total + v
    return before, total


def exclusive_scan(x, name):
    n = SIZES[name]
    e = lax.ppermute(x, name, [(j, j + 1) for j in range(n - 1)])
    d = 1
    while d < n:
        e = e + lax.ppermute(e, name, [(j, j + d) for j in range(n - d)])
        d *= 2
    return e


def prefix_over_ctx(state):
    before_y, total_y = exclusive_and_total(state, "y")
    before_x, total_xy = exclusive_and_total(total_y, "xh")
    return exclusive_scan(total_xy, "z") + before_x + before_y


def project(tokens, ws, split):
    w = jnp.stack(ws)
    g = lax.all_gather(w, "xh", axis=1)
    a, b = g[..., :split], g[..., split:]
    a = ring_gather(a, "y", axis=1)
    b = lax.all_gather(b, "z", axis=1)
    a = lax.all_gather(a, "z", axis=1)
    b = ring_gather(b, "y", axis=1)
    t = tokens.shape[0]
    k = w.shape[1]
    tok = tokens.reshape(t, SIZES["z"], SIZES["xh"], SIZES["y"], k)
    tok_a = tok.transpose(0, 1, 3, 2, 4).reshape(t, -1)
    tok_b = tok.transpose(0, 3, 1, 2, 4).reshape(t, -1)
    out_a = jnp.einsum("tk,wkn->wtn", tok_a, a.reshape(len(ws), -1, split), preferred_element_type=jnp.float32)
    out_b = jnp.einsum("tk,wkn->wtn", tok_b, b.reshape(len(ws), -1, w.shape[2] - split), preferred_element_type=jnp.float32)
    return jnp.concatenate([out_a, out_b], axis=-1)


def local(tokens, w_query, w_key, w_value):
    tok_rows = tokens.shape[0]
    width_group = w_query.shape[1]
    head_count = width_group // DH
    split = width_group // 2
    kv = project(tokens, [w_key, w_value], split).astype(jnp.bfloat16).reshape(2, tok_rows, head_count, DH)
    key_rows, value_rows = kv[0], kv[1]
    own_total = jnp.einsum("khd,khe->hde", key_rows, value_rows, preferred_element_type=jnp.float32)
    start_state = prefix_over_ctx(own_total)
    query_rows = project(tokens, [w_query], split).astype(jnp.bfloat16).reshape(tok_rows, head_count, DH)
    causal_mask = jnp.tril(jnp.ones((BLOCK, BLOCK), dtype=bool))
    scores = jnp.einsum("qhd,khd->hqk", query_rows, key_rows, preferred_element_type=jnp.float32)
    scores = jnp.where(causal_mask[None], scores, 0.0).astype(jnp.bfloat16)
    local_term = jnp.einsum("hqk,khd->qhd", scores, value_rows, preferred_element_type=jnp.float32)
    carried = jnp.einsum(
        "qhd,hde->qhe",
        query_rows.astype(jnp.float32),
        start_state,
        precision=lax.Precision.HIGHEST,
    )
    attended_raw = carried + local_term
    scale_inv = lax.rsqrt(jnp.mean(attended_raw * attended_raw, axis=-1, keepdims=True) + epsilon)
    return (attended_raw * scale_inv).astype(jnp.bfloat16).reshape(tok_rows, width_group)


def solution(mesh):
    fine = fine_mesh(mesh)
    return jax.shard_map(
        local,
        mesh=fine,
        in_specs=(P(CTX, None), P(CTX, "hd"), P(CTX, "hd"), P(CTX, "hd")),
        out_specs=P(CTX, "hd"),
        check_vma=False,
    )
```

time: 288 us -> 232 us (0.81)
  the two profiles are of different devices: /device:TPU:62 before, /device:TPU:192 now
where the time goes in v2:
time: 232 us; the launch traced here: 231 us
  waiting for transfers between devices  92.2 us (40%)
  blocking collectives  38.5 us (17%)
  local copies, waits for them, and re-layouts  36.9 us (16%)
  starting transfers between devices  29.3 us (13%)
  matrix products  18.1 us (8%)
  between operations  13.6 us (6%)
  other arithmetic  2.76 us (1%)
    ppermute x11, waiting for transfers between devices, ring_values(): r = lax.ppermute(r, name, right)  54 us
    ppermute x3, waiting for transfers between devices, exclusive_scan(): e = e + lax.ppermute(e, name, [(j, j + d) for j in range(n - d)])  29.3 us
    all_gather x1, blocking collectives, project(): b = lax.all_gather(b, 'z', axis=1)  24.6 us
    unnamed x51, local copies, waits for them, and re-layouts  21.9 us
    all_gather x2, blocking collectives, project(): g = lax.all_gather(w, 'xh', axis=1)  13.8 us
    ppermute x11, starting transfers between devices, ring_values(): r = lax.ppermute(r, name, right)  11.9 us
    dot_general x2, matrix products, project(): jnp.einsum('tk,wkn->wtn', tok_a, a.reshape(len(ws), -1, split), preferred...  10.1 us
    ppermute x5, starting transfers between devices, ring_values(): l = lax.ppermute(l, name, left)  8.13 us
  transfers between devices with their start and end apart: 23, of which 13 were waited for; matrix products, arithmetic and copies ran while one was open for 23% of the time, Pallas kernels for 0%

profile of v2, /device:TPU:192, one launch (start us, length us, event | category | flops | bytes accessed | tf_op | source)
XLA Modules:
  0.0 231.3 jit_solution(14087807475237284064)
XLA Ops:
  6.5 0.9 pad_maximum_fusion.2
  7.5 7.4 %all-gather = bf16[2,128,512]{2,1,0:T(8,128)(2,1)S(1)} all-gather(bf16[2,64,512]{2,1,0:T(8,128)(2,1)S(1)} %pad_maximum_fusion.2), channel_id=2, replica_groups=mesh['z'=8,'xh'=2,'y'=4,'hd'=4] {'xh'}, dimensions={1}, use_global_device_ids=true | all-gather | bytes 393216 | tf_op jit(solution)/shard_map/all_gather | solution.py:73
  14.9 0.7 fusion.51
  15.5 3.0 %collective-permute-start = (bf16[2,2,64,256]{3,2,1,0:T(8,128)(2,1)S(1)}, bf16[2,2,64,256]{3,2,1,0:T(8,128)(2,1)S(1)}, u32[]{:S(2)}, u32[]{:S(2)}) collective-permute-start(bf16[2,2,64,256]{3,2,1,0:T(8,128)(2,1)S(1)} %get-tuple-element.7), channel_id=1, source_target_pairs={{0,12},{4,0},{8,4},{12,8},{1,13},{5,1},{9,5},{13,9},{2,14},{6,2},{... | collective-permute-start | bytes 393224 | tf_op jit(solution)/shard_map/ppermute | solution.py:30
  18.7 6.1 %collective-permute-done.1 = bf16[2,2,64,256]{3,2,1,0:T(8,128)(2,1)S(1)} collective-permute-done((bf16[2,2,64,256]{3,2,1,0:T(8,128)(2,1)S(1)}, bf16[2,2,64,256]{3,2,1,0:T(8,128)(2,1)S(1)}, u32[]{:S(2)}, u32[]{:S(2)}) %collective-permute-start.1) | collective-permute-done | bytes 131104 | tf_op jit(solution)/shard_map/ppermute | solution.py:27
  24.7 6.2 %collective-permute-done.2 = bf16[2,2,64,256]{3,2,1,0:T(8,128)(2,1)S(1)} collective-permute-done((bf16[2,2,64,256]{3,2,1,0:T(8,128)(2,1)S(1)}, bf16[2,2,64,256]{3,2,1,0:T(8,128)(2,1)S(1)}, u32[]{:S(2)}, u32[]{:S(2)}) %collective-permute-start.2) | collective-permute-done | bytes 131104 | tf_op jit(solution)/shard_map/ppermute | solution.py:27
  31.0 0.8 constant_dynamic-slice_fusion.2
  31.9 6.4 %all-gather.3 = bf16[128,512]{1,0:T(8,128)(2,1)S(1)} all-gather(bf16[64,512]{1,0:T(8,128)(2,1)S(1)} %copy-done.10), channel_id=5, replica_groups=mesh['z'=8,'xh'=2,'y'=4,'hd'=4] {'xh'}, dimensions={0}, use_global_device_ids=true | all-gather | bytes 196608 | tf_op jit(solution)/shard_map/all_gather | solution.py:73
  38.4 24.6 %all-gather.5 = bf16[8,2,64,256]{3,2,1,0:T(8,128)(2,1)S(1)} all-gather(bf16[1,2,64,256]{3,2,1,0:T(8,128)(2,1)S(1)} %get-tuple-element.10), channel_id=7, replica_groups=mesh['z'=8,'xh'=2,'y'=4,'hd'=4] {'z'}, dimensions={0}, use_global_device_ids=true | all-gather | bytes 589824 | tf_op jit(solution)/shard_map/all_gather | solution.py:76
  63.0 2.0 collective-permute-start.18
  65.1 1.2 collective-permute-start.14
  66.3 0.8 collective-permute-start.15
  67.1 6.5 %copy.64 = bf16[512,4096]{0,1:T(8,128)(2,1)} copy(bf16[512,4096]{1,0:T(8,128)(2,1)} %param.4) | data formatting | bytes 8388608 | tf_op args[0]
  73.5 4.9 %copy.73 = bf16[512,4,8,2,64]{0,4,3,2,1:T(8,128)(2,1)} copy(bf16[512,4,8,2,64]{0,4,1,3,2:T(8,128)(2,1)} %bitcast.111) | data formatting | bytes 8388608 | tf_op jit(solution)/shard_map/transpose | solution.py:83
  78.5 2.5 %copy.72 = bf16[512,8,4,2,64]{0,4,3,2,1:T(8,128)(2,1)} copy(bf16[512,8,4,2,64]{0,4,2,3,1:T(8,128)(2,1)S(1)} %bitcast.113) | data formatting | bytes 8388608 | tf_op jit(solution)/shard_map/transpose | solution.py:82
  80.9 0.6 constant_dynamic-update-slice_fusion.7
  81.6 0.8 bitcast_dynamic-update-slice_fusion.12
  82.4 0.8 iota_compare_fusion
  83.2 2.5 %copy.66 = bf16[2,8,2,64,256]{4,3,2,0,1:T(8,128)(2,1)} copy(bf16[2,8,2,64,256]{4,3,2,1,0:T(8,128)(2,1)} %bitcast.115) | data formatting | bytes 2097152 | tf_op jit(solution)/shard_map/all_gather | solution.py:76
  86.3 0.6 constant_dynamic-update-slice_fusion.6
  86.9 2.4 %collective-permute-done.16 = bf16[1,2,64,256]{3,2,1,0:T(8,128)(2,1)S(1)} collective-permute-done((bf16[1,2,64,256]{3,2,1,0:T(8,128)(2,1)S(1)}, bf16[1,2,64,256]{3,2,1,0:T(8,128)(2,1)S(1)}, u32[]{:S(2)}, u32[]{:S(2)}) %collective-permute-start.16) | collective-permute-done | bytes 65568 | tf_op jit(solution)/shard_map/ppermute | solution.py:27
  89.3 0.6 constant_dynamic-update-slice_fusion.5
  90.0 0.6 constant_dynamic-update-slice_fusion.4
  90.6 0.6 constant_dynamic-update-slice_fusion.3
  91.2 1.2 collective-permute-start.3
  92.4 0.6 constant_dynamic-update-slice_fusion.2
  93.0 16.2 %collective-permute-done.4 = bf16[2,8,2,64,256]{4,3,2,0,1:T(8,128)(2,1)S(1)} collective-permute-done((bf16[2,8,2,64,256]{4,3,2,0,1:T(8,128)(2,1)}, bf16[2,8,2,64,256]{4,3,2,0,1:T(8,128)(2,1)S(1)}, u32[]{:S(2)}, u32[]{:S(2)}) %collective-permute-start.4) | collective-permute-done | bytes 1048608 | tf_op jit(solution)/shard_map/ppermute | solution.py:27
  109.2 1.3 collective-permute-start.5
  110.6 0.6 constant_dynamic-update-slice_fusion.1
  111.2 0.6 constant_dynamic-update-slice_fusion
  111.8 1.7 constant_dynamic-slice_fusion.1
  113.5 2.6 %collective-permute-start.19 = (bf16[1,8,2,64,256]{4,3,2,1,0:T(8,128)(2,1)S(1)}, bf16[1,8,2,64,256]{4,3,2,1,0:T(8,128)(2,1)}, u32[]{:S(2)}, u32[]{:S(2)}) collective-permute-start(bf16[1,8,2,64,256]{4,3,2,1,0:T(8,128)(2,1)S(1)} %collective-permute-done.18), channel_id=1, source_target_pairs={{0,4},{4,8},{8,12},{12,0},{1,5},{5,9},{9,13},{13,1},{2,6},{6,10},{... | collective-permute-start | bytes 1572872 | tf_op jit(solution)/shard_map/ppermute | solution.py:27
  116.3 1.3 bitcast_dynamic-update-slice_fusion.4
  117.6 13.5 %collective-permute-done.5 = bf16[2,8,2,64,256]{4,3,2,0,1:T(8,128)(2,1)} collective-permute-done((bf16[2,8,2,64,256]{4,3,2,0,1:T(8,128)(2,1)S(1)}, bf16[2,8,2,64,256]{4,3,2,0,1:T(8,128)(2,1)}, u32[]{:S(2)}, u32[]{:S(2)}) %collective-permute-start.5) | collective-permute-done | bytes 1048608 | tf_op jit(solution)/shard_map/ppermute | solution.py:27
  131.1 1.3 bitcast_dynamic-update-slice_fusion.2
  132.6 1.5 bitcast_dynamic-update-slice_fusion.5
  134.1 1.4 bitcast_dynamic-update-slice_fusion.3
  135.6 2.4 %fusion.26 = bf16[2,512,256]{1,2,0:T(8,128)(2,1)S(1)} fusion(bf16[512,4,8,2,64,1]{0,4,1,3,2,5:T(8,128)(2,1)S(1)} %bitcast.114, bf16[2,8,8,2,64,256]{5,4,3,0,2,1:T(8,128)(2,1)S(1)} %bitcast_dynamic-update-slice_fusion.1, s32[]{:T(128)S(6)} %select_n.64), kind=kOutput, calls=%fused_computation.14 | convolution fusion | flops 2147745792 | bytes 8912900 | tf_op jit(solution)/shard_map/tk,wkn->wtn/dot_general | solution.py:85
  138.0 6.0 %fusion.23 = bf16[2,512,256]{1,2,0:T(8,128)(2,1)S(1)} fusion(bf16[2,8,4,2,64,256]{5,4,3,0,2,1:T(8,128)(2,1)} %bitcast.138, bf16[512,8,4,2,64,1]{0,4,2,3,1,5:T(8,128)(2,1)} %bitcast.112), kind=kOutput, calls=%fused_computation.13 | convolution fusion | flops 2147745792 | bytes 8912896 | tf_op jit(solution)/shard_map/tk,wkn->wtn/dot_general | solution.py:84
  144.3 0.7 collective-permute-start.6
  145.0 1.1 bitcast_dynamic-update-slice_fusion.10
  146.1 1.1 bitcast_dynamic-update-slice_fusion.8
  147.2 2.7 %collective-permute-start.7 = (f32[4,128,128]{2,1,0:T(8,128)S(1)}, f32[4,128,128]{2,1,0:T(8,128)S(1)}, u32[]{:S(2)}, u32[]{:S(2)}) collective-permute-start(f32[4,128,128]{2,1,0:T(8,128)S(1)} %fusion.53), channel_id=1, source_target_pairs={{0,12},{4,0},{8,4},{12,8},{1,13},{5,1},{9,5},{13,9},{2,14},{6,2},{... | collective-permute-start | bytes 786440 | tf_op jit(solution)/shard_map/ppermute | solution.py:30
  149.9 2.1 collective-permute-done.6
  152.1 2.1 collective-permute-done.7
  154.2 5.3 %collective-permute-done.8 = f32[4,128,128]{2,1,0:T(8,128)S(1)} collective-permute-done((f32[4,128,128]{2,1,0:T(8,128)S(1)}, f32[4,128,128]{2,1,0:T(8,128)S(1)}, u32[]{:S(2)}, u32[]{:S(2)}) %collective-permute-start.8) | collective-permute-done | bytes 262176 | tf_op jit(solution)/shard_map/ppermute | solution.py:27
  159.7 3.8 %collective-permute-start.9 = (f32[4,128,128]{2,1,0:T(8,128)S(1)}, f32[4,128,128]{2,1,0:T(8,128)S(1)}, u32[]{:S(2)}, u32[]{:S(2)}) collective-permute-start(f32[4,128,128]{2,1,0:T(8,128)S(1)} %add_add_fusion), channel_id=1, source_target_pairs={{0,16},{16,0},{1,17},{17,1},{2,18},{18,2},{3,19},{19,3},{4,20},{20... | collective-permute-start | bytes 786440 | tf_op jit(solution)/shard_map/ppermute | solution.py:27
  163.5 1.1 bitcast_dynamic-update-slice_fusion.11
  164.5 1.1 bitcast_dynamic-update-slice_fusion.9
  165.6 2.2 collective-permute-done.9
  167.8 4.2 %collective-permute-start.10 = (f32[4,128,128]{2,1,0:T(8,128)S(1)}, f32[4,128,128]{2,1,0:T(8,128)S(1)}, u32[]{:S(2)}, u32[]{:S(2)}) collective-permute-start(f32[4,128,128]{2,1,0:T(8,128)S(1)} %add.77), channel_id=1, source_target_pairs={{0,32},{32,64},{64,96},{96,128},{128,160},{160,192},{192,224},{1,3... | collective-permute-start | bytes 786440 | tf_op jit(solution)/shard_map/ppermute | solution.py:57
  172.4 6.7 %collective-permute-done.10 = f32[4,128,128]{2,1,0:T(8,128)S(1)} collective-permute-done((f32[4,128,128]{2,1,0:T(8,128)S(1)}, f32[4,128,128]{2,1,0:T(8,128)S(1)}, u32[]{:S(2)}, u32[]{:S(2)}) %collective-permute-start.10) | collective-permute-done | bytes 262176 | tf_op jit(solution)/shard_map/ppermute | solution.py:57
  179.1 2.4 %collective-permute-start.11 = (f32[4,128,128]{2,1,0:T(8,128)S(1)}, f32[4,128,128]{2,1,0:T(8,128)S(1)}, u32[]{:S(2)}, u32[]{:S(2)}) collective-permute-start(f32[4,128,128]{2,1,0:T(8,128)S(1)} %collective-permute-done.10), channel_id=1, source_target_pairs={{0,32},{32,64},{64,96},{96,128},{128,160},{160,192},{192,224},{1,3... | collective-permute-start | bytes 786440 | tf_op jit(solution)/shard_map/ppermute | solution.py:60
  181.5 1.3 fusion.32
  182.8 6.3 %collective-permute-done.11 = f32[4,128,128]{2,1,0:T(8,128)S(1)} collective-permute-done((f32[4,128,128]{2,1,0:T(8,128)S(1)}, f32[4,128,128]{2,1,0:T(8,128)S(1)}, u32[]{:S(2)}, u32[]{:S(2)}) %collective-permute-start.11) | collective-permute-done | bytes 262176 | tf_op jit(solution)/shard_map/ppermute | solution.py:60
  189.1 1.3 collective-permute-start.12
  190.4 4.1 %fusion.31 = bf16[1,512,256]{1,2,0:T(8,128)(2,1)S(1)} fusion(bf16[4096,256]{1,0:T(8,128)(2,1)} %bitcast.139, bf16[512,4096]{0,1:T(8,128)(2,1)} %bitcast.120), kind=kOutput, calls=%fused_computation.17 | convolution fusion | flops 1073872896 | bytes 6553600 | tf_op jit(solution)/shard_map/tk,wkn->wtn/dot_general | solution.py:84
  194.6 11.3 %collective-permute-done.12 = f32[4,128,128]{2,1,0:T(8,128)S(1)} collective-permute-done((f32[4,128,128]{2,1,0:T(8,128)S(1)}, f32[4,128,128]{2,1,0:T(8,128)S(1)}, u32[]{:S(2)}, u32[]{:S(2)}) %collective-permute-start.12) | collective-permute-done | bytes 262176 | tf_op jit(solution)/shard_map/ppermute | solution.py:60
  205.9 0.7 add.79
  206.6 1.3 collective-permute-start.13
  207.9 2.3 %fusion.5 = f32[4,128,512]{2,1,0:T(8,128)S(1)} fusion(bf16[512,4,128]{0,2,1:T(8,128)(2,1)S(1)} %bitcast.130, bf16[512,4,128]{0,2,1:T(8,128)(2,1)S(1)} %bitcast.131, bf16[512,4,128]{0,2,1:T(8,128)(2,1)S(1)} %bitcast.128, pred[512,512]{1,0:T(8,128)(4,1)} %iota_compare_fusion), kind=kOutput, calls=%fused_computation.6 | convolution fusion | flops 538968064 | bytes 2883584 | tf_op jit(solution)/shard_map/hqk,khd->qhd/dot_general | solution.py:102
  210.2 11.7 %collective-permute-done.13 = f32[4,128,128]{2,1,0:T(8,128)} collective-permute-done((f32[4,128,128]{2,1,0:T(8,128)}, f32[4,128,128]{2,1,0:T(8,128)}, u32[]{:S(2)}, u32[]{:S(2)}) %collective-permute-start.13) | collective-permute-done | bytes 262176 | tf_op jit(solution)/shard_map/ppermute | solution.py:60
  221.9 1.7 multiply_reduce_fusion
  223.8 1.0 copy.78
  (69 shorter events, 2.2 us)
Async XLA Ops:
  6.5 25.4 %copy-start.10 = (bf16[64,512]{1,0:T(8,128)(2,1)S(1)}, bf16[64,512]{1,0:T(8,128)(2,1)}, u32[]{:S(2)}) copy-start(bf16[64,512]{1,0:T(8,128)(2,1)} %param.5) | copy-start | bytes 196612
  6.5 76.7 %all-gather.12.cloned.1.call-start = ((), (), s32[]{:S(2)}) async-start(), calls=%async_computation.1 | async-start | bytes 1179648 | tf_op jit(solution)/shard_map/all_gather | solution.py:76
  15.5 9.2 %collective-permute-start = (bf16[2,2,64,256]{3,2,1,0:T(8,128)(2,1)S(1)}, bf16[2,2,64,256]{3,2,1,0:T(8,128)(2,1)S(1)}, u32[]{:S(2)}, u32[]{:S(2)}) collective-permute-start(bf16[2,2,64,256]{3,2,1,0:T(8,128)(2,1)S(1)} %get-tuple-element.7), channel_id=1, source_target_pairs={{0,12},{4,0},{8,4},{12,8},{1,13},{5,1},{9,5},{13,9},{2,14},{6,2},{... | collective-permute-start | bytes 393224 | tf_op jit(solution)/shard_map/ppermute | solution.py:30
  18.5 6.2 %collective-permute-start.1 = (bf16[2,2,64,256]{3,2,1,0:T(8,128)(2,1)S(1)}, bf16[2,2,64,256]{3,2,1,0:T(8,128)(2,1)S(1)}, u32[]{:S(2)}, u32[]{:S(2)}) collective-permute-start(bf16[2,2,64,256]{3,2,1,0:T(8,128)(2,1)S(1)} %get-tuple-element.7), channel_id=1, source_target_pairs={{0,4},{4,8},{8,12},{12,0},{1,5},{5,9},{9,13},{13,1},{2,6},{6,10},{... | collective-permute-start | bytes 393224 | tf_op jit(solution)/shard_map/ppermute | solution.py:27
  18.6 119.4 %all-gather.10.cloned.1.call-start = ((), (), s32[]{:S(2)}) async-start(), calls=%async_computation | async-start | bytes 4718592 | tf_op jit(solution)/shard_map/all_gather | solution.py:77
  24.7 6.2 %collective-permute-start.2 = (bf16[2,2,64,256]{3,2,1,0:T(8,128)(2,1)S(1)}, bf16[2,2,64,256]{3,2,1,0:T(8,128)(2,1)S(1)}, u32[]{:S(2)}, u32[]{:S(2)}) collective-permute-start(bf16[2,2,64,256]{3,2,1,0:T(8,128)(2,1)S(1)} %collective-permute-done.1), channel_id=1, source_target_pairs={{0,4},{4,8},{8,12},{12,0},{1,5},{5,9},{9,13},{13,1},{2,6},{6,10},{... | collective-permute-start | bytes 393224 | tf_op jit(solution)/shard_map/ppermute | solution.py:27
  31.9 158.6 %all-gather.14.cloned.1.call-start = ((), (), s32[]{:S(2)}) async-start(), calls=%async_computation.2 | async-start | bytes 2359296 | tf_op jit(solution)/shard_map/all_gather | solution.py:77
  63.0 82.0 %collective-permute-start.17 = (bf16[1,8,2,64,256]{4,3,2,1,0:T(8,128)(2,1)S(1)}, bf16[1,8,2,64,256]{4,3,2,1,0:T(8,128)(2,1)}, u32[]{:S(2)}, u32[]{:S(2)}) collective-permute-start(bf16[1,8,2,64,256]{4,3,2,1,0:T(8,128)(2,1)S(1)} %bitcast.118), channel_id=1, source_target_pairs={{0,12},{4,0},{8,4},{12,8},{1,13},{5,1},{9,5},{13,9},{2,14},{6,2},{... | collective-permute-start | bytes 1572872 | tf_op jit(solution)/shard_map/ppermute | solution.py:30
  63.0 50.5 %collective-permute-start.18 = (bf16[1,8,2,64,256]{4,3,2,1,0:T(8,128)(2,1)S(1)}, bf16[1,8,2,64,256]{4,3,2,1,0:T(8,128)(2,1)S(1)}, u32[]{:S(2)}, u32[]{:S(2)}) collective-permute-start(bf16[1,8,2,64,256]{4,3,2,1,0:T(8,128)(2,1)S(1)} %bitcast.119), channel_id=1, source_target_pairs={{0,4},{4,8},{8,12},{12,0},{1,5},{5,9},{9,13},{13,1},{2,6},{6,10},{... | collective-permute-start | bytes 1572872 | tf_op jit(solution)/shard_map/ppermute | solution.py:27
  65.1 21.2 %collective-permute-start.14 = (bf16[1,2,64,256]{3,2,1,0:T(8,128)(2,1)S(1)}, bf16[1,2,64,256]{3,2,1,0:T(8,128)(2,1)S(1)}, u32[]{:S(2)}, u32[]{:S(2)}) collective-permute-start(bf16[1,2,64,256]{3,2,1,0:T(8,128)(2,1)S(1)} %get-tuple-element.9), channel_id=1, source_target_pairs={{0,12},{4,0},{8,4},{12,8},{1,13},{5,1},{9,5},{13,9},{2,14},{6,2},{... | collective-permute-start | bytes 196616 | tf_op jit(solution)/shard_map/ppermute | solution.py:30
  66.3 16.9 %collective-permute-start.15 = (bf16[1,2,64,256]{3,2,1,0:T(8,128)(2,1)S(1)}, bf16[1,2,64,256]{3,2,1,0:T(8,128)(2,1)S(1)}, u32[]{:S(2)}, u32[]{:S(2)}) collective-permute-start(bf16[1,2,64,256]{3,2,1,0:T(8,128)(2,1)S(1)} %get-tuple-element.9), channel_id=1, source_target_pairs={{0,4},{4,8},{8,12},{12,0},{1,5},{5,9},{9,13},{13,1},{2,6},{6,10},{... | collective-permute-start | bytes 196616 | tf_op jit(solution)/shard_map/ppermute | solution.py:27
  73.5 4.9 %copy-start = (bf16[512,4096]{0,1:T(8,128)(2,1)S(1)}, bf16[512,4096]{0,1:T(8,128)(2,1)}, u32[]{:S(2)}) copy-start(bf16[512,4096]{0,1:T(8,128)(2,1)} %copy.64) | copy-start | bytes 12582916
  83.2 6.2 %collective-permute-start.16 = (bf16[1,2,64,256]{3,2,1,0:T(8,128)(2,1)S(1)}, bf16[1,2,64,256]{3,2,1,0:T(8,128)(2,1)S(1)}, u32[]{:S(2)}, u32[]{:S(2)}) collective-permute-start(bf16[1,2,64,256]{3,2,1,0:T(8,128)(2,1)S(1)} %collective-permute-done.15), channel_id=1, source_target_pairs={{0,4},{4,8},{8,12},{12,0},{1,5},{5,9},{9,13},{13,1},{2,6},{6,10},{... | collective-permute-start | bytes 196616 | tf_op jit(solution)/shard_map/ppermute | solution.py:27
  83.2 33.0 %copy-start.2 = (bf16[2,16,64,256]{3,2,1,0:T(8,128)(2,1)S(1)}, bf16[2,16,64,256]{3,2,1,0:T(8,128)(2,1)}, u32[]{:S(2)}) copy-start(bf16[2,16,64,256]{3,2,1,0:T(8,128)(2,1)} %all-gather.12.cloned.1.call-done) | copy-start | bytes 3145732
  85.7 23.5 %collective-permute-start.4 = (bf16[2,8,2,64,256]{4,3,2,0,1:T(8,128)(2,1)}, bf16[2,8,2,64,256]{4,3,2,0,1:T(8,128)(2,1)S(1)}, u32[]{:S(2)}, u32[]{:S(2)}) collective-permute-start(bf16[2,8,2,64,256]{4,3,2,0,1:T(8,128)(2,1)} %copy.66), channel_id=1, source_target_pairs={{0,4},{4,8},{8,12},{12,0},{1,5},{5,9},{9,13},{13,1},{2,6},{6,10},{... | collective-permute-start | bytes 3145736 | tf_op jit(solution)/shard_map/ppermute | solution.py:27
  91.2 25.0 %collective-permute-start.3 = (bf16[2,8,2,64,256]{4,3,2,0,1:T(8,128)(2,1)}, bf16[2,8,2,64,256]{4,3,2,0,1:T(8,128)(2,1)}, u32[]{:S(2)}, u32[]{:S(2)}) collective-permute-start(bf16[2,8,2,64,256]{4,3,2,0,1:T(8,128)(2,1)} %copy.66), channel_id=1, source_target_pairs={{0,12},{4,0},{8,4},{12,8},{1,13},{5,1},{9,5},{13,9},{2,14},{6,2},{... | collective-permute-start | bytes 3145736 | tf_op jit(solution)/shard_map/ppermute | solution.py:30
  109.2 21.9 %collective-permute-start.5 = (bf16[2,8,2,64,256]{4,3,2,0,1:T(8,128)(2,1)S(1)}, bf16[2,8,2,64,256]{4,3,2,0,1:T(8,128)(2,1)}, u32[]{:S(2)}, u32[]{:S(2)}) collective-permute-start(bf16[2,8,2,64,256]{4,3,2,0,1:T(8,128)(2,1)S(1)} %collective-permute-done.4), channel_id=1, source_target_pairs={{0,4},{4,8},{8,12},{12,0},{1,5},{5,9},{9,13},{13,1},{2,6},{6,10},{... | collective-permute-start | bytes 3145736 | tf_op jit(solution)/shard_map/ppermute | solution.py:27
  113.5 32.6 %collective-permute-start.19 = (bf16[1,8,2,64,256]{4,3,2,1,0:T(8,128)(2,1)S(1)}, bf16[1,8,2,64,256]{4,3,2,1,0:T(8,128)(2,1)}, u32[]{:S(2)}, u32[]{:S(2)}) collective-permute-start(bf16[1,8,2,64,256]{4,3,2,1,0:T(8,128)(2,1)S(1)} %collective-permute-done.18), channel_id=1, source_target_pairs={{0,4},{4,8},{8,12},{12,0},{1,5},{5,9},{9,13},{13,1},{2,6},{6,10},{... | collective-permute-start | bytes 1572872 | tf_op jit(solution)/shard_map/ppermute | solution.py:27
  132.5 3.0 %copy-start.1 = (bf16[512,4096]{0,1:T(8,128)(2,1)S(1)}, bf16[512,4096]{0,1:T(8,128)(2,1)}, u32[]{:S(2)}) copy-start(bf16[512,4096]{0,1:T(8,128)(2,1)} %copy.64) | copy-start | bytes 12582916
  137.9 7.1 %copy-start.4 = (bf16[1,8,8,2,64,256]{5,4,3,2,1,0:T(8,128)(2,1)S(1)}, bf16[1,8,8,2,64,256]{5,4,3,2,1,0:T(8,128)(2,1)}, u32[]{:S(2)}) copy-start(bf16[1,8,8,2,64,256]{5,4,3,2,1,0:T(8,128)(2,1)} %bitcast_dynamic-update-slice_fusion.12) | copy-start | bytes 12582916
  144.3 7.7 %collective-permute-start.6 = (f32[4,128,128]{2,1,0:T(8,128)S(1)}, f32[4,128,128]{2,1,0:T(8,128)S(1)}, u32[]{:S(2)}, u32[]{:S(2)}) collective-permute-start(f32[4,128,128]{2,1,0:T(8,128)S(1)} %fusion.53), channel_id=1, source_target_pairs={{0,4},{4,8},{8,12},{12,0},{1,5},{5,9},{9,13},{13,1},{2,6},{6,10},{... | collective-permute-start | bytes 786440 | tf_op jit(solution)/shard_map/ppermute | solution.py:27
  147.2 7.0 %collective-permute-start.7 = (f32[4,128,128]{2,1,0:T(8,128)S(1)}, f32[4,128,128]{2,1,0:T(8,128)S(1)}, u32[]{:S(2)}, u32[]{:S(2)}) collective-permute-start(f32[4,128,128]{2,1,0:T(8,128)S(1)} %fusion.53), channel_id=1, source_target_pairs={{0,12},{4,0},{8,4},{12,8},{1,13},{5,1},{9,5},{13,9},{2,14},{6,2},{... | collective-permute-start | bytes 786440 | tf_op jit(solution)/shard_map/ppermute | solution.py:30
  152.0 7.6 %collective-permute-start.8 = (f32[4,128,128]{2,1,0:T(8,128)S(1)}, f32[4,128,128]{2,1,0:T(8,128)S(1)}, u32[]{:S(2)}, u32[]{:S(2)}) collective-permute-start(f32[4,128,128]{2,1,0:T(8,128)S(1)} %collective-permute-done.6), channel_id=1, source_target_pairs={{0,4},{4,8},{8,12},{12,0},{1,5},{5,9},{9,13},{13,1},{2,6},{6,10},{... | collective-permute-start | bytes 786440 | tf_op jit(solution)/shard_map/ppermute | solution.py:27
  154.2 18.1 %copy-start.5 = (f32[4,128,128]{2,1,0:T(8,128)}, f32[4,128,128]{2,1,0:T(8,128)S(1)}, u32[]{:S(2)}) copy-start(f32[4,128,128]{2,1,0:T(8,128)S(1)} %collective-permute-done.7) | copy-start | bytes 786436
  159.6 12.8 %copy-start.7 = (f32[4,128,128]{2,1,0:T(8,128)}, f32[4,128,128]{2,1,0:T(8,128)S(1)}, u32[]{:S(2)}) copy-start(f32[4,128,128]{2,1,0:T(8,128)S(1)} %collective-permute-done.8) | copy-start | bytes 786436
  159.7 21.8 %copy-start.3 = (bf16[512,4,8,2,64]{0,4,3,2,1:T(8,128)(2,1)S(1)}, bf16[512,4,8,2,64]{0,4,3,2,1:T(8,128)(2,1)}, u32[]{:S(2)}) copy-start(bf16[512,4,8,2,64]{0,4,3,2,1:T(8,128)(2,1)} %copy.73) | copy-start | bytes 12582916
  159.7 8.1 %collective-permute-start.9 = (f32[4,128,128]{2,1,0:T(8,128)S(1)}, f32[4,128,128]{2,1,0:T(8,128)S(1)}, u32[]{:S(2)}, u32[]{:S(2)}) collective-permute-start(f32[4,128,128]{2,1,0:T(8,128)S(1)} %add_add_fusion), channel_id=1, source_target_pairs={{0,16},{16,0},{1,17},{17,1},{2,18},{18,2},{3,19},{19,3},{4,20},{20... | collective-permute-start | bytes 786440 | tf_op jit(solution)/shard_map/ppermute | solution.py:27
  167.8 15.0 %copy-start.9 = (f32[4,128,128]{2,1,0:T(8,128)}, f32[4,128,128]{2,1,0:T(8,128)S(1)}, u32[]{:S(2)}) copy-start(f32[4,128,128]{2,1,0:T(8,128)S(1)} %collective-permute-done.9) | copy-start | bytes 786436
  167.8 11.2 %collective-permute-start.10 = (f32[4,128,128]{2,1,0:T(8,128)S(1)}, f32[4,128,128]{2,1,0:T(8,128)S(1)}, u32[]{:S(2)}, u32[]{:S(2)}) collective-permute-start(f32[4,128,128]{2,1,0:T(8,128)S(1)} %add.77), channel_id=1, source_target_pairs={{0,32},{32,64},{64,96},{96,128},{128,160},{160,192},{192,224},{1,3... | collective-permute-start | bytes 786440 | tf_op jit(solution)/shard_map/ppermute | solution.py:57
  179.1 10.0 %collective-permute-start.11 = (f32[4,128,128]{2,1,0:T(8,128)S(1)}, f32[4,128,128]{2,1,0:T(8,128)S(1)}, u32[]{:S(2)}, u32[]{:S(2)}) collective-permute-start(f32[4,128,128]{2,1,0:T(8,128)S(1)} %collective-permute-done.10), channel_id=1, source_target_pairs={{0,32},{32,64},{64,96},{96,128},{128,160},{160,192},{192,224},{1,3... | collective-permute-start | bytes 786440 | tf_op jit(solution)/shard_map/ppermute | solution.py:60
  189.1 16.8 %collective-permute-start.12 = (f32[4,128,128]{2,1,0:T(8,128)S(1)}, f32[4,128,128]{2,1,0:T(8,128)S(1)}, u32[]{:S(2)}, u32[]{:S(2)}) collective-permute-start(f32[4,128,128]{2,1,0:T(8,128)S(1)} %add.78), channel_id=1, source_target_pairs={{0,64},{32,96},{64,128},{96,160},{128,192},{160,224},{1,65},{33,97... | collective-permute-start | bytes 786440 | tf_op jit(solution)/shard_map/ppermute | solution.py:60
  194.5 27.4 %copy-start.6 = (f32[4,128,128]{2,1,0:T(8,128)S(1)}, f32[4,128,128]{2,1,0:T(8,128)}, u32[]{:S(2)}) copy-start(f32[4,128,128]{2,1,0:T(8,128)} %copy-done.5) | copy-start | bytes 786436
  194.5 27.3 %copy-start.8 = (f32[4,128,128]{2,1,0:T(8,128)S(1)}, f32[4,128,128]{2,1,0:T(8,128)}, u32[]{:S(2)}) copy-start(f32[4,128,128]{2,1,0:T(8,128)} %copy-done.7) | copy-start | bytes 786436
  206.6 15.3 %collective-permute-start.13 = (f32[4,128,128]{2,1,0:T(8,128)}, f32[4,128,128]{2,1,0:T(8,128)}, u32[]{:S(2)}, u32[]{:S(2)}) collective-permute-start(f32[4,128,128]{2,1,0:T(8,128)} %add.79), channel_id=1, source_target_pairs={{0,128},{32,160},{64,192},{96,224},{1,129},{33,161},{65,193},{97,2... | collective-permute-start | bytes 786440 | tf_op jit(solution)/shard_map/ppermute | solution.py:60
Sparse Core Ops, SparseCore 0:
  18.7 37.7 all-gather.11
  58.3 53.6 all-gather.9
  113.7 40.5 all-gather.13

commit v3 on v2

--- a/solution.py
+++ b/solution.py
@@ -41,31 +41,34 @@
     return jnp.roll(stacked, lax.axis_index(name), axis=axis)
 
 
-def exclusive_and_total(x, name):
-    n = SIZES[name]
-    idx = lax.axis_index(name)
+def direct_values(x, name, n):
+    size = SIZES[name]
+    got = []
+    for k in range(1, n):
+        pairs = [(j, j - j % n + (j % n + k) % n) for j in range(size)]
+        got.append((k, lax.ppermute(x, name, pairs)))
+    return got
+
+
+def exclusive_and_total(x, name, n=None):
+    n = n or SIZES[name]
+    idx = lax.axis_index(name) % n
     before = jnp.zeros_like(x)
     total = x
-    for k, v in ring_values(x, name, n):
+    for k, v in direct_values(x, name, n):
         before = before + jnp.where(k <= idx, v, 0.0)
         total = total + v
     return before, total
 
 
-def exclusive_scan(x, name):
-    n = SIZES[name]
-    e = lax.ppermute(x, name, [(j, j + 1) for j in range(n - 1)])
-    d = 1
-    while d < n:
-        e = e + lax.ppermute(e, name, [(j, j + d) for j in range(n - d)])
-        d *= 2
-    return e
-
-
 def prefix_over_ctx(state):
     before_y, total_y = exclusive_and_total(state, "y")
     before_x, total_xy = exclusive_and_total(total_y, "xh")
-    return exclusive_scan(total_xy, "z") + before_x + before_y
+    half = SIZES["z"] // 2
+    before_zl, total_zl = exclusive_and_total(total_xy, "z", half)
+    other = lax.ppermute(total_zl, "z", [(j, (j + half) % SIZES["z"]) for j in range(SIZES["z"])])
+    before_zh = jnp.where(lax.axis_index("z") >= half, other, 0.0)
+    return before_zh + before_zl + before_x + before_y
 
 
 def project(tokens, ws, split):
@@ -73,16 +76,26 @@
     g = lax.all_gather(w, "xh", axis=1)
     a, b = g[..., :split], g[..., split:]
     a = ring_gather(a, "y", axis=1)
-    b = lax.all_gather(b, "z", axis=1)
-    a = lax.all_gather(a, "z", axis=1)
-    b = ring_gather(b, "y", axis=1)
+    b = ring_gather(b, "z", axis=1)
     t = tokens.shape[0]
     k = w.shape[1]
     tok = tokens.reshape(t, SIZES["z"], SIZES["xh"], SIZES["y"], k)
-    tok_a = tok.transpose(0, 1, 3, 2, 4).reshape(t, -1)
-    tok_b = tok.transpose(0, 3, 1, 2, 4).reshape(t, -1)
-    out_a = jnp.einsum("tk,wkn->wtn", tok_a, a.reshape(len(ws), -1, split), preferred_element_type=jnp.float32)
-    out_b = jnp.einsum("tk,wkn->wtn", tok_b, b.reshape(len(ws), -1, w.shape[2] - split), preferred_element_type=jnp.float32)
+    tok_a = jnp.roll(tok.transpose(1, 0, 3, 2, 4), -lax.axis_index("z"), axis=0).reshape(SIZES["z"], t, -1)
+    tok_b = jnp.roll(tok.transpose(3, 0, 1, 2, 4), -lax.axis_index("y"), axis=0).reshape(SIZES["y"], t, -1)
+
+    def last_stage(x, name, toks):
+        n = SIZES[name]
+        pieces = [(0, x)] + [((n - d) % n, v) for d, v in ring_values(x, name, n)]
+        out = None
+        for m, v in pieces:
+            part = jnp.einsum(
+                "tk,wkn->wtn", toks[m], v.reshape(len(ws), -1, v.shape[-1]), preferred_element_type=jnp.float32
+            )
+            out = part if out is None else out + part
+        return out
+
+    out_a = last_stage(a, "z", tok_a)
+    out_b = last_stage(b, "y", tok_b)
     return jnp.concatenate([out_a, out_b], axis=-1)
 
 
@@ -91,11 +104,11 @@
     width_group = w_query.shape[1]
     head_count = width_group // DH
     split = width_group // 2
-    kv = project(tokens, [w_key, w_value], split).astype(jnp.bfloat16).reshape(2, tok_rows, head_count, DH)
-    key_rows, value_rows = kv[0], kv[1]
+    qkv = project(tokens, [w_query, w_key, w_value], split).astype(jnp.bfloat16)
+    qkv = qkv.reshape(3, tok_rows, head_count, DH)
+    query_rows, key_rows, value_rows = qkv[0], qkv[1], qkv[2]
     own_total = jnp.einsum("khd,khe->hde", key_rows, value_rows, preferred_element_type=jnp.float32)
     start_state = prefix_over_ctx(own_total)
-    query_rows = project(tokens, [w_query], split).astype(jnp.bfloat16).reshape(tok_rows, head_count, DH)
     causal_mask = jnp.tril(jnp.ones((BLOCK, BLOCK), dtype=bool))
     scores = jnp.einsum("qhd,khd->hqk", query_rows, key_rows, preferred_element_type=jnp.float32)
     scores = jnp.where(causal_mask[None], scores, 0.0).astype(jnp.bfloat16)

time: 232 us -> 211 us (0.909)
  the two profiles are of different devices: /device:TPU:192 before, /device:TPU:62 now
where the time goes in v3:
time: 211 us; the launch traced here: 210 us
  waiting for transfers between devices  114 us (54%)
  starting transfers between devices  39.3 us (19%)
  local copies, waits for them, and re-layouts  24.8 us (12%)
  matrix products  13.4 us (6%)
  other arithmetic  9.08 us (4%)
  blocking collectives  8.81 us (4%)
    ppermute x12, waiting for transfers between devices, ring_values(): r = lax.ppermute(r, name, right)  71.7 us
    ppermute x7, waiting for transfers between devices, direct_values(): got.append((k, lax.ppermute(x, name, pairs)))  33.5 us
    ppermute x8, starting transfers between devices, ring_values(): l = lax.ppermute(l, name, left)  16.5 us
    unnamed x47, local copies, waits for them, and re-layouts  14.5 us
    ppermute x12, starting transfers between devices, ring_values(): r = lax.ppermute(r, name, right)  11.7 us
    ppermute x7, starting transfers between devices, direct_values(): got.append((k, lax.ppermute(x, name, pairs)))  9.43 us
    ppermute x1, waiting for transfers between devices, prefix_over_ctx(): lax.ppermute(total_zl, 'z', [(j, (j + half) % SIZES['z']) for j in range(...  9.14 us
    dot_general x12, matrix products, last_stage(): jnp.einsum('tk,wkn->wtn', toks[m], v.reshape(len(ws), -1, v.shape[-1]), p...  9.05 us
  transfers between devices with their start and end apart: 28, of which 15 were waited for; matrix products, arithmetic and copies ran while one was open for 19% of the time, Pallas kernels for 0%

profile of v3, /device:TPU:62, one launch (start us, length us, event | category | flops | bytes accessed | tf_op | source)
XLA Modules:
  0.0 210.2 jit_solution(4867515693215436316)
XLA Ops:
  0.0 0.9 pad_maximum_fusion.1
  0.9 8.8 %all-gather = bf16[3,128,512]{2,1,0:T(8,128)(2,1)S(1)} all-gather(bf16[3,64,512]{2,1,0:T(8,128)(2,1)S(1)} %pad_maximum_fusion.1), channel_id=2, replica_groups=mesh['z'=8,'xh'=2,'y'=4,'hd'=4] {'xh'}, dimensions={1}, use_global_device_ids=true | all-gather | bytes 589824 | tf_op jit(solution)/shard_map/all_gather | solution.py:76
  9.7 0.8 fusion.36
  10.6 1.9 collective-permute-start.13
  12.6 0.7 collective-permute-start
  13.3 2.5 %collective-permute-start.1 = (bf16[3,2,64,256]{3,2,1,0:T(8,128)(2,1)}, bf16[3,2,64,256]{3,2,1,0:T(8,128)(2,1)}, u32[]{:S(2)}, u32[]{:S(2)}) collective-permute-start(bf16[3,2,64,256]{3,2,1,0:T(8,128)(2,1)} %get-tuple-element.21), channel_id=1, source_target_pairs={{0,4},{4,8},{8,12},{12,0},{1,5},{5,9},{9,13},{13,1},{2,6},{6,10},{... | collective-permute-start | bytes 589832 | tf_op jit(solution)/shard_map/ppermute | solution.py:27
  15.8 0.7 bitcast_dynamic-update-slice_fusion.20
  16.5 6.5 %copy.39 = bf16[512,4096]{0,1:T(8,128)(2,1)} copy(bf16[512,4096]{1,0:T(8,128)(2,1)} %param.4) | data formatting | bytes 8388608 | tf_op args[0]
  23.0 3.1 %fusion = bf16[4,512,8,2,64]{1,4,0,3,2:T(8,128)(2,1)S(1)} fusion(s32[]{:T(128)S(6)} %select_n.119, bf16[4,512,8,2,64]{1,4,0,3,2:T(8,128)(2,1)} %bitcast.142), kind=kLoop, calls=%fused_computation.4 | loop fusion | flops 2097152 | bytes 8388612 | tf_op jit(solution)/shard_map/jit(_roll_dynamic)/concatenate | solution.py:84
  26.1 1.8 fusion.34
  27.9 3.1 %fusion.1 = bf16[8,512,4,2,64]{1,4,2,3,0:T(8,128)(2,1)S(1)} fusion(s32[]{:T(128)S(6)} %select_n.115, bf16[8,512,4,2,64]{1,4,2,3,0:T(8,128)(2,1)} %bitcast.143), kind=kLoop, calls=%fused_computation.5 | loop fusion | flops 2097152 | bytes 8388612 | tf_op jit(solution)/shard_map/jit(_roll_dynamic)/concatenate | solution.py:83
  31.6 0.8 copy.52
  32.5 0.9 copy.43
  33.3 0.8 copy.46
  34.2 0.9 copy.40
  35.1 4.0 %collective-permute-start.11 = (bf16[3,2,64,256]{3,2,1,0:T(8,128)(2,1)}, bf16[3,2,64,256]{3,2,1,0:T(8,128)(2,1)S(1)}, u32[]{:S(2)}, u32[]{:S(2)}) collective-permute-start(bf16[3,2,64,256]{3,2,1,0:T(8,128)(2,1)} %collective-permute-done.10), channel_id=1, source_target_pairs={{0,224},{32,0},{64,32},{96,64},{128,96},{160,128},{192,160},{224,1... | collective-permute-start | bytes 589832 | tf_op jit(solution)/shard_map/ppermute | solution.py:30
  39.2 1.6 bitcast_dynamic-update-slice_fusion.18
  40.9 0.9 bitcast_dynamic-update-slice_fusion.2
  41.8 3.3 %collective-permute-done.2 = bf16[3,2,64,256]{3,2,1,0:T(8,128)(2,1)S(1)} collective-permute-done((bf16[3,2,64,256]{3,2,1,0:T(8,128)(2,1)}, bf16[3,2,64,256]{3,2,1,0:T(8,128)(2,1)S(1)}, u32[]{:S(2)}, u32[]{:S(2)}) %collective-permute-start.2) | collective-permute-done | bytes 196640 | tf_op jit(solution)/shard_map/ppermute | solution.py:27
  45.1 0.9 bitcast_dynamic-update-slice_fusion.22
  46.1 1.1 bitcast_dynamic-update-slice_fusion.3
  47.2 0.9 bitcast_dynamic-update-slice_fusion.23
  48.2 1.2 collective-permute-start.3
  49.4 2.2 %collective-permute-start.4 = (bf16[3,4,2,64,256]{4,3,2,1,0:T(8,128)(2,1)S(1)}, bf16[3,4,2,64,256]{4,3,2,1,0:T(8,128)(2,1)S(1)}, u32[]{:S(2)}, u32[]{:S(2)}) collective-permute-start(bf16[3,4,2,64,256]{4,3,2,1,0:T(8,128)(2,1)S(1)} %constant_dynamic-slice_fusion.1), channel_id=1, source_target_pairs={{0,224},{32,0},{64,32},{96,64},{128,96},{160,128},{192,160},{224,1... | collective-permute-start | bytes 2359304 | tf_op jit(solution)/shard_map/ppermute | solution.py:30
  51.6 3.2 %collective-permute-start.12 = (bf16[3,2,64,256]{3,2,1,0:T(8,128)(2,1)S(1)}, bf16[3,2,64,256]{3,2,1,0:T(8,128)(2,1)S(1)}, u32[]{:S(2)}, u32[]{:S(2)}) collective-permute-start(bf16[3,2,64,256]{3,2,1,0:T(8,128)(2,1)S(1)} %collective-permute-done.11), channel_id=1, source_target_pairs={{0,224},{32,0},{64,32},{96,64},{128,96},{160,128},{192,160},{224,1... | collective-permute-start | bytes 589832 | tf_op jit(solution)/shard_map/ppermute | solution.py:30
  54.8 15.7 %collective-permute-done.15 = bf16[3,2,64,256]{3,2,1,0:T(8,128)(2,1)S(1)} collective-permute-done((bf16[3,2,64,256]{3,2,1,0:T(8,128)(2,1)S(1)}, bf16[3,2,64,256]{3,2,1,0:T(8,128)(2,1)S(1)}, u32[]{:S(2)}, u32[]{:S(2)}) %collective-permute-start.15) | collective-permute-done | bytes 196640 | tf_op jit(solution)/shard_map/ppermute | solution.py:27
  70.5 1.5 collective-permute-start.16
  72.0 5.1 %collective-permute-done.16 = bf16[3,2,64,256]{3,2,1,0:T(8,128)(2,1)S(1)} collective-permute-done((bf16[3,2,64,256]{3,2,1,0:T(8,128)(2,1)S(1)}, bf16[3,2,64,256]{3,2,1,0:T(8,128)(2,1)S(1)}, u32[]{:S(2)}, u32[]{:S(2)}) %collective-permute-start.16) | collective-permute-done | bytes 196640 | tf_op jit(solution)/shard_map/ppermute | solution.py:27
  77.2 0.9 bitcast_dynamic-update-slice_fusion.6
  78.1 0.9 bitcast_dynamic-update-slice_fusion.19
  79.2 0.9 bitcast_dynamic-update-slice_fusion.7
  80.3 1.3 collective-permute-start.17
  82.2 0.9 collective-permute-start.18
  83.9 2.7 %collective-permute-start.6 = (bf16[3,4,2,64,256]{4,3,2,1,0:T(8,128)(2,1)S(1)}, bf16[3,4,2,64,256]{4,3,2,1,0:T(8,128)(2,1)S(1)}, u32[]{:S(2)}, u32[]{:S(2)}) collective-permute-start(bf16[3,4,2,64,256]{4,3,2,1,0:T(8,128)(2,1)S(1)} %collective-permute-done.4), channel_id=1, source_target_pairs={{0,224},{32,0},{64,32},{96,64},{128,96},{160,128},{192,160},{224,1... | collective-permute-start | bytes 2359304 | tf_op jit(solution)/shard_map/ppermute | solution.py:30
  86.6 1.0 fusion.44
  89.3 12.0 %collective-permute-done.5 = bf16[3,4,2,64,256]{4,3,2,1,0:T(8,128)(2,1)S(1)} collective-permute-done((bf16[3,4,2,64,256]{4,3,2,1,0:T(8,128)(2,1)S(1)}, bf16[3,4,2,64,256]{4,3,2,1,0:T(8,128)(2,1)S(1)}, u32[]{:S(2)}, u32[]{:S(2)}) %collective-permute-start.5) | collective-permute-done | bytes 786464 | tf_op jit(solution)/shard_map/ppermute | solution.py:27
  101.6 2.6 %collective-permute-start.8 = (bf16[3,4,2,64,256]{4,3,2,1,0:T(8,128)(2,1)S(1)}, bf16[3,4,2,64,256]{4,3,2,1,0:T(8,128)(2,1)S(1)}, u32[]{:S(2)}, u32[]{:S(2)}) collective-permute-start(bf16[3,4,2,64,256]{4,3,2,1,0:T(8,128)(2,1)S(1)} %collective-permute-done.6), channel_id=1, source_target_pairs={{0,224},{32,0},{64,32},{96,64},{128,96},{160,128},{192,160},{224,1... | collective-permute-start | bytes 2359304 | tf_op jit(solution)/shard_map/ppermute | solution.py:30
  105.5 9.3 %collective-permute-done.17 = bf16[3,8,2,64,256]{4,3,2,0,1:T(8,128)(2,1)S(1)} collective-permute-done((bf16[3,8,2,64,256]{4,3,2,0,1:T(8,128)(2,1)S(1)}, bf16[3,8,2,64,256]{4,3,2,0,1:T(8,128)(2,1)S(1)}, u32[]{:S(2)}, u32[]{:S(2)}) %collective-permute-start.17) | collective-permute-done | bytes 1572896 | tf_op jit(solution)/shard_map/ppermute | solution.py:27
  114.9 1.3 collective-permute-start.19
  116.2 1.0 fusion.45
  117.4 0.9 collective-permute-start.9
  118.4 1.0 fusion.46
  120.6 11.5 %collective-permute-done.9 = bf16[3,4,2,64,256]{4,3,2,1,0:T(8,128)(2,1)S(1)} collective-permute-done((bf16[3,4,2,64,256]{4,3,2,1,0:T(8,128)(2,1)S(1)}, bf16[3,4,2,64,256]{4,3,2,1,0:T(8,128)(2,1)S(1)}, u32[]{:S(2)}, u32[]{:S(2)}) %collective-permute-start.9) | collective-permute-done | bytes 786464 | tf_op jit(solution)/shard_map/ppermute | solution.py:27
  132.1 0.9 fusion.5
  133.0 14.9 %collective-permute-done.19 = bf16[3,8,2,64,256]{4,3,2,0,1:T(8,128)(2,1)S(1)} collective-permute-done((bf16[3,8,2,64,256]{4,3,2,0,1:T(8,128)(2,1)S(1)}, bf16[3,8,2,64,256]{4,3,2,0,1:T(8,128)(2,1)S(1)}, u32[]{:S(2)}, u32[]{:S(2)}) %collective-permute-start.19) | collective-permute-done | bytes 1572896 | tf_op jit(solution)/shard_map/ppermute | solution.py:27
  148.0 1.0 fusion.4
  149.4 1.3 collective-permute-start.20
  151.7 4.2 %collective-permute-done.20 = f32[4,128,128]{2,1,0:T(8,128)S(1)} collective-permute-done((f32[4,128,128]{2,1,0:T(8,128)S(1)}, f32[4,128,128]{2,1,0:T(8,128)S(1)}, u32[]{:S(2)}, u32[]{:S(2)}) %collective-permute-start.20) | collective-permute-done | bytes 262176 | tf_op jit(solution)/shard_map/ppermute | solution.py:49
  155.9 2.8 %collective-permute-done.21 = f32[4,128,128]{2,1,0:T(8,128)S(1)} collective-permute-done((f32[4,128,128]{2,1,0:T(8,128)S(1)}, f32[4,128,128]{2,1,0:T(8,128)S(1)}, u32[]{:S(2)}, u32[]{:S(2)}) %collective-permute-start.21) | collective-permute-done | bytes 262176 | tf_op jit(solution)/shard_map/ppermute | solution.py:49
  158.7 2.7 %collective-permute-done.22 = f32[4,128,128]{2,1,0:T(8,128)S(1)} collective-permute-done((f32[4,128,128]{2,1,0:T(8,128)S(1)}, f32[4,128,128]{2,1,0:T(8,128)S(1)}, u32[]{:S(2)}, u32[]{:S(2)}) %collective-permute-start.22) | collective-permute-done | bytes 262176 | tf_op jit(solution)/shard_map/ppermute | solution.py:49
  161.5 1.5 collective-permute-start.23
  163.0 6.5 %collective-permute-done.23 = f32[4,128,128]{2,1,0:T(8,128)S(1)} collective-permute-done((f32[4,128,128]{2,1,0:T(8,128)S(1)}, f32[4,128,128]{2,1,0:T(8,128)S(1)}, u32[]{:S(2)}, u32[]{:S(2)}) %collective-permute-start.23) | collective-permute-done | bytes 262176 | tf_op jit(solution)/shard_map/ppermute | solution.py:49
  169.5 0.7 collective-permute-start.24
  170.2 5.0 %collective-permute-start.25 = (f32[4,128,128]{2,1,0:T(8,128)S(1)}, f32[4,128,128]{2,1,0:T(8,128)S(1)}, u32[]{:S(2)}, u32[]{:S(2)}) collective-permute-start(f32[4,128,128]{2,1,0:T(8,128)S(1)} %add.168), channel_id=1, source_target_pairs={{0,64},{32,96},{64,0},{96,32},{128,192},{160,224},{192,128},{224,1... | collective-permute-start | bytes 786440 | tf_op jit(solution)/shard_map/ppermute | solution.py:49
  175.2 0.8 iota_compare_fusion
  176.0 1.2 collective-permute-done.24
  177.2 13.0 %collective-permute-done.25 = f32[4,128,128]{2,1,0:T(8,128)S(1)} collective-permute-done((f32[4,128,128]{2,1,0:T(8,128)S(1)}, f32[4,128,128]{2,1,0:T(8,128)S(1)}, u32[]{:S(2)}, u32[]{:S(2)}) %collective-permute-start.25) | collective-permute-done | bytes 262176 | tf_op jit(solution)/shard_map/ppermute | solution.py:49
  190.2 3.1 %collective-permute-done.26 = f32[4,128,128]{2,1,0:T(8,128)S(1)} collective-permute-done((f32[4,128,128]{2,1,0:T(8,128)S(1)}, f32[4,128,128]{2,1,0:T(8,128)S(1)}, u32[]{:S(2)}, u32[]{:S(2)}) %collective-permute-start.26) | collective-permute-done | bytes 262176 | tf_op jit(solution)/shard_map/ppermute | solution.py:49
  193.3 0.8 add_add_fusion
  194.1 1.7 collective-permute-start.27
  195.8 2.3 %fusion.2 = f32[4,128,512]{2,1,0:T(8,128)S(1)} fusion(bf16[512,4,128]{0,2,1:T(8,128)(2,1)S(1)} %bitcast.164, bf16[512,4,128]{0,2,1:T(8,128)(2,1)S(1)} %bitcast.165, bf16[512,4,128]{0,2,1:T(8,128)(2,1)S(1)} %bitcast.162, pred[512,512]{1,0:T(8,128)(4,1)} %iota_compare_fusion), kind=kOutput, calls=%fused_computation.11 | convolution fusion | flops 538968064 | bytes 2883584 | tf_op jit(solution)/shard_map/hqk,khd->qhd/dot_general | solution.py:115
  198.2 9.1 %collective-permute-done.27 = f32[4,128,128]{2,1,0:T(8,128)} collective-permute-done((f32[4,128,128]{2,1,0:T(8,128)}, f32[4,128,128]{2,1,0:T(8,128)}, u32[]{:S(2)}, u32[]{:S(2)}) %collective-permute-start.27) | collective-permute-done | bytes 262176 | tf_op jit(solution)/shard_map/ppermute | solution.py:69
  207.3 1.7 multiply_reduce_fusion
  209.2 1.0 copy.79
  (85 shorter events, 9.2 us)
Async XLA Ops:
  10.5 24.6 %collective-permute-start.10 = (bf16[3,2,64,256]{3,2,1,0:T(8,128)(2,1)}, bf16[3,2,64,256]{3,2,1,0:T(8,128)(2,1)}, u32[]{:S(2)}, u32[]{:S(2)}) collective-permute-start(bf16[3,2,64,256]{3,2,1,0:T(8,128)(2,1)} %get-tuple-element.20), channel_id=1, source_target_pairs={{0,224},{32,0},{64,32},{96,64},{128,96},{160,128},{192,160},{224,1... | collective-permute-start | bytes 589832 | tf_op jit(solution)/shard_map/ppermute | solution.py:30
  10.6 28.5 %collective-permute-start.13 = (bf16[3,2,64,256]{3,2,1,0:T(8,128)(2,1)}, bf16[3,2,64,256]{3,2,1,0:T(8,128)(2,1)}, u32[]{:S(2)}, u32[]{:S(2)}) collective-permute-start(bf16[3,2,64,256]{3,2,1,0:T(8,128)(2,1)} %get-tuple-element.20), channel_id=1, source_target_pairs={{0,32},{32,64},{64,96},{96,128},{128,160},{160,192},{192,224},{224... | collective-permute-start | bytes 589832 | tf_op jit(solution)/shard_map/ppermute | solution.py:27
  12.6 28.3 %collective-permute-start = (bf16[3,2,64,256]{3,2,1,0:T(8,128)(2,1)}, bf16[3,2,64,256]{3,2,1,0:T(8,128)(2,1)}, u32[]{:S(2)}, u32[]{:S(2)}) collective-permute-start(bf16[3,2,64,256]{3,2,1,0:T(8,128)(2,1)} %get-tuple-element.21), channel_id=1, source_target_pairs={{0,12},{4,0},{8,4},{12,8},{1,13},{5,1},{9,5},{13,9},{2,14},{6,2},{... | collective-permute-start | bytes 589832 | tf_op jit(solution)/shard_map/ppermute | solution.py:30
  13.3 25.8 %collective-permute-start.1 = (bf16[3,2,64,256]{3,2,1,0:T(8,128)(2,1)}, bf16[3,2,64,256]{3,2,1,0:T(8,128)(2,1)}, u32[]{:S(2)}, u32[]{:S(2)}) collective-permute-start(bf16[3,2,64,256]{3,2,1,0:T(8,128)(2,1)} %get-tuple-element.21), channel_id=1, source_target_pairs={{0,4},{4,8},{8,12},{12,0},{1,5},{5,9},{9,13},{13,1},{2,6},{6,10},{... | collective-permute-start | bytes 589832 | tf_op jit(solution)/shard_map/ppermute | solution.py:27
  35.1 16.5 %collective-permute-start.11 = (bf16[3,2,64,256]{3,2,1,0:T(8,128)(2,1)}, bf16[3,2,64,256]{3,2,1,0:T(8,128)(2,1)S(1)}, u32[]{:S(2)}, u32[]{:S(2)}) collective-permute-start(bf16[3,2,64,256]{3,2,1,0:T(8,128)(2,1)} %collective-permute-done.10), channel_id=1, source_target_pairs={{0,224},{32,0},{64,32},{96,64},{128,96},{160,128},{192,160},{224,1... | collective-permute-start | bytes 589832 | tf_op jit(solution)/shard_map/ppermute | solution.py:30
  39.1 15.6 %collective-permute-start.14 = (bf16[3,2,64,256]{3,2,1,0:T(8,128)(2,1)}, bf16[3,2,64,256]{3,2,1,0:T(8,128)(2,1)S(1)}, u32[]{:S(2)}, u32[]{:S(2)}) collective-permute-start(bf16[3,2,64,256]{3,2,1,0:T(8,128)(2,1)} %collective-permute-done.13), channel_id=1, source_target_pairs={{0,32},{32,64},{64,96},{96,128},{128,160},{160,192},{192,224},{224... | collective-permute-start | bytes 589832 | tf_op jit(solution)/shard_map/ppermute | solution.py:27
  39.1 6.0 %collective-permute-start.2 = (bf16[3,2,64,256]{3,2,1,0:T(8,128)(2,1)}, bf16[3,2,64,256]{3,2,1,0:T(8,128)(2,1)S(1)}, u32[]{:S(2)}, u32[]{:S(2)}) collective-permute-start(bf16[3,2,64,256]{3,2,1,0:T(8,128)(2,1)} %collective-permute-done.1), channel_id=1, source_target_pairs={{0,4},{4,8},{8,12},{12,0},{1,5},{5,9},{9,13},{13,1},{2,6},{6,10},{... | collective-permute-start | bytes 589832 | tf_op jit(solution)/shard_map/ppermute | solution.py:27
  46.1 8.7 %copy-start.11 = (bf16[3,16,2,64,256]{4,3,2,0,1:T(8,128)(2,1)S(1)}, bf16[3,16,2,64,256]{4,3,2,0,1:T(8,128)(2,1)}, u32[]{:S(2)}) copy-start(bf16[3,16,2,64,256]{4,3,2,0,1:T(8,128)(2,1)} %bitcast_dynamic-update-slice_fusion.18) | copy-start | bytes 9437188
  48.2 35.0 %collective-permute-start.3 = (bf16[3,4,2,64,256]{4,3,2,1,0:T(8,128)(2,1)S(1)}, bf16[3,4,2,64,256]{4,3,2,1,0:T(8,128)(2,1)S(1)}, u32[]{:S(2)}, u32[]{:S(2)}) collective-permute-start(bf16[3,4,2,64,256]{4,3,2,1,0:T(8,128)(2,1)S(1)} %constant_dynamic-slice_fusion.1), channel_id=1, source_target_pairs={{0,32},{32,64},{64,96},{96,128},{128,160},{160,192},{192,224},{224... | collective-permute-start | bytes 2359304 | tf_op jit(solution)/shard_map/ppermute | solution.py:27
  49.4 34.5 %collective-permute-start.4 = (bf16[3,4,2,64,256]{4,3,2,1,0:T(8,128)(2,1)S(1)}, bf16[3,4,2,64,256]{4,3,2,1,0:T(8,128)(2,1)S(1)}, u32[]{:S(2)}, u32[]{:S(2)}) collective-permute-start(bf16[3,4,2,64,256]{4,3,2,1,0:T(8,128)(2,1)S(1)} %constant_dynamic-slice_fusion.1), channel_id=1, source_target_pairs={{0,224},{32,0},{64,32},{96,64},{128,96},{160,128},{192,160},{224,1... | collective-permute-start | bytes 2359304 | tf_op jit(solution)/shard_map/ppermute | solution.py:30
  51.6 20.4 %collective-permute-start.12 = (bf16[3,2,64,256]{3,2,1,0:T(8,128)(2,1)S(1)}, bf16[3,2,64,256]{3,2,1,0:T(8,128)(2,1)S(1)}, u32[]{:S(2)}, u32[]{:S(2)}) collective-permute-start(bf16[3,2,64,256]{3,2,1,0:T(8,128)(2,1)S(1)} %collective-permute-done.11), channel_id=1, source_target_pairs={{0,224},{32,0},{64,32},{96,64},{128,96},{160,128},{192,160},{224,1... | collective-permute-start | bytes 589832 | tf_op jit(solution)/shard_map/ppermute | solution.py:30
  54.8 15.7 %collective-permute-start.15 = (bf16[3,2,64,256]{3,2,1,0:T(8,128)(2,1)S(1)}, bf16[3,2,64,256]{3,2,1,0:T(8,128)(2,1)S(1)}, u32[]{:S(2)}, u32[]{:S(2)}) collective-permute-start(bf16[3,2,64,256]{3,2,1,0:T(8,128)(2,1)S(1)} %collective-permute-done.14), channel_id=1, source_target_pairs={{0,32},{32,64},{64,96},{96,128},{128,160},{160,192},{192,224},{224... | collective-permute-start | bytes 589832 | tf_op jit(solution)/shard_map/ppermute | solution.py:27
  70.5 6.6 %collective-permute-start.16 = (bf16[3,2,64,256]{3,2,1,0:T(8,128)(2,1)S(1)}, bf16[3,2,64,256]{3,2,1,0:T(8,128)(2,1)S(1)}, u32[]{:S(2)}, u32[]{:S(2)}) collective-permute-start(bf16[3,2,64,256]{3,2,1,0:T(8,128)(2,1)S(1)} %collective-permute-done.15), channel_id=1, source_target_pairs={{0,32},{32,64},{64,96},{96,128},{128,160},{160,192},{192,224},{224... | collective-permute-start | bytes 589832 | tf_op jit(solution)/shard_map/ppermute | solution.py:27
  80.1 1.5 copy-start.3
  80.3 34.5 %collective-permute-start.17 = (bf16[3,8,2,64,256]{4,3,2,0,1:T(8,128)(2,1)S(1)}, bf16[3,8,2,64,256]{4,3,2,0,1:T(8,128)(2,1)S(1)}, u32[]{:S(2)}, u32[]{:S(2)}) collective-permute-start(bf16[3,8,2,64,256]{4,3,2,0,1:T(8,128)(2,1)S(1)} %constant_dynamic-slice_fusion), channel_id=1, source_target_pairs={{0,4},{4,8},{8,12},{12,0},{1,5},{5,9},{9,13},{13,1},{2,6},{6,10},{... | collective-permute-start | bytes 4718600 | tf_op jit(solution)/shard_map/ppermute | solution.py:27
  82.2 4.4 %copy-start.6 = (bf16[1,512,8,2,64]{1,4,0,3,2:T(8,128)(2,1)S(1)}, bf16[1,512,8,2,64]{1,4,0,3,2:T(8,128)(2,1)}, u32[]{:S(2)}) copy-start(bf16[1,512,8,2,64]{1,4,0,3,2:T(8,128)(2,1)} %get-tuple-element.7) | copy-start | bytes 3145732
  82.2 35.0 %collective-permute-start.18 = (bf16[3,8,2,64,256]{4,3,2,0,1:T(8,128)(2,1)S(1)}, bf16[3,8,2,64,256]{4,3,2,0,1:T(8,128)(2,1)S(1)}, u32[]{:S(2)}, u32[]{:S(2)}) collective-permute-start(bf16[3,8,2,64,256]{4,3,2,0,1:T(8,128)(2,1)S(1)} %constant_dynamic-slice_fusion), channel_id=1, source_target_pairs={{0,12},{4,0},{8,4},{12,8},{1,13},{5,1},{9,5},{13,9},{2,14},{6,2},{... | collective-permute-start | bytes 4718600 | tf_op jit(solution)/shard_map/ppermute | solution.py:30
  83.2 18.1 %collective-permute-start.5 = (bf16[3,4,2,64,256]{4,3,2,1,0:T(8,128)(2,1)S(1)}, bf16[3,4,2,64,256]{4,3,2,1,0:T(8,128)(2,1)S(1)}, u32[]{:S(2)}, u32[]{:S(2)}) collective-permute-start(bf16[3,4,2,64,256]{4,3,2,1,0:T(8,128)(2,1)S(1)} %collective-permute-done.3), channel_id=1, source_target_pairs={{0,32},{32,64},{64,96},{96,128},{128,160},{160,192},{192,224},{224... | collective-permute-start | bytes 2359304 | tf_op jit(solution)/shard_map/ppermute | solution.py:27
  83.9 17.7 %collective-permute-start.6 = (bf16[3,4,2,64,256]{4,3,2,1,0:T(8,128)(2,1)S(1)}, bf16[3,4,2,64,256]{4,3,2,1,0:T(8,128)(2,1)S(1)}, u32[]{:S(2)}, u32[]{:S(2)}) collective-permute-start(bf16[3,4,2,64,256]{4,3,2,1,0:T(8,128)(2,1)S(1)} %collective-permute-done.4), channel_id=1, source_target_pairs={{0,224},{32,0},{64,32},{96,64},{128,96},{160,128},{192,160},{224,1... | collective-permute-start | bytes 2359304 | tf_op jit(solution)/shard_map/ppermute | solution.py:30
  86.6 1.0 copy-start.1
  87.7 1.1 copy-start.2
  89.3 15.6 %copy-start = (bf16[1,512,4,2,64]{1,4,3,2,0:T(8,128)(2,1)S(1)}, bf16[1,512,4,2,64]{1,4,3,2,0:T(8,128)(2,1)}, u32[]{:S(2)}) copy-start(bf16[1,512,4,2,64]{1,4,3,2,0:T(8,128)(2,1)} %copy.52) | copy-start | bytes 1572868
  101.3 16.1 %collective-permute-start.7 = (bf16[3,4,2,64,256]{4,3,2,1,0:T(8,128)(2,1)S(1)}, bf16[3,4,2,64,256]{4,3,2,1,0:T(8,128)(2,1)S(1)}, u32[]{:S(2)}, u32[]{:S(2)}) collective-permute-start(bf16[3,4,2,64,256]{4,3,2,1,0:T(8,128)(2,1)S(1)} %collective-permute-done.5), channel_id=1, source_target_pairs={{0,32},{32,64},{64,96},{96,128},{128,160},{160,192},{192,224},{224... | collective-permute-start | bytes 2359304 | tf_op jit(solution)/shard_map/ppermute | solution.py:27
  101.6 18.4 %collective-permute-start.8 = (bf16[3,4,2,64,256]{4,3,2,1,0:T(8,128)(2,1)S(1)}, bf16[3,4,2,64,256]{4,3,2,1,0:T(8,128)(2,1)S(1)}, u32[]{:S(2)}, u32[]{:S(2)}) collective-permute-start(bf16[3,4,2,64,256]{4,3,2,1,0:T(8,128)(2,1)S(1)} %collective-permute-done.6), channel_id=1, source_target_pairs={{0,224},{32,0},{64,32},{96,64},{128,96},{160,128},{192,160},{224,1... | collective-permute-start | bytes 2359304 | tf_op jit(solution)/shard_map/ppermute | solution.py:30
  105.5 10.7 %copy-start.5 = (bf16[1,512,8,2,64]{1,4,0,3,2:T(8,128)(2,1)S(1)}, bf16[1,512,8,2,64]{1,4,0,3,2:T(8,128)(2,1)}, u32[]{:S(2)}) copy-start(bf16[1,512,8,2,64]{1,4,0,3,2:T(8,128)(2,1)} %get-tuple-element.5) | copy-start | bytes 3145732
  114.9 33.0 %collective-permute-start.19 = (bf16[3,8,2,64,256]{4,3,2,0,1:T(8,128)(2,1)S(1)}, bf16[3,8,2,64,256]{4,3,2,0,1:T(8,128)(2,1)S(1)}, u32[]{:S(2)}, u32[]{:S(2)}) collective-permute-start(bf16[3,8,2,64,256]{4,3,2,0,1:T(8,128)(2,1)S(1)} %collective-permute-done.17), channel_id=1, source_target_pairs={{0,4},{4,8},{8,12},{12,0},{1,5},{5,9},{9,13},{13,1},{2,6},{6,10},{... | collective-permute-start | bytes 4718600 | tf_op jit(solution)/shard_map/ppermute | solution.py:27
  117.2 1.2 copy-start.4
  117.4 14.7 %collective-permute-start.9 = (bf16[3,4,2,64,256]{4,3,2,1,0:T(8,128)(2,1)S(1)}, bf16[3,4,2,64,256]{4,3,2,1,0:T(8,128)(2,1)S(1)}, u32[]{:S(2)}, u32[]{:S(2)}) collective-permute-start(bf16[3,4,2,64,256]{4,3,2,1,0:T(8,128)(2,1)S(1)} %collective-permute-done.7), channel_id=1, source_target_pairs={{0,32},{32,64},{64,96},{96,128},{128,160},{160,192},{192,224},{224... | collective-permute-start | bytes 2359304 | tf_op jit(solution)/shard_map/ppermute | solution.py:27
  149.4 6.4 %collective-permute-start.20 = (f32[4,128,128]{2,1,0:T(8,128)S(1)}, f32[4,128,128]{2,1,0:T(8,128)S(1)}, u32[]{:S(2)}, u32[]{:S(2)}) collective-permute-start(f32[4,128,128]{2,1,0:T(8,128)S(1)} %fusion.47), channel_id=1, source_target_pairs={{0,4},{4,8},{8,12},{12,0},{1,5},{5,9},{9,13},{13,1},{2,6},{6,10},{... | collective-permute-start | bytes 786440 | tf_op jit(solution)/shard_map/ppermute | solution.py:49
  150.7 8.0 %collective-permute-start.21 = (f32[4,128,128]{2,1,0:T(8,128)S(1)}, f32[4,128,128]{2,1,0:T(8,128)S(1)}, u32[]{:S(2)}, u32[]{:S(2)}) collective-permute-start(f32[4,128,128]{2,1,0:T(8,128)S(1)} %fusion.47), channel_id=1, source_target_pairs={{0,8},{4,12},{8,0},{12,4},{1,9},{5,13},{9,1},{13,5},{2,10},{6,14},... | collective-permute-start | bytes 786440 | tf_op jit(solution)/shard_map/ppermute | solution.py:49
  151.2 10.2 %collective-permute-start.22 = (f32[4,128,128]{2,1,0:T(8,128)S(1)}, f32[4,128,128]{2,1,0:T(8,128)S(1)}, u32[]{:S(2)}, u32[]{:S(2)}) collective-permute-start(f32[4,128,128]{2,1,0:T(8,128)S(1)} %fusion.47), channel_id=1, source_target_pairs={{0,12},{4,0},{8,4},{12,8},{1,13},{5,1},{9,5},{13,9},{2,14},{6,2},{... | collective-permute-start | bytes 786440 | tf_op jit(solution)/shard_map/ppermute | solution.py:49
  161.5 8.0 %collective-permute-start.23 = (f32[4,128,128]{2,1,0:T(8,128)S(1)}, f32[4,128,128]{2,1,0:T(8,128)S(1)}, u32[]{:S(2)}, u32[]{:S(2)}) collective-permute-start(f32[4,128,128]{2,1,0:T(8,128)S(1)} %add_add_fusion.1), channel_id=1, source_target_pairs={{0,16},{16,0},{1,17},{17,1},{2,18},{18,2},{3,19},{19,3},{4,20},{20... | collective-permute-start | bytes 786440 | tf_op jit(solution)/shard_map/ppermute | solution.py:49
  169.5 0.7 copy-start.7
  169.5 7.7 %collective-permute-start.24 = (f32[4,128,128]{2,1,0:T(8,128)S(1)}, f32[4,128,128]{2,1,0:T(8,128)S(1)}, u32[]{:S(2)}, u32[]{:S(2)}) collective-permute-start(f32[4,128,128]{2,1,0:T(8,128)S(1)} %add.168), channel_id=1, source_target_pairs={{0,32},{32,64},{64,96},{96,0},{128,160},{160,192},{192,224},{224,1... | collective-permute-start | bytes 786440 | tf_op jit(solution)/shard_map/ppermute | solution.py:49
  170.2 20.0 %collective-permute-start.25 = (f32[4,128,128]{2,1,0:T(8,128)S(1)}, f32[4,128,128]{2,1,0:T(8,128)S(1)}, u32[]{:S(2)}, u32[]{:S(2)}) collective-permute-start(f32[4,128,128]{2,1,0:T(8,128)S(1)} %add.168), channel_id=1, source_target_pairs={{0,64},{32,96},{64,0},{96,32},{128,192},{160,224},{192,128},{224,1... | collective-permute-start | bytes 786440 | tf_op jit(solution)/shard_map/ppermute | solution.py:49
  175.2 18.1 %collective-permute-start.26 = (f32[4,128,128]{2,1,0:T(8,128)S(1)}, f32[4,128,128]{2,1,0:T(8,128)S(1)}, u32[]{:S(2)}, u32[]{:S(2)}) collective-permute-start(f32[4,128,128]{2,1,0:T(8,128)S(1)} %add.168), channel_id=1, source_target_pairs={{0,96},{32,0},{64,32},{96,64},{128,224},{160,128},{192,160},{224,1... | collective-permute-start | bytes 786440 | tf_op jit(solution)/shard_map/ppermute | solution.py:49
  177.2 18.7 %copy-start.8 = (f32[4,128,128]{2,1,0:T(8,128)}, f32[4,128,128]{2,1,0:T(8,128)S(1)}, u32[]{:S(2)}) copy-start(f32[4,128,128]{2,1,0:T(8,128)S(1)} %collective-permute-done.24) | copy-start | bytes 786436
  190.2 5.6 %copy-start.9 = (f32[4,128,128]{2,1,0:T(8,128)}, f32[4,128,128]{2,1,0:T(8,128)S(1)}, u32[]{:S(2)}) copy-start(f32[4,128,128]{2,1,0:T(8,128)S(1)} %collective-permute-done.25) | copy-start | bytes 786436
  193.3 2.5 %copy-start.10 = (f32[4,128,128]{2,1,0:T(8,128)}, f32[4,128,128]{2,1,0:T(8,128)S(1)}, u32[]{:S(2)}) copy-start(f32[4,128,128]{2,1,0:T(8,128)S(1)} %collective-permute-done.26) | copy-start | bytes 786436
  194.1 13.2 %collective-permute-start.27 = (f32[4,128,128]{2,1,0:T(8,128)}, f32[4,128,128]{2,1,0:T(8,128)}, u32[]{:S(2)}, u32[]{:S(2)}) collective-permute-start(f32[4,128,128]{2,1,0:T(8,128)} %add_add_fusion), channel_id=1, source_target_pairs={{0,128},{32,160},{64,192},{96,224},{128,0},{160,32},{192,64},{224,... | collective-permute-start | bytes 786440 | tf_op jit(solution)/shard_map/ppermute | solution.py:69

commit v4 on v3

--- a/solution.py
+++ b/solution.py
@@ -85,12 +85,25 @@
 
     def last_stage(x, name, toks):
         n = SIZES[name]
-        pieces = [(0, x)] + [((n - d) % n, v) for d, v in ring_values(x, name, n)]
+        count = len(ws)
+        x = x.reshape(count, -1, k, x.shape[-1])
+        toks = toks.reshape(n, t, -1, k)
+        right = [(j, (j + 1) % n) for j in range(n)]
+        left = [(j, (j - 1) % n) for j in range(n)]
+        half = k // 2
+        pieces = [(0, x, 0, k)]
+        r = l = x
+        for d in range(1, n // 2 + 1):
+            if d < n - d:
+                r = lax.ppermute(r, name, right)
+                l = lax.ppermute(l, name, left)
+                pieces += [(n - d, r, 0, k), (d, l, 0, k)]
+            else:
+                pieces.append((d, lax.ppermute(r[:, :, :half], name, right), 0, half))
+                pieces.append((d, lax.ppermute(l[:, :, half:], name, left), half, k))
         out = None
-        for m, v in pieces:
-            part = jnp.einsum(
-                "tk,wkn->wtn", toks[m], v.reshape(len(ws), -1, v.shape[-1]), preferred_element_type=jnp.float32
-            )
+        for m, v, lo, hi in pieces:
+            part = jnp.einsum("tjk,wjkn->wtn", toks[m][:, :, lo:hi], v, preferred_element_type=jnp.float32)
             out = part if out is None else out + part
         return out
 

time: 211 us -> 192 us (0.910)
  waiting for transfers between devices: 114 us -> 85.1 us
  starting transfers between devices: 39.3 us -> 48.7 us
    ppermute x12 -> x6, waiting for transfers between devices: 71.7 us -> 23 us  [ring_values(): r = lax.ppermute(r, name, right)]
    ppermute x0 -> x12, waiting for transfers between devices: none -> 27.6 us  [the longest x4 21.8 us: last_stage(): r = lax.ppermute(r, name, right)]
    ppermute x0 -> x12, starting transfers between devices: none -> 17.6 us  [the longest x4 7.14 us: last_stage(): l = lax.ppermute(l, name, left)]
    ppermute x8 -> x4, starting transfers between devices: 16.5 us -> 8.02 us  [ring_values(): l = lax.ppermute(l, name, left)]
    ppermute x12 -> x6, starting transfers between devices: 11.7 us -> 6.37 us  [ring_values(): r = lax.ppermute(r, name, right)]
    ppermute x1, waiting for transfers between devices: 9.14 us -> 4.4 us  [prefix_over_ctx(): lax.ppermute(total_zl, 'z', [(j, (j + half) % SIZES['z']) for j in range(...]
    ppermute x1, starting transfers between devices: 1.72 us -> 6.34 us  [prefix_over_ctx(): lax.ppermute(total_zl, 'z', [(j, (j + half) % SIZES['z']) for j in range(...]
    ppermute x7, waiting for transfers between devices: 33.5 us -> 30.1 us  [direct_values(): got.append((k, lax.ppermute(x, name, pairs)))]
  transfers between devices with their start and end apart: 28 -> 30, of which waited for: 15 -> 15; matrix products, arithmetic and copies ran while one was open for 19% -> 20% of each run, Pallas kernels for 0% -> 0%
where the time goes in v4:
time: 192 us; the launch traced here: 191 us
  waiting for transfers between devices  85.1 us (44%)
  starting transfers between devices  48.7 us (25%)
  local copies, waits for them, and re-layouts  24.5 us (13%)
  matrix products  14 us (7%)
  other arithmetic  9.06 us (5%)
  blocking collectives  8.81 us (5%)
    ppermute x7, waiting for transfers between devices, direct_values(): got.append((k, lax.ppermute(x, name, pairs)))  30.1 us
    ppermute x6, waiting for transfers between devices, ring_values(): r = lax.ppermute(r, name, right)  23 us
    ppermute x4, waiting for transfers between devices, last_stage(): r = lax.ppermute(r, name, right)  21.8 us
    unnamed x51, local copies, waits for them, and re-layouts  13 us
    ppermute x7, starting transfers between devices, direct_values(): got.append((k, lax.ppermute(x, name, pairs)))  10.4 us
    dot_general x14, matrix products, last_stage(): jnp.einsum('tjk,wjkn->wtn', toks[m][:, :, lo:hi], v, preferred_element_ty...  9.63 us
    all_gather x1, blocking collectives, project(): g = lax.all_gather(w, 'xh', axis=1)  8.81 us
    slice x10, local copies, waits for them, and re-layouts, last_stage(): toks[m][:, :, lo:hi]  8.2 us
  transfers between devices with their start and end apart: 30, of which 15 were waited for; matrix products, arithmetic and copies ran while one was open for 20% of the time, Pallas kernels for 0%

profile of v4, /device:TPU:62, one launch (start us, length us, event | category | flops | bytes accessed | tf_op | source)
XLA Modules:
  0.0 190.7 jit_solution(8605838861174503518)
XLA Ops:
  0.0 0.9 pad_maximum_fusion.1
  0.9 8.8 %all-gather = bf16[3,128,512]{2,1,0:T(8,128)(2,1)S(1)} all-gather(bf16[3,64,512]{2,1,0:T(8,128)(2,1)S(1)} %pad_maximum_fusion.1), channel_id=2, replica_groups=mesh['z'=8,'xh'=2,'y'=4,'hd'=4] {'xh'}, dimensions={1}, use_global_device_ids=true | all-gather | bytes 589824 | tf_op jit(solution)/shard_map/all_gather | solution.py:76
  9.7 0.8 fusion.41
  10.7 1.9 %collective-permute-start.14 = (bf16[3,2,64,256]{3,2,1,0:T(8,128)(2,1)}, bf16[3,2,64,256]{3,2,1,0:T(8,128)(2,1)S(1)}, u32[]{:S(2)}, u32[]{:S(2)}) collective-permute-start(bf16[3,2,64,256]{3,2,1,0:T(8,128)(2,1)} %get-tuple-element.20), channel_id=1, source_target_pairs={{0,32},{32,64},{64,96},{96,128},{128,160},{160,192},{192,224},{224... | collective-permute-start | bytes 589832 | tf_op jit(solution)/shard_map/ppermute | solution.py:27
  13.3 2.5 %collective-permute-start.1 = (bf16[3,2,64,256]{3,2,1,0:T(8,128)(2,1)}, bf16[3,2,64,256]{3,2,1,0:T(8,128)(2,1)}, u32[]{:S(2)}, u32[]{:S(2)}) collective-permute-start(bf16[3,2,64,256]{3,2,1,0:T(8,128)(2,1)} %get-tuple-element.21), channel_id=1, source_target_pairs={{0,4},{4,8},{8,12},{12,0},{1,5},{5,9},{9,13},{13,1},{2,6},{6,10},{... | collective-permute-start | bytes 589832 | tf_op jit(solution)/shard_map/ppermute | solution.py:27
  16.5 6.5 %copy.24 = bf16[512,4096]{0,1:T(8,128)(2,1)} copy(bf16[512,4096]{1,0:T(8,128)(2,1)} %param.4) | data formatting | bytes 8388608 | tf_op args[0]
  23.0 3.1 %fusion = bf16[4,512,8,2,64]{1,4,0,3,2:T(8,128)(2,1)S(1)} fusion(s32[]{:T(128)S(6)} %select_n.119, bf16[4,512,8,2,64]{1,4,0,3,2:T(8,128)(2,1)} %bitcast.234), kind=kLoop, calls=%fused_computation.4 | loop fusion | flops 2097152 | bytes 8388612 | tf_op jit(solution)/shard_map/jit(_roll_dynamic)/concatenate | solution.py:84
  26.1 1.8 fusion.39
  27.9 3.1 %fusion.1 = bf16[8,512,4,2,64]{1,4,2,3,0:T(8,128)(2,1)S(1)} fusion(s32[]{:T(128)S(6)} %select_n.115, bf16[8,512,4,2,64]{1,4,2,3,0:T(8,128)(2,1)} %bitcast.235), kind=kLoop, calls=%fused_computation.5 | loop fusion | flops 2097152 | bytes 8388612 | tf_op jit(solution)/shard_map/jit(_roll_dynamic)/concatenate | solution.py:83
  31.5 0.8 copy.32
  32.4 0.8 copy.30
  33.2 0.8 copy.28
  34.0 0.9 copy.29
  34.9 0.8 copy.26
  35.7 0.8 copy.27
  36.6 0.8 copy.25
  37.5 4.0 %collective-permute-start.12 = (bf16[3,2,64,256]{3,2,1,0:T(8,128)(2,1)S(1)}, bf16[3,2,64,256]{3,2,1,0:T(8,128)(2,1)S(1)}, u32[]{:S(2)}, u32[]{:S(2)}) collective-permute-start(bf16[3,2,64,256]{3,2,1,0:T(8,128)(2,1)S(1)} %collective-permute-done.11), channel_id=1, source_target_pairs={{0,224},{32,0},{64,32},{96,64},{128,96},{160,128},{192,160},{224,1... | collective-permute-start | bytes 589832 | tf_op jit(solution)/shard_map/ppermute | solution.py:30
  42.3 0.9 bitcast_dynamic-update-slice_fusion.2
  43.3 4.2 %collective-permute-done.2 = bf16[3,2,64,256]{3,2,1,0:T(8,128)(2,1)S(1)} collective-permute-done((bf16[3,2,64,256]{3,2,1,0:T(8,128)(2,1)}, bf16[3,2,64,256]{3,2,1,0:T(8,128)(2,1)S(1)}, u32[]{:S(2)}, u32[]{:S(2)}) %collective-permute-start.2) | collective-permute-done | bytes 196640 | tf_op jit(solution)/shard_map/ppermute | solution.py:27
  47.5 0.9 bitcast_dynamic-update-slice_fusion.22
  48.5 1.0 bitcast_dynamic-update-slice_fusion.3
  49.5 0.9 bitcast_dynamic-update-slice_fusion.23
  50.5 1.2 collective-permute-start.3
  51.7 2.2 %collective-permute-start.4 = (bf16[3,8,64,256]{3,2,1,0:T(8,128)(2,1)S(1)}, bf16[3,8,64,256]{3,2,1,0:T(8,128)(2,1)S(1)}, u32[]{:S(2)}, u32[]{:S(2)}) collective-permute-start(bf16[3,8,64,256]{3,2,1,0:T(8,128)(2,1)S(1)} %bitcast.258), channel_id=1, source_target_pairs={{0,224},{32,0},{64,32},{96,64},{128,96},{160,128},{192,160},{224,1... | collective-permute-start | bytes 2359304 | tf_op jit(solution)/shard_map/ppermute | solution.py:99
  53.9 3.2 %collective-permute-start.13 = (bf16[3,2,64,256]{3,2,1,0:T(8,128)(2,1)S(1)}, bf16[3,2,64,256]{3,2,1,0:T(8,128)(2,1)S(1)}, u32[]{:S(2)}, u32[]{:S(2)}) collective-permute-start(bf16[3,2,64,256]{3,2,1,0:T(8,128)(2,1)S(1)} %collective-permute-done.12), channel_id=1, source_target_pairs={{0,224},{32,0},{64,32},{96,64},{128,96},{160,128},{192,160},{224,1... | collective-permute-start | bytes 589832 | tf_op jit(solution)/shard_map/ppermute | solution.py:30
  58.0 1.0 copy-done.6
  59.0 13.7 %collective-permute-done.16 = bf16[3,2,64,256]{3,2,1,0:T(8,128)(2,1)S(1)} collective-permute-done((bf16[3,2,64,256]{3,2,1,0:T(8,128)(2,1)S(1)}, bf16[3,2,64,256]{3,2,1,0:T(8,128)(2,1)S(1)}, u32[]{:S(2)}, u32[]{:S(2)}) %collective-permute-start.16) | collective-permute-done | bytes 196640 | tf_op jit(solution)/shard_map/ppermute | solution.py:27
  72.7 1.6 collective-permute-start.17
  74.3 5.1 %collective-permute-done.17 = bf16[3,2,64,256]{3,2,1,0:T(8,128)(2,1)S(1)} collective-permute-done((bf16[3,2,64,256]{3,2,1,0:T(8,128)(2,1)S(1)}, bf16[3,2,64,256]{3,2,1,0:T(8,128)(2,1)S(1)}, u32[]{:S(2)}, u32[]{:S(2)}) %collective-permute-start.17) | collective-permute-done | bytes 196640 | tf_op jit(solution)/shard_map/ppermute | solution.py:27
  80.0 1.3 collective-permute-start.18
  81.3 0.8 collective-permute-start.19
  82.1 1.2 collective-permute-start.5
  83.4 2.1 %collective-permute-start.6 = (bf16[3,8,64,256]{3,2,1,0:T(8,128)(2,1)S(1)}, bf16[3,8,64,256]{3,2,1,0:T(8,128)(2,1)S(1)}, u32[]{:S(2)}, u32[]{:S(2)}) collective-permute-start(bf16[3,8,64,256]{3,2,1,0:T(8,128)(2,1)S(1)} %collective-permute-done.4), channel_id=1, source_target_pairs={{0,224},{32,0},{64,32},{96,64},{128,96},{160,128},{192,160},{224,1... | collective-permute-start | bytes 2359304 | tf_op jit(solution)/shard_map/ppermute | solution.py:99
  85.5 1.0 fusion.48
  88.2 12.0 %collective-permute-done.5 = bf16[3,8,64,256]{3,2,1,0:T(8,128)(2,1)S(1)} collective-permute-done((bf16[3,8,64,256]{3,2,1,0:T(8,128)(2,1)S(1)}, bf16[3,8,64,256]{3,2,1,0:T(8,128)(2,1)S(1)}, u32[]{:S(2)}, u32[]{:S(2)}) %collective-permute-start.5) | collective-permute-done | bytes 786464 | tf_op jit(solution)/shard_map/ppermute | solution.py:98
  100.1 0.9 collective-permute-start.7
  101.1 2.0 %collective-permute-start.8 = (bf16[3,8,64,256]{3,2,1,0:T(8,128)(2,1)S(1)}, bf16[3,8,64,256]{3,2,1,0:T(8,128)(2,1)S(1)}, u32[]{:S(2)}, u32[]{:S(2)}) collective-permute-start(bf16[3,8,64,256]{3,2,1,0:T(8,128)(2,1)S(1)} %collective-permute-done.6), channel_id=1, source_target_pairs={{0,224},{32,0},{64,32},{96,64},{128,96},{160,128},{192,160},{224,1... | collective-permute-start | bytes 2359304 | tf_op jit(solution)/shard_map/ppermute | solution.py:99
  104.8 9.8 %collective-permute-done.18 = bf16[3,16,64,256]{3,2,1,0:T(8,128)(2,1)S(1)} collective-permute-done((bf16[3,16,64,256]{3,2,1,0:T(8,128)(2,1)S(1)}, bf16[3,16,64,256]{3,2,1,0:T(8,128)(2,1)S(1)}, u32[]{:S(2)}, u32[]{:S(2)}) %collective-permute-start.18) | collective-permute-done | bytes 1572896 | tf_op jit(solution)/shard_map/ppermute | solution.py:98
  114.6 1.3 collective-permute-start.20
  116.0 0.9 collective-permute-start.21
  116.9 1.0 fusion.49
  117.9 1.3 collective-permute-start.9
  119.2 1.0 fusion.50
  120.2 2.4 %collective-permute-start.10 = (bf16[3,8,32,256]{3,2,1,0:T(8,128)(2,1)S(1)}, bf16[3,8,32,256]{3,2,1,0:T(8,128)(2,1)S(1)}, u32[]{:S(2)}, u32[]{:S(2)}) collective-permute-start(bf16[3,8,32,256]{3,2,1,0:T(8,128)(2,1)S(1)} %slice.128), channel_id=1, source_target_pairs={{0,224},{32,0},{64,32},{96,64},{128,96},{160,128},{192,160},{224,1... | collective-permute-start | bytes 1179656 | tf_op jit(solution)/shard_map/ppermute | solution.py:103
  123.2 3.8 %collective-permute-done.9 = bf16[3,8,32,256]{3,2,1,0:T(8,128)(2,1)S(1)} collective-permute-done((bf16[3,8,32,256]{3,2,1,0:T(8,128)(2,1)S(1)}, bf16[3,8,32,256]{3,2,1,0:T(8,128)(2,1)S(1)}, u32[]{:S(2)}, u32[]{:S(2)}) %collective-permute-start.9) | collective-permute-done | bytes 393248 | tf_op jit(solution)/shard_map/ppermute | solution.py:102
  127.4 1.4 collective-permute-done.10
  131.2 0.9 fusion.6
  132.5 1.3 collective-permute-start.22
  133.8 0.9 collective-permute-start.23
  134.7 4.2 %collective-permute-done.22 = f32[4,128,128]{2,1,0:T(8,128)S(1)} collective-permute-done((f32[4,128,128]{2,1,0:T(8,128)S(1)}, f32[4,128,128]{2,1,0:T(8,128)S(1)}, u32[]{:S(2)}, u32[]{:S(2)}) %collective-permute-start.22) | collective-permute-done | bytes 262176 | tf_op jit(solution)/shard_map/ppermute | solution.py:49
  139.0 2.8 %collective-permute-done.23 = f32[4,128,128]{2,1,0:T(8,128)S(1)} collective-permute-done((f32[4,128,128]{2,1,0:T(8,128)S(1)}, f32[4,128,128]{2,1,0:T(8,128)S(1)}, u32[]{:S(2)}, u32[]{:S(2)}) %collective-permute-start.23) | collective-permute-done | bytes 262176 | tf_op jit(solution)/shard_map/ppermute | solution.py:49
  141.8 2.7 %collective-permute-done.24 = f32[4,128,128]{2,1,0:T(8,128)S(1)} collective-permute-done((f32[4,128,128]{2,1,0:T(8,128)S(1)}, f32[4,128,128]{2,1,0:T(8,128)S(1)}, u32[]{:S(2)}, u32[]{:S(2)}) %collective-permute-start.24) | collective-permute-done | bytes 262176 | tf_op jit(solution)/shard_map/ppermute | solution.py:49
  144.5 1.5 collective-permute-start.25
  146.0 6.5 %collective-permute-done.25 = f32[4,128,128]{2,1,0:T(8,128)S(1)} collective-permute-done((f32[4,128,128]{2,1,0:T(8,128)S(1)}, f32[4,128,128]{2,1,0:T(8,128)S(1)}, u32[]{:S(2)}, u32[]{:S(2)}) %collective-permute-start.25) | collective-permute-done | bytes 262176 | tf_op jit(solution)/shard_map/ppermute | solution.py:49
  152.5 2.1 %collective-permute-start.26 = (f32[4,128,128]{2,1,0:T(8,128)S(1)}, f32[4,128,128]{2,1,0:T(8,128)S(1)}, u32[]{:S(2)}, u32[]{:S(2)}) collective-permute-start(f32[4,128,128]{2,1,0:T(8,128)S(1)} %add.177), channel_id=1, source_target_pairs={{0,32},{32,64},{64,96},{96,0},{128,160},{160,192},{192,224},{224,1... | collective-permute-start | bytes 786440 | tf_op jit(solution)/shard_map/ppermute | solution.py:49
  154.6 3.4 %collective-permute-start.27 = (f32[4,128,128]{2,1,0:T(8,128)S(1)}, f32[4,128,128]{2,1,0:T(8,128)S(1)}, u32[]{:S(2)}, u32[]{:S(2)}) collective-permute-start(f32[4,128,128]{2,1,0:T(8,128)S(1)} %add.177), channel_id=1, source_target_pairs={{0,64},{32,96},{64,0},{96,32},{128,192},{160,224},{192,128},{224,1... | collective-permute-start | bytes 786440 | tf_op jit(solution)/shard_map/ppermute | solution.py:49
  158.0 1.2 collective-permute-start.28
  160.0 10.6 %collective-permute-done.27 = f32[4,128,128]{2,1,0:T(8,128)S(1)} collective-permute-done((f32[4,128,128]{2,1,0:T(8,128)S(1)}, f32[4,128,128]{2,1,0:T(8,128)S(1)}, u32[]{:S(2)}, u32[]{:S(2)}) %collective-permute-start.27) | collective-permute-done | bytes 262176 | tf_op jit(solution)/shard_map/ppermute | solution.py:49
  170.7 3.2 %collective-permute-done.28 = f32[4,128,128]{2,1,0:T(8,128)S(1)} collective-permute-done((f32[4,128,128]{2,1,0:T(8,128)S(1)}, f32[4,128,128]{2,1,0:T(8,128)S(1)}, u32[]{:S(2)}, u32[]{:S(2)}) %collective-permute-start.28) | collective-permute-done | bytes 262176 | tf_op jit(solution)/shard_map/ppermute | solution.py:49
  174.7 6.3 %collective-permute-start.29 = (f32[4,128,128]{2,1,0:T(8,128)}, f32[4,128,128]{2,1,0:T(8,128)}, u32[]{:S(2)}, u32[]{:S(2)}) collective-permute-start(f32[4,128,128]{2,1,0:T(8,128)} %add_add_fusion), channel_id=1, source_target_pairs={{0,128},{32,160},{64,192},{96,224},{128,0},{160,32},{192,64},{224,... | collective-permute-start | bytes 786440 | tf_op jit(solution)/shard_map/ppermute | solution.py:69
  181.1 2.3 %fusion.2 = f32[4,128,512]{2,1,0:T(8,128)S(1)} fusion(bf16[512,4,128]{0,2,1:T(8,128)(2,1)S(1)} %bitcast.246, bf16[512,4,128]{0,2,1:T(8,128)(2,1)S(1)} %bitcast.247, bf16[512,4,128]{0,2,1:T(8,128)(2,1)S(1)} %bitcast.244, pred[512,512]{1,0:T(8,128)(4,1)} %iota_compare_fusion), kind=kOutput, calls=%fused_computation.11 | convolution fusion | flops 538968064 | bytes 2883584 | tf_op jit(solution)/shard_map/hqk,khd->qhd/dot_general | solution.py:128
  183.4 4.4 %collective-permute-done.29 = f32[4,128,128]{2,1,0:T(8,128)} collective-permute-done((f32[4,128,128]{2,1,0:T(8,128)}, f32[4,128,128]{2,1,0:T(8,128)}, u32[]{:S(2)}, u32[]{:S(2)}) %collective-permute-start.29) | collective-permute-done | bytes 262176 | tf_op jit(solution)/shard_map/ppermute | solution.py:69
  187.8 1.7 multiply_reduce_fusion
  189.7 1.0 copy.37
  (96 shorter events, 13.6 us)
Async XLA Ops:
  10.5 27.0 %collective-permute-start.11 = (bf16[3,2,64,256]{3,2,1,0:T(8,128)(2,1)}, bf16[3,2,64,256]{3,2,1,0:T(8,128)(2,1)S(1)}, u32[]{:S(2)}, u32[]{:S(2)}) collective-permute-start(bf16[3,2,64,256]{3,2,1,0:T(8,128)(2,1)} %get-tuple-element.20), channel_id=1, source_target_pairs={{0,224},{32,0},{64,32},{96,64},{128,96},{160,128},{192,160},{224,1... | collective-permute-start | bytes 589832 | tf_op jit(solution)/shard_map/ppermute | solution.py:30
  10.7 30.9 %collective-permute-start.14 = (bf16[3,2,64,256]{3,2,1,0:T(8,128)(2,1)}, bf16[3,2,64,256]{3,2,1,0:T(8,128)(2,1)S(1)}, u32[]{:S(2)}, u32[]{:S(2)}) collective-permute-start(bf16[3,2,64,256]{3,2,1,0:T(8,128)(2,1)} %get-tuple-element.20), channel_id=1, source_target_pairs={{0,32},{32,64},{64,96},{96,128},{128,160},{160,192},{192,224},{224... | collective-permute-start | bytes 589832 | tf_op jit(solution)/shard_map/ppermute | solution.py:27
  12.6 29.8 %collective-permute-start = (bf16[3,2,64,256]{3,2,1,0:T(8,128)(2,1)}, bf16[3,2,64,256]{3,2,1,0:T(8,128)(2,1)}, u32[]{:S(2)}, u32[]{:S(2)}) collective-permute-start(bf16[3,2,64,256]{3,2,1,0:T(8,128)(2,1)} %get-tuple-element.21), channel_id=1, source_target_pairs={{0,12},{4,0},{8,4},{12,8},{1,13},{5,1},{9,5},{13,9},{2,14},{6,2},{... | collective-permute-start | bytes 589832 | tf_op jit(solution)/shard_map/ppermute | solution.py:30
  13.3 28.2 %collective-permute-start.1 = (bf16[3,2,64,256]{3,2,1,0:T(8,128)(2,1)}, bf16[3,2,64,256]{3,2,1,0:T(8,128)(2,1)}, u32[]{:S(2)}, u32[]{:S(2)}) collective-permute-start(bf16[3,2,64,256]{3,2,1,0:T(8,128)(2,1)} %get-tuple-element.21), channel_id=1, source_target_pairs={{0,4},{4,8},{8,12},{12,0},{1,5},{5,9},{9,13},{13,1},{2,6},{6,10},{... | collective-permute-start | bytes 589832 | tf_op jit(solution)/shard_map/ppermute | solution.py:27
  37.5 16.4 %collective-permute-start.12 = (bf16[3,2,64,256]{3,2,1,0:T(8,128)(2,1)S(1)}, bf16[3,2,64,256]{3,2,1,0:T(8,128)(2,1)S(1)}, u32[]{:S(2)}, u32[]{:S(2)}) collective-permute-start(bf16[3,2,64,256]{3,2,1,0:T(8,128)(2,1)S(1)} %collective-permute-done.11), channel_id=1, source_target_pairs={{0,224},{32,0},{64,32},{96,64},{128,96},{160,128},{192,160},{224,1... | collective-permute-start | bytes 589832 | tf_op jit(solution)/shard_map/ppermute | solution.py:30
  41.5 16.2 %collective-permute-start.15 = (bf16[3,2,64,256]{3,2,1,0:T(8,128)(2,1)S(1)}, bf16[3,2,64,256]{3,2,1,0:T(8,128)(2,1)S(1)}, u32[]{:S(2)}, u32[]{:S(2)}) collective-permute-start(bf16[3,2,64,256]{3,2,1,0:T(8,128)(2,1)S(1)} %collective-permute-done.14), channel_id=1, source_target_pairs={{0,32},{32,64},{64,96},{96,128},{128,160},{160,192},{192,224},{224... | collective-permute-start | bytes 589832 | tf_op jit(solution)/shard_map/ppermute | solution.py:27
  41.5 6.0 %collective-permute-start.2 = (bf16[3,2,64,256]{3,2,1,0:T(8,128)(2,1)}, bf16[3,2,64,256]{3,2,1,0:T(8,128)(2,1)S(1)}, u32[]{:S(2)}, u32[]{:S(2)}) collective-permute-start(bf16[3,2,64,256]{3,2,1,0:T(8,128)(2,1)} %collective-permute-done.1), channel_id=1, source_target_pairs={{0,4},{4,8},{8,12},{12,0},{1,5},{5,9},{9,13},{13,1},{2,6},{6,10},{... | collective-permute-start | bytes 589832 | tf_op jit(solution)/shard_map/ppermute | solution.py:27
  48.5 8.6 %copy-start.13 = (bf16[1,512,4,2,64]{1,4,3,2,0:T(8,128)(2,1)S(1)}, bf16[1,512,4,2,64]{1,4,3,2,0:T(8,128)(2,1)}, u32[]{:S(2)}) copy-start(bf16[1,512,4,2,64]{1,4,3,2,0:T(8,128)(2,1)} %copy.25) | copy-start | bytes 1572868
  50.5 31.6 %collective-permute-start.3 = (bf16[3,8,64,256]{3,2,1,0:T(8,128)(2,1)S(1)}, bf16[3,8,64,256]{3,2,1,0:T(8,128)(2,1)S(1)}, u32[]{:S(2)}, u32[]{:S(2)}) collective-permute-start(bf16[3,8,64,256]{3,2,1,0:T(8,128)(2,1)S(1)} %bitcast.257), channel_id=1, source_target_pairs={{0,32},{32,64},{64,96},{96,128},{128,160},{160,192},{192,224},{224... | collective-permute-start | bytes 2359304 | tf_op jit(solution)/shard_map/ppermute | solution.py:98
  51.7 31.6 %collective-permute-start.4 = (bf16[3,8,64,256]{3,2,1,0:T(8,128)(2,1)S(1)}, bf16[3,8,64,256]{3,2,1,0:T(8,128)(2,1)S(1)}, u32[]{:S(2)}, u32[]{:S(2)}) collective-permute-start(bf16[3,8,64,256]{3,2,1,0:T(8,128)(2,1)S(1)} %bitcast.258), channel_id=1, source_target_pairs={{0,224},{32,0},{64,32},{96,64},{128,96},{160,128},{192,160},{224,1... | collective-permute-start | bytes 2359304 | tf_op jit(solution)/shard_map/ppermute | solution.py:99
  53.9 20.4 %collective-permute-start.13 = (bf16[3,2,64,256]{3,2,1,0:T(8,128)(2,1)S(1)}, bf16[3,2,64,256]{3,2,1,0:T(8,128)(2,1)S(1)}, u32[]{:S(2)}, u32[]{:S(2)}) collective-permute-start(bf16[3,2,64,256]{3,2,1,0:T(8,128)(2,1)S(1)} %collective-permute-done.12), channel_id=1, source_target_pairs={{0,224},{32,0},{64,32},{96,64},{128,96},{160,128},{192,160},{224,1... | collective-permute-start | bytes 589832 | tf_op jit(solution)/shard_map/ppermute | solution.py:30
  57.1 1.9 copy-start.6
  57.7 15.0 %collective-permute-start.16 = (bf16[3,2,64,256]{3,2,1,0:T(8,128)(2,1)S(1)}, bf16[3,2,64,256]{3,2,1,0:T(8,128)(2,1)S(1)}, u32[]{:S(2)}, u32[]{:S(2)}) collective-permute-start(bf16[3,2,64,256]{3,2,1,0:T(8,128)(2,1)S(1)} %collective-permute-done.15), channel_id=1, source_target_pairs={{0,32},{32,64},{64,96},{96,128},{128,160},{160,192},{192,224},{224... | collective-permute-start | bytes 589832 | tf_op jit(solution)/shard_map/ppermute | solution.py:27
  72.7 6.7 %collective-permute-start.17 = (bf16[3,2,64,256]{3,2,1,0:T(8,128)(2,1)S(1)}, bf16[3,2,64,256]{3,2,1,0:T(8,128)(2,1)S(1)}, u32[]{:S(2)}, u32[]{:S(2)}) collective-permute-start(bf16[3,2,64,256]{3,2,1,0:T(8,128)(2,1)S(1)} %collective-permute-done.16), channel_id=1, source_target_pairs={{0,32},{32,64},{64,96},{96,128},{128,160},{160,192},{192,224},{224... | collective-permute-start | bytes 589832 | tf_op jit(solution)/shard_map/ppermute | solution.py:27
  79.9 5.6 %copy-start.1 = (bf16[1,512,8,2,64]{1,4,0,3,2:T(8,128)(2,1)S(1)}, bf16[1,512,8,2,64]{1,4,0,3,2:T(8,128)(2,1)}, u32[]{:S(2)}) copy-start(bf16[1,512,8,2,64]{1,4,0,3,2:T(8,128)(2,1)} %get-tuple-element.5) | copy-start | bytes 3145732
  80.0 34.5 %collective-permute-start.18 = (bf16[3,16,64,256]{3,2,1,0:T(8,128)(2,1)S(1)}, bf16[3,16,64,256]{3,2,1,0:T(8,128)(2,1)S(1)}, u32[]{:S(2)}, u32[]{:S(2)}) collective-permute-start(bf16[3,16,64,256]{3,2,1,0:T(8,128)(2,1)S(1)} %bitcast.249), channel_id=1, source_target_pairs={{0,4},{4,8},{8,12},{12,0},{1,5},{5,9},{9,13},{13,1},{2,6},{6,10},{... | collective-permute-start | bytes 4718600 | tf_op jit(solution)/shard_map/ppermute | solution.py:98
  81.3 34.6 %collective-permute-start.19 = (bf16[3,16,64,256]{3,2,1,0:T(8,128)(2,1)S(1)}, bf16[3,16,64,256]{3,2,1,0:T(8,128)(2,1)S(1)}, u32[]{:S(2)}, u32[]{:S(2)}) collective-permute-start(bf16[3,16,64,256]{3,2,1,0:T(8,128)(2,1)S(1)} %bitcast.250), channel_id=1, source_target_pairs={{0,12},{4,0},{8,4},{12,8},{1,13},{5,1},{9,5},{13,9},{2,14},{6,2},{... | collective-permute-start | bytes 4718600 | tf_op jit(solution)/shard_map/ppermute | solution.py:99
  82.1 18.0 %collective-permute-start.5 = (bf16[3,8,64,256]{3,2,1,0:T(8,128)(2,1)S(1)}, bf16[3,8,64,256]{3,2,1,0:T(8,128)(2,1)S(1)}, u32[]{:S(2)}, u32[]{:S(2)}) collective-permute-start(bf16[3,8,64,256]{3,2,1,0:T(8,128)(2,1)S(1)} %collective-permute-done.3), channel_id=1, source_target_pairs={{0,32},{32,64},{64,96},{96,128},{128,160},{160,192},{192,224},{224... | collective-permute-start | bytes 2359304 | tf_op jit(solution)/shard_map/ppermute | solution.py:98
  83.4 17.7 %collective-permute-start.6 = (bf16[3,8,64,256]{3,2,1,0:T(8,128)(2,1)S(1)}, bf16[3,8,64,256]{3,2,1,0:T(8,128)(2,1)S(1)}, u32[]{:S(2)}, u32[]{:S(2)}) collective-permute-start(bf16[3,8,64,256]{3,2,1,0:T(8,128)(2,1)S(1)} %collective-permute-done.4), channel_id=1, source_target_pairs={{0,224},{32,0},{64,32},{96,64},{128,96},{160,128},{192,160},{224,1... | collective-permute-start | bytes 2359304 | tf_op jit(solution)/shard_map/ppermute | solution.py:99
  85.5 1.0 copy-start.11
  86.5 1.0 copy-start.12
  87.6 15.5 %copy-start.9 = (bf16[1,512,4,2,64]{1,4,3,2,0:T(8,128)(2,1)S(1)}, bf16[1,512,4,2,64]{1,4,3,2,0:T(8,128)(2,1)}, u32[]{:S(2)}) copy-start(bf16[1,512,4,2,64]{1,4,3,2,0:T(8,128)(2,1)} %copy.28) | copy-start | bytes 1572868
  100.1 17.7 %collective-permute-start.7 = (bf16[3,8,64,256]{3,2,1,0:T(8,128)(2,1)S(1)}, bf16[3,8,64,256]{3,2,1,0:T(8,128)(2,1)S(1)}, u32[]{:S(2)}, u32[]{:S(2)}) collective-permute-start(bf16[3,8,64,256]{3,2,1,0:T(8,128)(2,1)S(1)} %collective-permute-done.5), channel_id=1, source_target_pairs={{0,32},{32,64},{64,96},{96,128},{128,160},{160,192},{192,224},{224... | collective-permute-start | bytes 2359304 | tf_op jit(solution)/shard_map/ppermute | solution.py:98
  101.1 19.1 %collective-permute-start.8 = (bf16[3,8,64,256]{3,2,1,0:T(8,128)(2,1)S(1)}, bf16[3,8,64,256]{3,2,1,0:T(8,128)(2,1)S(1)}, u32[]{:S(2)}, u32[]{:S(2)}) collective-permute-start(bf16[3,8,64,256]{3,2,1,0:T(8,128)(2,1)S(1)} %collective-permute-done.6), channel_id=1, source_target_pairs={{0,224},{32,0},{64,32},{96,64},{128,96},{160,128},{192,160},{224,1... | collective-permute-start | bytes 2359304 | tf_op jit(solution)/shard_map/ppermute | solution.py:99
  103.1 1.0 copy-start.10
  104.7 12.1 %copy-start = (bf16[1,512,8,2,64]{1,4,0,3,2:T(8,128)(2,1)S(1)}, bf16[1,512,8,2,64]{1,4,0,3,2:T(8,128)(2,1)}, u32[]{:S(2)}) copy-start(bf16[1,512,8,2,64]{1,4,0,3,2:T(8,128)(2,1)} %get-tuple-element.7) | copy-start | bytes 3145732
  114.6 14.6 %collective-permute-start.20 = (bf16[3,16,32,256]{3,2,1,0:T(8,128)(2,1)S(1)}, bf16[3,16,32,256]{3,2,1,0:T(8,128)(2,1)S(1)}, u32[]{:S(2)}, u32[]{:S(2)}) collective-permute-start(bf16[3,16,32,256]{3,2,1,0:T(8,128)(2,1)S(1)} %slice.134), channel_id=1, source_target_pairs={{0,4},{4,8},{8,12},{12,0},{1,5},{5,9},{9,13},{13,1},{2,6},{6,10},{... | collective-permute-start | bytes 2359304 | tf_op jit(solution)/shard_map/ppermute | solution.py:102
  116.0 14.4 %collective-permute-start.21 = (bf16[3,16,32,256]{3,2,1,0:T(8,128)(2,1)S(1)}, bf16[3,16,32,256]{3,2,1,0:T(8,128)(2,1)S(1)}, u32[]{:S(2)}, u32[]{:S(2)}) collective-permute-start(bf16[3,16,32,256]{3,2,1,0:T(8,128)(2,1)S(1)} %slice.137), channel_id=1, source_target_pairs={{0,12},{4,0},{8,4},{12,8},{1,13},{5,1},{9,5},{13,9},{2,14},{6,2},{... | collective-permute-start | bytes 2359304 | tf_op jit(solution)/shard_map/ppermute | solution.py:103
  117.9 9.1 %collective-permute-start.9 = (bf16[3,8,32,256]{3,2,1,0:T(8,128)(2,1)S(1)}, bf16[3,8,32,256]{3,2,1,0:T(8,128)(2,1)S(1)}, u32[]{:S(2)}, u32[]{:S(2)}) collective-permute-start(bf16[3,8,32,256]{3,2,1,0:T(8,128)(2,1)S(1)} %slice.125), channel_id=1, source_target_pairs={{0,32},{32,64},{64,96},{96,128},{128,160},{160,192},{192,224},{224... | collective-permute-start | bytes 1179656 | tf_op jit(solution)/shard_map/ppermute | solution.py:102
  119.2 3.4 %copy-start.8 = (bf16[1,512,4,2,64]{1,4,3,2,0:T(8,128)(2,1)S(1)}, bf16[1,512,4,2,64]{1,4,3,2,0:T(8,128)(2,1)}, u32[]{:S(2)}) copy-start(bf16[1,512,4,2,64]{1,4,3,2,0:T(8,128)(2,1)} %copy.30) | copy-start | bytes 1572868
  120.2 8.5 %collective-permute-start.10 = (bf16[3,8,32,256]{3,2,1,0:T(8,128)(2,1)S(1)}, bf16[3,8,32,256]{3,2,1,0:T(8,128)(2,1)S(1)}, u32[]{:S(2)}, u32[]{:S(2)}) collective-permute-start(bf16[3,8,32,256]{3,2,1,0:T(8,128)(2,1)S(1)} %slice.128), channel_id=1, source_target_pairs={{0,224},{32,0},{64,32},{96,64},{128,96},{160,128},{192,160},{224,1... | collective-permute-start | bytes 1179656 | tf_op jit(solution)/shard_map/ppermute | solution.py:103
  122.6 4.4 %copy-start.7 = (bf16[1,512,4,2,64]{1,4,3,2,0:T(8,128)(2,1)S(1)}, bf16[1,512,4,2,64]{1,4,3,2,0:T(8,128)(2,1)}, u32[]{:S(2)}) copy-start(bf16[1,512,4,2,64]{1,4,3,2,0:T(8,128)(2,1)} %copy.32) | copy-start | bytes 1572868
  132.5 6.4 %collective-permute-start.22 = (f32[4,128,128]{2,1,0:T(8,128)S(1)}, f32[4,128,128]{2,1,0:T(8,128)S(1)}, u32[]{:S(2)}, u32[]{:S(2)}) collective-permute-start(f32[4,128,128]{2,1,0:T(8,128)S(1)} %fusion.51), channel_id=1, source_target_pairs={{0,4},{4,8},{8,12},{12,0},{1,5},{5,9},{9,13},{13,1},{2,6},{6,10},{... | collective-permute-start | bytes 786440 | tf_op jit(solution)/shard_map/ppermute | solution.py:49
  133.8 8.0 %collective-permute-start.23 = (f32[4,128,128]{2,1,0:T(8,128)S(1)}, f32[4,128,128]{2,1,0:T(8,128)S(1)}, u32[]{:S(2)}, u32[]{:S(2)}) collective-permute-start(f32[4,128,128]{2,1,0:T(8,128)S(1)} %fusion.51), channel_id=1, source_target_pairs={{0,8},{4,12},{8,0},{12,4},{1,9},{5,13},{9,1},{13,5},{2,10},{6,14},... | collective-permute-start | bytes 786440 | tf_op jit(solution)/shard_map/ppermute | solution.py:49
  134.7 9.8 %collective-permute-start.24 = (f32[4,128,128]{2,1,0:T(8,128)S(1)}, f32[4,128,128]{2,1,0:T(8,128)S(1)}, u32[]{:S(2)}, u32[]{:S(2)}) collective-permute-start(f32[4,128,128]{2,1,0:T(8,128)S(1)} %fusion.51), channel_id=1, source_target_pairs={{0,12},{4,0},{8,4},{12,8},{1,13},{5,1},{9,5},{13,9},{2,14},{6,2},{... | collective-permute-start | bytes 786440 | tf_op jit(solution)/shard_map/ppermute | solution.py:49
  144.5 8.0 %collective-permute-start.25 = (f32[4,128,128]{2,1,0:T(8,128)S(1)}, f32[4,128,128]{2,1,0:T(8,128)S(1)}, u32[]{:S(2)}, u32[]{:S(2)}) collective-permute-start(f32[4,128,128]{2,1,0:T(8,128)S(1)} %add_add_fusion.1), channel_id=1, source_target_pairs={{0,16},{16,0},{1,17},{17,1},{2,18},{18,2},{3,19},{19,3},{4,20},{20... | collective-permute-start | bytes 786440 | tf_op jit(solution)/shard_map/ppermute | solution.py:49
  152.5 2.1 %copy-start.2 = (f32[4,128,128]{2,1,0:T(8,128)}, f32[4,128,128]{2,1,0:T(8,128)S(1)}, u32[]{:S(2)}) copy-start(f32[4,128,128]{2,1,0:T(8,128)S(1)} %collective-permute-done.25) | copy-start | bytes 786436
  152.5 7.5 %collective-permute-start.26 = (f32[4,128,128]{2,1,0:T(8,128)S(1)}, f32[4,128,128]{2,1,0:T(8,128)S(1)}, u32[]{:S(2)}, u32[]{:S(2)}) collective-permute-start(f32[4,128,128]{2,1,0:T(8,128)S(1)} %add.177), channel_id=1, source_target_pairs={{0,32},{32,64},{64,96},{96,0},{128,160},{160,192},{192,224},{224,1... | collective-permute-start | bytes 786440 | tf_op jit(solution)/shard_map/ppermute | solution.py:49
  154.6 16.0 %collective-permute-start.27 = (f32[4,128,128]{2,1,0:T(8,128)S(1)}, f32[4,128,128]{2,1,0:T(8,128)S(1)}, u32[]{:S(2)}, u32[]{:S(2)}) collective-permute-start(f32[4,128,128]{2,1,0:T(8,128)S(1)} %add.177), channel_id=1, source_target_pairs={{0,64},{32,96},{64,0},{96,32},{128,192},{160,224},{192,128},{224,1... | collective-permute-start | bytes 786440 | tf_op jit(solution)/shard_map/ppermute | solution.py:49
  158.0 15.9 %collective-permute-start.28 = (f32[4,128,128]{2,1,0:T(8,128)S(1)}, f32[4,128,128]{2,1,0:T(8,128)S(1)}, u32[]{:S(2)}, u32[]{:S(2)}) collective-permute-start(f32[4,128,128]{2,1,0:T(8,128)S(1)} %add.177), channel_id=1, source_target_pairs={{0,96},{32,0},{64,32},{96,64},{128,224},{160,128},{192,160},{224,1... | collective-permute-start | bytes 786440 | tf_op jit(solution)/shard_map/ppermute | solution.py:49
  160.0 21.0 %copy-start.3 = (f32[4,128,128]{2,1,0:T(8,128)}, f32[4,128,128]{2,1,0:T(8,128)S(1)}, u32[]{:S(2)}) copy-start(f32[4,128,128]{2,1,0:T(8,128)S(1)} %collective-permute-done.26) | copy-start | bytes 786436
  170.7 10.4 %copy-start.4 = (f32[4,128,128]{2,1,0:T(8,128)}, f32[4,128,128]{2,1,0:T(8,128)S(1)}, u32[]{:S(2)}) copy-start(f32[4,128,128]{2,1,0:T(8,128)S(1)} %collective-permute-done.27) | copy-start | bytes 786436
  173.9 7.1 %copy-start.5 = (f32[4,128,128]{2,1,0:T(8,128)}, f32[4,128,128]{2,1,0:T(8,128)S(1)}, u32[]{:S(2)}) copy-start(f32[4,128,128]{2,1,0:T(8,128)S(1)} %collective-permute-done.28) | copy-start | bytes 786436
  174.7 13.1 %collective-permute-start.29 = (f32[4,128,128]{2,1,0:T(8,128)}, f32[4,128,128]{2,1,0:T(8,128)}, u32[]{:S(2)}, u32[]{:S(2)}) collective-permute-start(f32[4,128,128]{2,1,0:T(8,128)} %add_add_fusion), channel_id=1, source_target_pairs={{0,128},{32,160},{64,192},{96,224},{128,0},{160,32},{192,64},{224,... | collective-permute-start | bytes 786440 | tf_op jit(solution)/shard_map/ppermute | solution.py:69

commit v5 on v4

--- a/solution.py
+++ b/solution.py
@@ -73,7 +73,8 @@
 
 def project(tokens, ws, split):
     w = jnp.stack(ws)
-    g = lax.all_gather(w, "xh", axis=1)
+    other = lax.ppermute(w, "xh", [(0, 1), (1, 0)])
+    g = jnp.roll(jnp.stack([w, other], axis=1), lax.axis_index("xh"), axis=1)
     a, b = g[..., :split], g[..., split:]
     a = ring_gather(a, "y", axis=1)
     b = ring_gather(b, "z", axis=1)

time: 192 us -> 179 us (0.932)
  local copies, waits for them, and re-layouts: 24.5 us -> 11.7 us
  blocking collectives: 8.81 us -> 0 us
  waiting for transfers between devices: 85.1 us -> 92.8 us
    ppermute x4, waiting for transfers between devices: 21.8 us -> 32.8 us  [last_stage(): r = lax.ppermute(r, name, right)]
    all_gather x1 -> x0, blocking collectives: 8.81 us -> none  [project(): g = lax.all_gather(w, 'xh', axis=1)]
    ppermute x6, waiting for transfers between devices: 23 us -> 14.7 us  [ring_values(): r = lax.ppermute(r, name, right)]
    slice x10, local copies, waits for them, and re-layouts: 8.2 us -> 2.19 us  [last_stage(): toks[m][:, :, lo:hi]]
    unnamed x51 -> x30, local copies, waits for them, and re-layouts: 13 us -> 7.87 us
    ppermute x4, starting transfers between devices: 4.62 us -> 0.51 us  [last_stage(): r = lax.ppermute(r, name, right)]
    ppermute x4, starting transfers between devices: 7.14 us -> 11.2 us  [last_stage(): l = lax.ppermute(l, name, left)]
    ppermute x1, waiting for transfers between devices: 4.4 us -> 8.16 us  [prefix_over_ctx(): lax.ppermute(total_zl, 'z', [(j, (j + half) % SIZES['z']) for j in range(...]
  transfers between devices with their start and end apart: 30 -> 31, of which waited for: 15 -> 19; matrix products, arithmetic and copies ran while one was open for 20% -> 15% of each run, Pallas kernels for 0% -> 0%
where the time goes in v5:
time: 179 us; the launch traced here: 176 us
  waiting for transfers between devices  92.8 us (52%)
  starting transfers between devices  46.9 us (26%)
  matrix products  14 us (8%)
  local copies, waits for them, and re-layouts  11.7 us (7%)
  other arithmetic  10 us (6%)
    ppermute x4, waiting for transfers between devices, last_stage(): r = lax.ppermute(r, name, right)  32.8 us
    ppermute x7, waiting for transfers between devices, direct_values(): got.append((k, lax.ppermute(x, name, pairs)))  31.6 us
    ppermute x6, waiting for transfers between devices, ring_values(): r = lax.ppermute(r, name, right)  14.7 us
    ppermute x4, starting transfers between devices, last_stage(): l = lax.ppermute(l, name, left)  11.2 us
    ppermute x7, starting transfers between devices, direct_values(): got.append((k, lax.ppermute(x, name, pairs)))  11.2 us
    dot_general x14, matrix products, last_stage(): jnp.einsum('tjk,wjkn->wtn', toks[m][:, :, lo:hi], v, preferred_element_ty...  9.6 us
    ppermute x1, waiting for transfers between devices, prefix_over_ctx(): lax.ppermute(total_zl, 'z', [(j, (j + half) % SIZES['z']) for j in range(...  8.16 us
    unnamed x30, local copies, waits for them, and re-layouts  7.87 us
  transfers between devices with their start and end apart: 31, of which 19 were waited for; matrix products, arithmetic and copies ran while one was open for 15% of the time, Pallas kernels for 0%

profile of v5, /device:TPU:62, one launch (start us, length us, event | category | flops | bytes accessed | tf_op | source)
XLA Modules:
  0.0 175.9 jit_solution(2041920626899337149)
XLA Ops:
  0.0 1.6 pad_maximum_fusion.1
  1.6 1.4 collective-permute-start
  3.0 6.5 %copy.14 = bf16[512,4096]{0,1:T(8,128)(2,1)} copy(bf16[512,4096]{1,0:T(8,128)(2,1)} %param.4) | data formatting | bytes 8388608 | tf_op args[0]
  9.5 3.1 %fusion = bf16[4,512,8,2,64]{1,4,0,3,2:T(8,128)(2,1)S(1)} fusion(s32[]{:T(128)S(6)} %select_n.129, bf16[4,512,8,2,64]{1,4,0,3,2:T(8,128)(2,1)} %bitcast.227), kind=kLoop, calls=%fused_computation.4 | loop fusion | flops 2097152 | bytes 8388612 | tf_op jit(solution)/shard_map/jit(_roll_dynamic)/concatenate | solution.py:85
  12.6 1.4 fusion.43
  14.0 3.1 %fusion.1 = bf16[8,512,4,2,64]{1,4,2,3,0:T(8,128)(2,1)S(1)} fusion(s32[]{:T(128)S(6)} %select_n.125, bf16[8,512,4,2,64]{1,4,2,3,0:T(8,128)(2,1)} %bitcast.228), kind=kLoop, calls=%fused_computation.5 | loop fusion | flops 2097152 | bytes 8388612 | tf_op jit(solution)/shard_map/jit(_roll_dynamic)/concatenate | solution.py:84
  17.6 1.9 %collective-permute-start.15 = (bf16[3,2,64,256]{3,2,0,1:T(8,128)(2,1)S(1)}, bf16[3,2,64,256]{3,2,0,1:T(8,128)(2,1)S(1)}, u32[]{:S(2)}, u32[]{:S(2)}) collective-permute-start(bf16[3,2,64,256]{3,2,0,1:T(8,128)(2,1)S(1)} %get-tuple-element.22), channel_id=1, source_target_pairs={{0,32},{32,64},{64,96},{96,128},{128,160},{160,192},{192,224},{224... | collective-permute-start | bytes 589832 | tf_op jit(solution)/shard_map/ppermute | solution.py:27
  19.6 0.7 collective-permute-start.1
  20.3 2.5 %collective-permute-start.2 = (bf16[3,2,64,256]{3,2,0,1:T(8,128)(2,1)S(1)}, bf16[3,2,64,256]{3,2,0,1:T(8,128)(2,1)S(1)}, u32[]{:S(2)}, u32[]{:S(2)}) collective-permute-start(bf16[3,2,64,256]{3,2,0,1:T(8,128)(2,1)S(1)} %get-tuple-element.23), channel_id=1, source_target_pairs={{0,4},{4,8},{8,12},{12,0},{1,5},{5,9},{9,13},{13,1},{2,6},{6,10},{... | collective-permute-start | bytes 589832 | tf_op jit(solution)/shard_map/ppermute | solution.py:27
  22.8 1.2 collective-permute-done.12
  24.1 3.3 %collective-permute-start.13 = (bf16[3,2,64,256]{3,2,0,1:T(8,128)(2,1)S(1)}, bf16[3,2,64,256]{3,2,0,1:T(8,128)(2,1)S(1)}, u32[]{:S(2)}, u32[]{:S(2)}) collective-permute-start(bf16[3,2,64,256]{3,2,0,1:T(8,128)(2,1)S(1)} %collective-permute-done.12), channel_id=1, source_target_pairs={{0,224},{32,0},{64,32},{96,64},{128,96},{160,128},{192,160},{224,1... | collective-permute-start | bytes 589832 | tf_op jit(solution)/shard_map/ppermute | solution.py:30
  27.4 0.5 collective-permute-done.15
  27.8 2.0 %collective-permute-start.3 = (bf16[3,2,64,256]{3,2,0,1:T(8,128)(2,1)S(1)}, bf16[3,2,64,256]{3,2,0,1:T(8,128)(2,1)S(1)}, u32[]{:S(2)}, u32[]{:S(2)}) collective-permute-start(bf16[3,2,64,256]{3,2,0,1:T(8,128)(2,1)S(1)} %collective-permute-done.2), channel_id=1, source_target_pairs={{0,4},{4,8},{8,12},{12,0},{1,5},{5,9},{9,13},{13,1},{2,6},{6,10},{... | collective-permute-start | bytes 589832 | tf_op jit(solution)/shard_map/ppermute | solution.py:27
  29.8 0.7 collective-permute-done.13
  30.5 3.7 %collective-permute-start.14 = (bf16[3,2,64,256]{3,2,0,1:T(8,128)(2,1)S(1)}, bf16[3,2,64,256]{3,2,0,1:T(8,128)(2,1)S(1)}, u32[]{:S(2)}, u32[]{:S(2)}) collective-permute-start(bf16[3,2,64,256]{3,2,0,1:T(8,128)(2,1)S(1)} %collective-permute-done.13), channel_id=1, source_target_pairs={{0,224},{32,0},{64,32},{96,64},{128,96},{160,128},{192,160},{224,1... | collective-permute-start | bytes 589832 | tf_op jit(solution)/shard_map/ppermute | solution.py:30
  34.2 0.5 collective-permute-done.16
  34.8 6.8 %collective-permute-done.17 = bf16[3,2,64,256]{3,2,0,1:T(8,128)(2,1)S(1)} collective-permute-done((bf16[3,2,64,256]{3,2,0,1:T(8,128)(2,1)S(1)}, bf16[3,2,64,256]{3,2,0,1:T(8,128)(2,1)S(1)}, u32[]{:S(2)}, u32[]{:S(2)}) %collective-permute-start.17) | collective-permute-done | bytes 196640 | tf_op jit(solution)/shard_map/ppermute | solution.py:27
  41.6 6.9 %collective-permute-done.18 = bf16[3,2,64,256]{3,2,0,1:T(8,128)(2,1)S(1)} collective-permute-done((bf16[3,2,64,256]{3,2,0,1:T(8,128)(2,1)S(1)}, bf16[3,2,64,256]{3,2,0,1:T(8,128)(2,1)S(1)}, u32[]{:S(2)}, u32[]{:S(2)}) %collective-permute-start.18) | collective-permute-done | bytes 196640 | tf_op jit(solution)/shard_map/ppermute | solution.py:27
  49.1 0.4 collective-permute-start.19
  49.6 1.9 %collective-permute-start.20 = (bf16[3,16,64,256]{3,2,1,0:T(8,128)(2,1)S(1)}, bf16[3,16,64,256]{3,2,1,0:T(8,128)(2,1)S(1)}, u32[]{:S(2)}, u32[]{:S(2)}) collective-permute-start(bf16[3,16,64,256]{3,2,1,0:T(8,128)(2,1)S(1)} %bitcast.238), channel_id=1, source_target_pairs={{0,12},{4,0},{8,4},{12,8},{1,13},{5,1},{9,5},{13,9},{2,14},{6,2},{... | collective-permute-start | bytes 4718600 | tf_op jit(solution)/shard_map/ppermute | solution.py:100
  51.7 3.3 %collective-permute-start.5 = (bf16[3,8,64,256]{3,2,1,0:T(8,128)(2,1)S(1)}, bf16[3,8,64,256]{3,2,1,0:T(8,128)(2,1)S(1)}, u32[]{:S(2)}, u32[]{:S(2)}) collective-permute-start(bf16[3,8,64,256]{3,2,1,0:T(8,128)(2,1)S(1)} %bitcast.246), channel_id=1, source_target_pairs={{0,224},{32,0},{64,32},{96,64},{128,96},{160,128},{192,160},{224,1... | collective-permute-start | bytes 2359304 | tf_op jit(solution)/shard_map/ppermute | solution.py:100
  55.0 0.5 fusion.44
  55.9 1.1 copy-done
  57.0 1.0 fusion.52
  58.0 11.7 %collective-permute-done.4 = bf16[3,8,64,256]{3,2,1,0:T(8,128)(2,1)S(1)} collective-permute-done((bf16[3,8,64,256]{3,2,1,0:T(8,128)(2,1)S(1)}, bf16[3,8,64,256]{3,2,1,0:T(8,128)(2,1)S(1)}, u32[]{:S(2)}, u32[]{:S(2)}) %collective-permute-start.4) | collective-permute-done | bytes 786464 | tf_op jit(solution)/shard_map/ppermute | solution.py:99
  69.7 0.6 fusion.46
  70.3 3.0 %collective-permute-start.7 = (bf16[3,8,64,256]{3,2,1,0:T(8,128)(2,1)S(1)}, bf16[3,8,64,256]{3,2,1,0:T(8,128)(2,1)S(1)}, u32[]{:S(2)}, u32[]{:S(2)}) collective-permute-start(bf16[3,8,64,256]{3,2,1,0:T(8,128)(2,1)S(1)} %collective-permute-done.5), channel_id=1, source_target_pairs={{0,224},{32,0},{64,32},{96,64},{128,96},{160,128},{192,160},{224,1... | collective-permute-start | bytes 2359304 | tf_op jit(solution)/shard_map/ppermute | solution.py:100
  73.3 0.6 fusion.47
  73.9 0.6 fusion.48
  74.5 9.3 %collective-permute-done.19 = bf16[3,16,64,256]{3,2,1,0:T(8,128)(2,1)S(1)} collective-permute-done((bf16[3,16,64,256]{3,2,1,0:T(8,128)(2,1)S(1)}, bf16[3,16,64,256]{3,2,1,0:T(8,128)(2,1)S(1)}, u32[]{:S(2)}, u32[]{:S(2)}) %collective-permute-start.19) | collective-permute-done | bytes 1572896 | tf_op jit(solution)/shard_map/ppermute | solution.py:99
  84.2 1.9 %collective-permute-start.22 = (bf16[3,16,32,256]{3,2,1,0:T(8,128)(2,1)S(1)}, bf16[3,16,32,256]{3,2,1,0:T(8,128)(2,1)S(1)}, u32[]{:S(2)}, u32[]{:S(2)}) collective-permute-start(bf16[3,16,32,256]{3,2,1,0:T(8,128)(2,1)S(1)} %slice.137), channel_id=1, source_target_pairs={{0,12},{4,0},{8,4},{12,8},{1,13},{5,1},{9,5},{13,9},{2,14},{6,2},{... | collective-permute-start | bytes 2359304 | tf_op jit(solution)/shard_map/ppermute | solution.py:104
  86.1 0.7 collective-permute-done.6
  86.8 1.0 fusion.53
  87.8 3.0 %collective-permute-start.9 = (bf16[3,8,64,256]{3,2,1,0:T(8,128)(2,1)S(1)}, bf16[3,8,64,256]{3,2,1,0:T(8,128)(2,1)S(1)}, u32[]{:S(2)}, u32[]{:S(2)}) collective-permute-start(bf16[3,8,64,256]{3,2,1,0:T(8,128)(2,1)S(1)} %collective-permute-done.7), channel_id=1, source_target_pairs={{0,224},{32,0},{64,32},{96,64},{128,96},{160,128},{192,160},{224,1... | collective-permute-start | bytes 2359304 | tf_op jit(solution)/shard_map/ppermute | solution.py:100
  90.9 1.0 fusion.54
  91.9 0.6 fusion.49
  92.5 0.6 fusion.50
  93.1 11.1 %collective-permute-done.8 = bf16[3,8,64,256]{3,2,1,0:T(8,128)(2,1)S(1)} collective-permute-done((bf16[3,8,64,256]{3,2,1,0:T(8,128)(2,1)S(1)}, bf16[3,8,64,256]{3,2,1,0:T(8,128)(2,1)S(1)}, u32[]{:S(2)}, u32[]{:S(2)}) %collective-permute-start.8) | collective-permute-done | bytes 786464 | tf_op jit(solution)/shard_map/ppermute | solution.py:99
  104.6 3.1 %collective-permute-start.11 = (bf16[3,8,32,256]{3,2,1,0:T(8,128)(2,1)S(1)}, bf16[3,8,32,256]{3,2,1,0:T(8,128)(2,1)S(1)}, u32[]{:S(2)}, u32[]{:S(2)}) collective-permute-start(bf16[3,8,32,256]{3,2,1,0:T(8,128)(2,1)S(1)} %slice.128), channel_id=1, source_target_pairs={{0,224},{32,0},{64,32},{96,64},{128,96},{160,128},{192,160},{224,1... | collective-permute-start | bytes 1179656 | tf_op jit(solution)/shard_map/ppermute | solution.py:104
  107.7 0.6 fusion.10
  108.3 0.7 fusion.7
  109.1 0.6 fusion.51
  109.7 3.6 %collective-permute-done.10 = bf16[3,8,32,256]{3,2,1,0:T(8,128)(2,1)S(1)} collective-permute-done((bf16[3,8,32,256]{3,2,1,0:T(8,128)(2,1)S(1)}, bf16[3,8,32,256]{3,2,1,0:T(8,128)(2,1)S(1)}, u32[]{:S(2)}, u32[]{:S(2)}) %collective-permute-start.10) | collective-permute-done | bytes 393248 | tf_op jit(solution)/shard_map/ppermute | solution.py:103
  113.6 0.4 fusion.14
  114.0 0.9 fusion.6
  115.4 1.0 collective-permute-start.23
  116.4 2.1 %collective-permute-start.24 = (f32[4,128,128]{2,1,0:T(8,128)S(1)}, f32[4,128,128]{2,1,0:T(8,128)S(1)}, u32[]{:S(2)}, u32[]{:S(2)}) collective-permute-start(f32[4,128,128]{2,1,0:T(8,128)S(1)} %fusion.55), channel_id=1, source_target_pairs={{0,8},{4,12},{8,0},{12,4},{1,9},{5,13},{9,1},{13,5},{2,10},{6,14},... | collective-permute-start | bytes 786440 | tf_op jit(solution)/shard_map/ppermute | solution.py:49
  118.5 3.3 %collective-permute-done.23 = f32[4,128,128]{2,1,0:T(8,128)S(1)} collective-permute-done((f32[4,128,128]{2,1,0:T(8,128)S(1)}, f32[4,128,128]{2,1,0:T(8,128)S(1)}, u32[]{:S(2)}, u32[]{:S(2)}) %collective-permute-start.23) | collective-permute-done | bytes 262176 | tf_op jit(solution)/shard_map/ppermute | solution.py:49
  121.8 2.6 %collective-permute-done.24 = f32[4,128,128]{2,1,0:T(8,128)S(1)} collective-permute-done((f32[4,128,128]{2,1,0:T(8,128)S(1)}, f32[4,128,128]{2,1,0:T(8,128)S(1)}, u32[]{:S(2)}, u32[]{:S(2)}) %collective-permute-start.24) | collective-permute-done | bytes 262176 | tf_op jit(solution)/shard_map/ppermute | solution.py:49
  124.4 2.7 %collective-permute-done.25 = f32[4,128,128]{2,1,0:T(8,128)S(1)} collective-permute-done((f32[4,128,128]{2,1,0:T(8,128)S(1)}, f32[4,128,128]{2,1,0:T(8,128)S(1)}, u32[]{:S(2)}, u32[]{:S(2)}) %collective-permute-start.25) | collective-permute-done | bytes 262176 | tf_op jit(solution)/shard_map/ppermute | solution.py:49
  127.2 2.2 %collective-permute-start.26 = (f32[4,128,128]{2,1,0:T(8,128)S(1)}, f32[4,128,128]{2,1,0:T(8,128)S(1)}, u32[]{:S(2)}, u32[]{:S(2)}) collective-permute-start(f32[4,128,128]{2,1,0:T(8,128)S(1)} %add_add_fusion.1), channel_id=1, source_target_pairs={{0,16},{16,0},{1,17},{17,1},{2,18},{18,2},{3,19},{19,3},{4,20},{20... | collective-permute-start | bytes 786440 | tf_op jit(solution)/shard_map/ppermute | solution.py:49
  129.4 5.8 %collective-permute-done.26 = f32[4,128,128]{2,1,0:T(8,128)S(1)} collective-permute-done((f32[4,128,128]{2,1,0:T(8,128)S(1)}, f32[4,128,128]{2,1,0:T(8,128)S(1)}, u32[]{:S(2)}, u32[]{:S(2)}) %collective-permute-start.26) | collective-permute-done | bytes 262176 | tf_op jit(solution)/shard_map/ppermute | solution.py:49
  135.2 1.1 collective-permute-start.27
  136.3 4.6 %collective-permute-start.28 = (f32[4,128,128]{2,1,0:T(8,128)S(1)}, f32[4,128,128]{2,1,0:T(8,128)S(1)}, u32[]{:S(2)}, u32[]{:S(2)}) collective-permute-start(f32[4,128,128]{2,1,0:T(8,128)S(1)} %add.186), channel_id=1, source_target_pairs={{0,64},{32,96},{64,0},{96,32},{128,192},{160,224},{192,128},{224,1... | collective-permute-start | bytes 786440 | tf_op jit(solution)/shard_map/ppermute | solution.py:49
  141.0 0.8 iota_compare_fusion
  141.7 1.1 collective-permute-done.27
  142.8 13.0 %collective-permute-done.28 = f32[4,128,128]{2,1,0:T(8,128)S(1)} collective-permute-done((f32[4,128,128]{2,1,0:T(8,128)S(1)}, f32[4,128,128]{2,1,0:T(8,128)S(1)}, u32[]{:S(2)}, u32[]{:S(2)}) %collective-permute-start.28) | collective-permute-done | bytes 262176 | tf_op jit(solution)/shard_map/ppermute | solution.py:49
  155.9 3.1 %collective-permute-done.29 = f32[4,128,128]{2,1,0:T(8,128)S(1)} collective-permute-done((f32[4,128,128]{2,1,0:T(8,128)S(1)}, f32[4,128,128]{2,1,0:T(8,128)S(1)}, u32[]{:S(2)}, u32[]{:S(2)}) %collective-permute-start.29) | collective-permute-done | bytes 262176 | tf_op jit(solution)/shard_map/ppermute | solution.py:49
  159.0 0.8 add_add_fusion
  159.8 2.7 %collective-permute-start.30 = (f32[4,128,128]{2,1,0:T(8,128)}, f32[4,128,128]{2,1,0:T(8,128)}, u32[]{:S(2)}, u32[]{:S(2)}) collective-permute-start(f32[4,128,128]{2,1,0:T(8,128)} %add_add_fusion), channel_id=1, source_target_pairs={{0,128},{32,160},{64,192},{96,224},{128,0},{160,32},{192,64},{224,... | collective-permute-start | bytes 786440 | tf_op jit(solution)/shard_map/ppermute | solution.py:69
  162.5 2.3 %fusion.2 = f32[4,128,512]{2,1,0:T(8,128)S(1)} fusion(bf16[512,4,128]{0,2,1:T(8,128)(2,1)S(1)} %bitcast.234, bf16[512,4,128]{0,2,1:T(8,128)(2,1)S(1)} %bitcast.235, bf16[512,4,128]{0,2,1:T(8,128)(2,1)S(1)} %bitcast.232, pred[512,512]{1,0:T(8,128)(4,1)} %iota_compare_fusion), kind=kOutput, calls=%fused_computation.11 | convolution fusion | flops 538968064 | bytes 2883584 | tf_op jit(solution)/shard_map/hqk,khd->qhd/dot_general | solution.py:129
  164.8 8.2 %collective-permute-done.30 = f32[4,128,128]{2,1,0:T(8,128)} collective-permute-done((f32[4,128,128]{2,1,0:T(8,128)}, f32[4,128,128]{2,1,0:T(8,128)}, u32[]{:S(2)}, u32[]{:S(2)}) %collective-permute-start.30) | collective-permute-done | bytes 262176 | tf_op jit(solution)/shard_map/ppermute | solution.py:69
  173.0 1.7 multiply_reduce_fusion
  174.9 1.0 copy.27
  (78 shorter events, 3.6 us)
Async XLA Ops:
  1.6 15.5 %collective-permute-start = (bf16[3,64,512]{2,1,0:T(8,128)(2,1)}, bf16[3,64,512]{2,1,0:T(8,128)(2,1)S(1)}, u32[]{:S(2)}, u32[]{:S(2)}) collective-permute-start(bf16[3,64,512]{2,1,0:T(8,128)(2,1)} %get-tuple-element.26), channel_id=1, source_target_pairs={{0,16},{16,0},{1,17},{17,1},{2,18},{18,2},{3,19},{19,3},{4,20},{20... | collective-permute-start | bytes 589832 | tf_op jit(solution)/shard_map/ppermute | solution.py:76
  17.5 6.6 %collective-permute-start.12 = (bf16[3,2,64,256]{3,2,0,1:T(8,128)(2,1)S(1)}, bf16[3,2,64,256]{3,2,0,1:T(8,128)(2,1)S(1)}, u32[]{:S(2)}, u32[]{:S(2)}) collective-permute-start(bf16[3,2,64,256]{3,2,0,1:T(8,128)(2,1)S(1)} %get-tuple-element.22), channel_id=1, source_target_pairs={{0,224},{32,0},{64,32},{96,64},{128,96},{160,128},{192,160},{224,1... | collective-permute-start | bytes 589832 | tf_op jit(solution)/shard_map/ppermute | solution.py:30
  17.6 10.2 %collective-permute-start.15 = (bf16[3,2,64,256]{3,2,0,1:T(8,128)(2,1)S(1)}, bf16[3,2,64,256]{3,2,0,1:T(8,128)(2,1)S(1)}, u32[]{:S(2)}, u32[]{:S(2)}) collective-permute-start(bf16[3,2,64,256]{3,2,0,1:T(8,128)(2,1)S(1)} %get-tuple-element.22), channel_id=1, source_target_pairs={{0,32},{32,64},{64,96},{96,128},{128,160},{160,192},{192,224},{224... | collective-permute-start | bytes 589832 | tf_op jit(solution)/shard_map/ppermute | solution.py:27
  19.6 10.3 %collective-permute-start.1 = (bf16[3,2,64,256]{3,2,0,1:T(8,128)(2,1)S(1)}, bf16[3,2,64,256]{3,2,0,1:T(8,128)(2,1)S(1)}, u32[]{:S(2)}, u32[]{:S(2)}) collective-permute-start(bf16[3,2,64,256]{3,2,0,1:T(8,128)(2,1)S(1)} %get-tuple-element.23), channel_id=1, source_target_pairs={{0,12},{4,0},{8,4},{12,8},{1,13},{5,1},{9,5},{13,9},{2,14},{6,2},{... | collective-permute-start | bytes 589832 | tf_op jit(solution)/shard_map/ppermute | solution.py:30
  20.3 7.6 %collective-permute-start.2 = (bf16[3,2,64,256]{3,2,0,1:T(8,128)(2,1)S(1)}, bf16[3,2,64,256]{3,2,0,1:T(8,128)(2,1)S(1)}, u32[]{:S(2)}, u32[]{:S(2)}) collective-permute-start(bf16[3,2,64,256]{3,2,0,1:T(8,128)(2,1)S(1)} %get-tuple-element.23), channel_id=1, source_target_pairs={{0,4},{4,8},{8,12},{12,0},{1,5},{5,9},{9,13},{13,1},{2,6},{6,10},{... | collective-permute-start | bytes 589832 | tf_op jit(solution)/shard_map/ppermute | solution.py:27
  24.1 6.5 %collective-permute-start.13 = (bf16[3,2,64,256]{3,2,0,1:T(8,128)(2,1)S(1)}, bf16[3,2,64,256]{3,2,0,1:T(8,128)(2,1)S(1)}, u32[]{:S(2)}, u32[]{:S(2)}) collective-permute-start(bf16[3,2,64,256]{3,2,0,1:T(8,128)(2,1)S(1)} %collective-permute-done.12), channel_id=1, source_target_pairs={{0,224},{32,0},{64,32},{96,64},{128,96},{160,128},{192,160},{224,1... | collective-permute-start | bytes 589832 | tf_op jit(solution)/shard_map/ppermute | solution.py:30
  27.8 6.9 %collective-permute-start.16 = (bf16[3,2,64,256]{3,2,0,1:T(8,128)(2,1)S(1)}, bf16[3,2,64,256]{3,2,0,1:T(8,128)(2,1)S(1)}, u32[]{:S(2)}, u32[]{:S(2)}) collective-permute-start(bf16[3,2,64,256]{3,2,0,1:T(8,128)(2,1)S(1)} %collective-permute-done.15), channel_id=1, source_target_pairs={{0,32},{32,64},{64,96},{96,128},{128,160},{160,192},{192,224},{224... | collective-permute-start | bytes 589832 | tf_op jit(solution)/shard_map/ppermute | solution.py:27
  27.8 6.9 %collective-permute-start.3 = (bf16[3,2,64,256]{3,2,0,1:T(8,128)(2,1)S(1)}, bf16[3,2,64,256]{3,2,0,1:T(8,128)(2,1)S(1)}, u32[]{:S(2)}, u32[]{:S(2)}) collective-permute-start(bf16[3,2,64,256]{3,2,0,1:T(8,128)(2,1)S(1)} %collective-permute-done.2), channel_id=1, source_target_pairs={{0,4},{4,8},{8,12},{12,0},{1,5},{5,9},{9,13},{13,1},{2,6},{6,10},{... | collective-permute-start | bytes 589832 | tf_op jit(solution)/shard_map/ppermute | solution.py:27
  30.5 11.0 %collective-permute-start.14 = (bf16[3,2,64,256]{3,2,0,1:T(8,128)(2,1)S(1)}, bf16[3,2,64,256]{3,2,0,1:T(8,128)(2,1)S(1)}, u32[]{:S(2)}, u32[]{:S(2)}) collective-permute-start(bf16[3,2,64,256]{3,2,0,1:T(8,128)(2,1)S(1)} %collective-permute-done.13), channel_id=1, source_target_pairs={{0,224},{32,0},{64,32},{96,64},{128,96},{160,128},{192,160},{224,1... | collective-permute-start | bytes 589832 | tf_op jit(solution)/shard_map/ppermute | solution.py:30
  34.7 6.9 %collective-permute-start.17 = (bf16[3,2,64,256]{3,2,0,1:T(8,128)(2,1)S(1)}, bf16[3,2,64,256]{3,2,0,1:T(8,128)(2,1)S(1)}, u32[]{:S(2)}, u32[]{:S(2)}) collective-permute-start(bf16[3,2,64,256]{3,2,0,1:T(8,128)(2,1)S(1)} %collective-permute-done.16), channel_id=1, source_target_pairs={{0,32},{32,64},{64,96},{96,128},{128,160},{160,192},{192,224},{224... | collective-permute-start | bytes 589832 | tf_op jit(solution)/shard_map/ppermute | solution.py:27
  41.6 7.0 %collective-permute-start.18 = (bf16[3,2,64,256]{3,2,0,1:T(8,128)(2,1)S(1)}, bf16[3,2,64,256]{3,2,0,1:T(8,128)(2,1)S(1)}, u32[]{:S(2)}, u32[]{:S(2)}) collective-permute-start(bf16[3,2,64,256]{3,2,0,1:T(8,128)(2,1)S(1)} %collective-permute-done.17), channel_id=1, source_target_pairs={{0,32},{32,64},{64,96},{96,128},{128,160},{160,192},{192,224},{224... | collective-permute-start | bytes 589832 | tf_op jit(solution)/shard_map/ppermute | solution.py:27
  49.1 34.7 %collective-permute-start.19 = (bf16[3,16,64,256]{3,2,1,0:T(8,128)(2,1)S(1)}, bf16[3,16,64,256]{3,2,1,0:T(8,128)(2,1)S(1)}, u32[]{:S(2)}, u32[]{:S(2)}) collective-permute-start(bf16[3,16,64,256]{3,2,1,0:T(8,128)(2,1)S(1)} %bitcast.237), channel_id=1, source_target_pairs={{0,4},{4,8},{8,12},{12,0},{1,5},{5,9},{9,13},{13,1},{2,6},{6,10},{... | collective-permute-start | bytes 4718600 | tf_op jit(solution)/shard_map/ppermute | solution.py:99
  49.6 34.6 %collective-permute-start.20 = (bf16[3,16,64,256]{3,2,1,0:T(8,128)(2,1)S(1)}, bf16[3,16,64,256]{3,2,1,0:T(8,128)(2,1)S(1)}, u32[]{:S(2)}, u32[]{:S(2)}) collective-permute-start(bf16[3,16,64,256]{3,2,1,0:T(8,128)(2,1)S(1)} %bitcast.238), channel_id=1, source_target_pairs={{0,12},{4,0},{8,4},{12,8},{1,13},{5,1},{9,5},{13,9},{2,14},{6,2},{... | collective-permute-start | bytes 4718600 | tf_op jit(solution)/shard_map/ppermute | solution.py:100
  51.6 18.1 %collective-permute-start.4 = (bf16[3,8,64,256]{3,2,1,0:T(8,128)(2,1)S(1)}, bf16[3,8,64,256]{3,2,1,0:T(8,128)(2,1)S(1)}, u32[]{:S(2)}, u32[]{:S(2)}) collective-permute-start(bf16[3,8,64,256]{3,2,1,0:T(8,128)(2,1)S(1)} %bitcast.245), channel_id=1, source_target_pairs={{0,32},{32,64},{64,96},{96,128},{128,160},{160,192},{192,224},{224... | collective-permute-start | bytes 2359304 | tf_op jit(solution)/shard_map/ppermute | solution.py:99
  51.7 18.6 %collective-permute-start.5 = (bf16[3,8,64,256]{3,2,1,0:T(8,128)(2,1)S(1)}, bf16[3,8,64,256]{3,2,1,0:T(8,128)(2,1)S(1)}, u32[]{:S(2)}, u32[]{:S(2)}) collective-permute-start(bf16[3,8,64,256]{3,2,1,0:T(8,128)(2,1)S(1)} %bitcast.246), channel_id=1, source_target_pairs={{0,224},{32,0},{64,32},{96,64},{128,96},{160,128},{192,160},{224,1... | collective-permute-start | bytes 2359304 | tf_op jit(solution)/shard_map/ppermute | solution.py:100
  55.7 1.2 copy-start
  69.7 17.2 %collective-permute-start.6 = (bf16[3,8,64,256]{3,2,1,0:T(8,128)(2,1)S(1)}, bf16[3,8,64,256]{3,2,1,0:T(8,128)(2,1)S(1)}, u32[]{:S(2)}, u32[]{:S(2)}) collective-permute-start(bf16[3,8,64,256]{3,2,1,0:T(8,128)(2,1)S(1)} %collective-permute-done.4), channel_id=1, source_target_pairs={{0,32},{32,64},{64,96},{96,128},{128,160},{160,192},{192,224},{224... | collective-permute-start | bytes 2359304 | tf_op jit(solution)/shard_map/ppermute | solution.py:99
  70.3 17.6 %collective-permute-start.7 = (bf16[3,8,64,256]{3,2,1,0:T(8,128)(2,1)S(1)}, bf16[3,8,64,256]{3,2,1,0:T(8,128)(2,1)S(1)}, u32[]{:S(2)}, u32[]{:S(2)}) collective-permute-start(bf16[3,8,64,256]{3,2,1,0:T(8,128)(2,1)S(1)} %collective-permute-done.5), channel_id=1, source_target_pairs={{0,224},{32,0},{64,32},{96,64},{128,96},{160,128},{192,160},{224,1... | collective-permute-start | bytes 2359304 | tf_op jit(solution)/shard_map/ppermute | solution.py:100
  83.9 23.9 %collective-permute-start.21 = (bf16[3,16,32,256]{3,2,1,0:T(8,128)(2,1)S(1)}, bf16[3,16,32,256]{3,2,1,0:T(8,128)(2,1)S(1)}, u32[]{:S(2)}, u32[]{:S(2)}) collective-permute-start(bf16[3,16,32,256]{3,2,1,0:T(8,128)(2,1)S(1)} %slice.134), channel_id=1, source_target_pairs={{0,4},{4,8},{8,12},{12,0},{1,5},{5,9},{9,13},{13,1},{2,6},{6,10},{... | collective-permute-start | bytes 2359304 | tf_op jit(solution)/shard_map/ppermute | solution.py:103
  84.2 24.2 %collective-permute-start.22 = (bf16[3,16,32,256]{3,2,1,0:T(8,128)(2,1)S(1)}, bf16[3,16,32,256]{3,2,1,0:T(8,128)(2,1)S(1)}, u32[]{:S(2)}, u32[]{:S(2)}) collective-permute-start(bf16[3,16,32,256]{3,2,1,0:T(8,128)(2,1)S(1)} %slice.137), channel_id=1, source_target_pairs={{0,12},{4,0},{8,4},{12,8},{1,13},{5,1},{9,5},{13,9},{2,14},{6,2},{... | collective-permute-start | bytes 2359304 | tf_op jit(solution)/shard_map/ppermute | solution.py:104
  86.8 17.4 %collective-permute-start.8 = (bf16[3,8,64,256]{3,2,1,0:T(8,128)(2,1)S(1)}, bf16[3,8,64,256]{3,2,1,0:T(8,128)(2,1)S(1)}, u32[]{:S(2)}, u32[]{:S(2)}) collective-permute-start(bf16[3,8,64,256]{3,2,1,0:T(8,128)(2,1)S(1)} %collective-permute-done.6), channel_id=1, source_target_pairs={{0,32},{32,64},{64,96},{96,128},{128,160},{160,192},{192,224},{224... | collective-permute-start | bytes 2359304 | tf_op jit(solution)/shard_map/ppermute | solution.py:99
  87.8 16.7 %collective-permute-start.9 = (bf16[3,8,64,256]{3,2,1,0:T(8,128)(2,1)S(1)}, bf16[3,8,64,256]{3,2,1,0:T(8,128)(2,1)S(1)}, u32[]{:S(2)}, u32[]{:S(2)}) collective-permute-start(bf16[3,8,64,256]{3,2,1,0:T(8,128)(2,1)S(1)} %collective-permute-done.7), channel_id=1, source_target_pairs={{0,224},{32,0},{64,32},{96,64},{128,96},{160,128},{192,160},{224,1... | collective-permute-start | bytes 2359304 | tf_op jit(solution)/shard_map/ppermute | solution.py:100
  104.2 9.0 %collective-permute-start.10 = (bf16[3,8,32,256]{3,2,1,0:T(8,128)(2,1)S(1)}, bf16[3,8,32,256]{3,2,1,0:T(8,128)(2,1)S(1)}, u32[]{:S(2)}, u32[]{:S(2)}) collective-permute-start(bf16[3,8,32,256]{3,2,1,0:T(8,128)(2,1)S(1)} %slice.125), channel_id=1, source_target_pairs={{0,32},{32,64},{64,96},{96,128},{128,160},{160,192},{192,224},{224... | collective-permute-start | bytes 1179656 | tf_op jit(solution)/shard_map/ppermute | solution.py:103
  104.6 9.0 %collective-permute-start.11 = (bf16[3,8,32,256]{3,2,1,0:T(8,128)(2,1)S(1)}, bf16[3,8,32,256]{3,2,1,0:T(8,128)(2,1)S(1)}, u32[]{:S(2)}, u32[]{:S(2)}) collective-permute-start(bf16[3,8,32,256]{3,2,1,0:T(8,128)(2,1)S(1)} %slice.128), channel_id=1, source_target_pairs={{0,224},{32,0},{64,32},{96,64},{128,96},{160,128},{192,160},{224,1... | collective-permute-start | bytes 1179656 | tf_op jit(solution)/shard_map/ppermute | solution.py:104
  115.4 6.4 %collective-permute-start.23 = (f32[4,128,128]{2,1,0:T(8,128)S(1)}, f32[4,128,128]{2,1,0:T(8,128)S(1)}, u32[]{:S(2)}, u32[]{:S(2)}) collective-permute-start(f32[4,128,128]{2,1,0:T(8,128)S(1)} %fusion.55), channel_id=1, source_target_pairs={{0,4},{4,8},{8,12},{12,0},{1,5},{5,9},{9,13},{13,1},{2,6},{6,10},{... | collective-permute-start | bytes 786440 | tf_op jit(solution)/shard_map/ppermute | solution.py:49
  116.4 8.0 %collective-permute-start.24 = (f32[4,128,128]{2,1,0:T(8,128)S(1)}, f32[4,128,128]{2,1,0:T(8,128)S(1)}, u32[]{:S(2)}, u32[]{:S(2)}) collective-permute-start(f32[4,128,128]{2,1,0:T(8,128)S(1)} %fusion.55), channel_id=1, source_target_pairs={{0,8},{4,12},{8,0},{12,4},{1,9},{5,13},{9,1},{13,5},{2,10},{6,14},... | collective-permute-start | bytes 786440 | tf_op jit(solution)/shard_map/ppermute | solution.py:49
  118.5 8.6 %collective-permute-start.25 = (f32[4,128,128]{2,1,0:T(8,128)S(1)}, f32[4,128,128]{2,1,0:T(8,128)S(1)}, u32[]{:S(2)}, u32[]{:S(2)}) collective-permute-start(f32[4,128,128]{2,1,0:T(8,128)S(1)} %fusion.55), channel_id=1, source_target_pairs={{0,12},{4,0},{8,4},{12,8},{1,13},{5,1},{9,5},{13,9},{2,14},{6,2},{... | collective-permute-start | bytes 786440 | tf_op jit(solution)/shard_map/ppermute | solution.py:49
  127.2 8.0 %collective-permute-start.26 = (f32[4,128,128]{2,1,0:T(8,128)S(1)}, f32[4,128,128]{2,1,0:T(8,128)S(1)}, u32[]{:S(2)}, u32[]{:S(2)}) collective-permute-start(f32[4,128,128]{2,1,0:T(8,128)S(1)} %add_add_fusion.1), channel_id=1, source_target_pairs={{0,16},{16,0},{1,17},{17,1},{2,18},{18,2},{3,19},{19,3},{4,20},{20... | collective-permute-start | bytes 786440 | tf_op jit(solution)/shard_map/ppermute | solution.py:49
  135.1 1.1 copy-start.1
  135.2 7.7 %collective-permute-start.27 = (f32[4,128,128]{2,1,0:T(8,128)S(1)}, f32[4,128,128]{2,1,0:T(8,128)S(1)}, u32[]{:S(2)}, u32[]{:S(2)}) collective-permute-start(f32[4,128,128]{2,1,0:T(8,128)S(1)} %add.186), channel_id=1, source_target_pairs={{0,32},{32,64},{64,96},{96,0},{128,160},{160,192},{192,224},{224,1... | collective-permute-start | bytes 786440 | tf_op jit(solution)/shard_map/ppermute | solution.py:49
  136.3 19.6 %collective-permute-start.28 = (f32[4,128,128]{2,1,0:T(8,128)S(1)}, f32[4,128,128]{2,1,0:T(8,128)S(1)}, u32[]{:S(2)}, u32[]{:S(2)}) collective-permute-start(f32[4,128,128]{2,1,0:T(8,128)S(1)} %add.186), channel_id=1, source_target_pairs={{0,64},{32,96},{64,0},{96,32},{128,192},{160,224},{192,128},{224,1... | collective-permute-start | bytes 786440 | tf_op jit(solution)/shard_map/ppermute | solution.py:49
  140.8 18.2 %collective-permute-start.29 = (f32[4,128,128]{2,1,0:T(8,128)S(1)}, f32[4,128,128]{2,1,0:T(8,128)S(1)}, u32[]{:S(2)}, u32[]{:S(2)}) collective-permute-start(f32[4,128,128]{2,1,0:T(8,128)S(1)} %add.186), channel_id=1, source_target_pairs={{0,96},{32,0},{64,32},{96,64},{128,224},{160,128},{192,160},{224,1... | collective-permute-start | bytes 786440 | tf_op jit(solution)/shard_map/ppermute | solution.py:49
  142.8 19.7 %copy-start.2 = (f32[4,128,128]{2,1,0:T(8,128)}, f32[4,128,128]{2,1,0:T(8,128)S(1)}, u32[]{:S(2)}) copy-start(f32[4,128,128]{2,1,0:T(8,128)S(1)} %collective-permute-done.27) | copy-start | bytes 786436
  155.9 6.6 %copy-start.3 = (f32[4,128,128]{2,1,0:T(8,128)}, f32[4,128,128]{2,1,0:T(8,128)S(1)}, u32[]{:S(2)}) copy-start(f32[4,128,128]{2,1,0:T(8,128)S(1)} %collective-permute-done.28) | copy-start | bytes 786436
  159.0 3.5 %copy-start.4 = (f32[4,128,128]{2,1,0:T(8,128)}, f32[4,128,128]{2,1,0:T(8,128)S(1)}, u32[]{:S(2)}) copy-start(f32[4,128,128]{2,1,0:T(8,128)S(1)} %collective-permute-done.29) | copy-start | bytes 786436
  159.8 13.2 %collective-permute-start.30 = (f32[4,128,128]{2,1,0:T(8,128)}, f32[4,128,128]{2,1,0:T(8,128)}, u32[]{:S(2)}, u32[]{:S(2)}) collective-permute-start(f32[4,128,128]{2,1,0:T(8,128)} %add_add_fusion), channel_id=1, source_target_pairs={{0,128},{32,160},{64,192},{96,224},{128,0},{160,32},{192,64},{224,... | collective-permute-start | bytes 786440 | tf_op jit(solution)/shard_map/ppermute | solution.py:69

commit v6 on v5

--- a/solution.py
+++ b/solution.py
@@ -64,11 +64,16 @@
 def prefix_over_ctx(state):
     before_y, total_y = exclusive_and_total(state, "y")
     before_x, total_xy = exclusive_and_total(total_y, "xh")
-    half = SIZES["z"] // 2
-    before_zl, total_zl = exclusive_and_total(total_xy, "z", half)
-    other = lax.ppermute(total_zl, "z", [(j, (j + half) % SIZES["z"]) for j in range(SIZES["z"])])
-    before_zh = jnp.where(lax.axis_index("z") >= half, other, 0.0)
-    return before_zh + before_zl + before_x + before_y
+    zi = lax.axis_index("z")
+    before_z = jnp.zeros_like(state)
+    total = total_xy
+    bit = 1
+    while bit < SIZES["z"]:
+        other = lax.ppermute(total, "z", [(j, j ^ bit) for j in range(SIZES["z"])])
+        before_z = before_z + jnp.where((zi & bit) != 0, other, 0.0)
+        total = total + other
+        bit *= 2
+    return before_z + before_x + before_y
 
 
 def project(tokens, ws, split):

time: 179 us -> 179 us (level)
  the two profiles are of different devices: /device:TPU:62 before, /device:TPU:6 now
where the time goes in v6:
time: 179 us
  waiting for transfers between devices  91.7 us (51%)
  starting transfers between devices  49.3 us (28%)
  matrix products  13.9 us (8%)
  local copies, waits for them, and re-layouts  13.1 us (7%)
  other arithmetic  10.1 us (6%)
    ppermute x4, waiting for transfers between devices, last_stage(): r = lax.ppermute(r, name, right)  30.4 us
    ppermute x3, waiting for transfers between devices, prefix_over_ctx(): other = lax.ppermute(total, 'z', [(j, j ^ bit) for j in range(SIZES['z'])])  28.3 us
    ppermute x4, starting transfers between devices, ring_values(): l = lax.ppermute(l, name, left)  16.3 us
    ppermute x6, waiting for transfers between devices, ring_values(): r = lax.ppermute(r, name, right)  16.1 us
    ppermute x4, waiting for transfers between devices, direct_values(): got.append((k, lax.ppermute(x, name, pairs)))  11.6 us
    ppermute x4, starting transfers between devices, last_stage(): l = lax.ppermute(l, name, left)  11.5 us
    dot_general x14, matrix products, last_stage(): jnp.einsum('tjk,wjkn->wtn', toks[m][:, :, lo:hi], v, preferred_element_ty...  9.6 us
    unnamed x28, local copies, waits for them, and re-layouts  9.28 us
  transfers between devices with their start and end apart: 30, of which 17 were waited for; matrix products, arithmetic and copies ran while one was open for 15% of the time, Pallas kernels for 0%

profile of v6, /device:TPU:6, one launch (start us, length us, event | category | flops | bytes accessed | tf_op | source)
XLA Modules:
  0.0 178.5 jit_solution(15128773004910280701)
XLA Ops:
  0.0 1.6 pad_maximum_fusion.1
  1.6 1.4 collective-permute-start
  3.0 6.5 %copy.14 = bf16[512,4096]{0,1:T(8,128)(2,1)} copy(bf16[512,4096]{1,0:T(8,128)(2,1)} %param.4) | data formatting | bytes 8388608 | tf_op args[0]
  9.5 3.1 %fusion = bf16[4,512,8,2,64]{1,4,0,3,2:T(8,128)(2,1)S(1)} fusion(s32[]{:T(128)S(6)} %select_n.119, bf16[4,512,8,2,64]{1,4,0,3,2:T(8,128)(2,1)} %bitcast.227), kind=kLoop, calls=%fused_computation.4 | loop fusion | flops 2097152 | bytes 8388612 | tf_op jit(solution)/shard_map/jit(_roll_dynamic)/concatenate | solution.py:90
  12.6 1.4 fusion.40
  14.0 3.1 %fusion.1 = bf16[8,512,4,2,64]{1,4,2,3,0:T(8,128)(2,1)S(1)} fusion(s32[]{:T(128)S(6)} %select_n.115, bf16[8,512,4,2,64]{1,4,2,3,0:T(8,128)(2,1)} %bitcast.228), kind=kLoop, calls=%fused_computation.5 | loop fusion | flops 2097152 | bytes 8388612 | tf_op jit(solution)/shard_map/jit(_roll_dynamic)/concatenate | solution.py:89
  17.5 5.9 %collective-permute-start.12 = (bf16[3,2,64,256]{3,2,0,1:T(8,128)(2,1)S(1)}, bf16[3,2,64,256]{3,2,0,1:T(8,128)(2,1)S(1)}, u32[]{:S(2)}, u32[]{:S(2)}) collective-permute-start(bf16[3,2,64,256]{3,2,0,1:T(8,128)(2,1)S(1)} %get-tuple-element.22), channel_id=1, source_target_pairs={{0,224},{32,0},{64,32},{96,64},{128,96},{160,128},{192,160},{224,1... | collective-permute-start | bytes 589832 | tf_op jit(solution)/shard_map/ppermute | solution.py:30
  23.4 3.0 %collective-permute-start.1 = (bf16[3,2,64,256]{3,2,0,1:T(8,128)(2,1)S(1)}, bf16[3,2,64,256]{3,2,0,1:T(8,128)(2,1)S(1)}, u32[]{:S(2)}, u32[]{:S(2)}) collective-permute-start(bf16[3,2,64,256]{3,2,0,1:T(8,128)(2,1)S(1)} %get-tuple-element.23), channel_id=1, source_target_pairs={{0,12},{4,0},{8,4},{12,8},{1,13},{5,1},{9,5},{13,9},{2,14},{6,2},{... | collective-permute-start | bytes 589832 | tf_op jit(solution)/shard_map/ppermute | solution.py:30
  26.4 0.8 collective-permute-done.12
  27.3 3.7 %collective-permute-start.13 = (bf16[3,2,64,256]{3,2,0,1:T(8,128)(2,1)S(1)}, bf16[3,2,64,256]{3,2,0,1:T(8,128)(2,1)S(1)}, u32[]{:S(2)}, u32[]{:S(2)}) collective-permute-start(bf16[3,2,64,256]{3,2,0,1:T(8,128)(2,1)S(1)} %collective-permute-done.12), channel_id=1, source_target_pairs={{0,224},{32,0},{64,32},{96,64},{128,96},{160,128},{192,160},{224,1... | collective-permute-start | bytes 589832 | tf_op jit(solution)/shard_map/ppermute | solution.py:30
  31.0 2.4 %collective-permute-done.2 = bf16[3,2,64,256]{3,2,0,1:T(8,128)(2,1)S(1)} collective-permute-done((bf16[3,2,64,256]{3,2,0,1:T(8,128)(2,1)S(1)}, bf16[3,2,64,256]{3,2,0,1:T(8,128)(2,1)S(1)}, u32[]{:S(2)}, u32[]{:S(2)}) %collective-permute-start.2) | collective-permute-done | bytes 196640 | tf_op jit(solution)/shard_map/ppermute | solution.py:27
  33.5 0.7 collective-permute-done.13
  34.1 3.7 %collective-permute-start.14 = (bf16[3,2,64,256]{3,2,0,1:T(8,128)(2,1)S(1)}, bf16[3,2,64,256]{3,2,0,1:T(8,128)(2,1)S(1)}, u32[]{:S(2)}, u32[]{:S(2)}) collective-permute-start(bf16[3,2,64,256]{3,2,0,1:T(8,128)(2,1)S(1)} %collective-permute-done.13), channel_id=1, source_target_pairs={{0,224},{32,0},{64,32},{96,64},{128,96},{160,128},{192,160},{224,1... | collective-permute-start | bytes 589832 | tf_op jit(solution)/shard_map/ppermute | solution.py:30
  37.9 2.4 %collective-permute-done.3 = bf16[3,2,64,256]{3,2,0,1:T(8,128)(2,1)S(1)} collective-permute-done((bf16[3,2,64,256]{3,2,0,1:T(8,128)(2,1)S(1)}, bf16[3,2,64,256]{3,2,0,1:T(8,128)(2,1)S(1)}, u32[]{:S(2)}, u32[]{:S(2)}) %collective-permute-start.3) | collective-permute-done | bytes 196640 | tf_op jit(solution)/shard_map/ppermute | solution.py:27
  40.3 4.4 %collective-permute-done.17 = bf16[3,2,64,256]{3,2,0,1:T(8,128)(2,1)S(1)} collective-permute-done((bf16[3,2,64,256]{3,2,0,1:T(8,128)(2,1)S(1)}, bf16[3,2,64,256]{3,2,0,1:T(8,128)(2,1)S(1)}, u32[]{:S(2)}, u32[]{:S(2)}) %collective-permute-start.17) | collective-permute-done | bytes 196640 | tf_op jit(solution)/shard_map/ppermute | solution.py:27
  44.7 6.9 %collective-permute-done.18 = bf16[3,2,64,256]{3,2,0,1:T(8,128)(2,1)S(1)} collective-permute-done((bf16[3,2,64,256]{3,2,0,1:T(8,128)(2,1)S(1)}, bf16[3,2,64,256]{3,2,0,1:T(8,128)(2,1)S(1)}, u32[]{:S(2)}, u32[]{:S(2)}) %collective-permute-start.18) | collective-permute-done | bytes 196640 | tf_op jit(solution)/shard_map/ppermute | solution.py:27
  52.2 1.8 %collective-permute-start.19 = (bf16[3,16,64,256]{3,2,1,0:T(8,128)(2,1)S(1)}, bf16[3,16,64,256]{3,2,1,0:T(8,128)(2,1)S(1)}, u32[]{:S(2)}, u32[]{:S(2)}) collective-permute-start(bf16[3,16,64,256]{3,2,1,0:T(8,128)(2,1)S(1)} %bitcast.237), channel_id=1, source_target_pairs={{0,4},{4,8},{8,12},{12,0},{1,5},{5,9},{9,13},{13,1},{2,6},{6,10},{... | collective-permute-start | bytes 4718600 | tf_op jit(solution)/shard_map/ppermute | solution.py:104
  54.0 1.7 collective-permute-start.20
  56.0 3.2 %collective-permute-start.5 = (bf16[3,8,64,256]{3,2,1,0:T(8,128)(2,1)S(1)}, bf16[3,8,64,256]{3,2,1,0:T(8,128)(2,1)S(1)}, u32[]{:S(2)}, u32[]{:S(2)}) collective-permute-start(bf16[3,8,64,256]{3,2,1,0:T(8,128)(2,1)S(1)} %bitcast.246), channel_id=1, source_target_pairs={{0,224},{32,0},{64,32},{96,64},{128,96},{160,128},{192,160},{224,1... | collective-permute-start | bytes 2359304 | tf_op jit(solution)/shard_map/ppermute | solution.py:105
  59.2 0.5 fusion.41
  60.1 1.1 copy-done.3
  61.1 1.0 fusion.49
  62.1 11.5 %collective-permute-done.4 = bf16[3,8,64,256]{3,2,1,0:T(8,128)(2,1)S(1)} collective-permute-done((bf16[3,8,64,256]{3,2,1,0:T(8,128)(2,1)S(1)}, bf16[3,8,64,256]{3,2,1,0:T(8,128)(2,1)S(1)}, u32[]{:S(2)}, u32[]{:S(2)}) %collective-permute-start.4) | collective-permute-done | bytes 786464 | tf_op jit(solution)/shard_map/ppermute | solution.py:104
  73.7 0.6 fusion.43
  74.3 3.3 %collective-permute-start.7 = (bf16[3,8,64,256]{3,2,1,0:T(8,128)(2,1)S(1)}, bf16[3,8,64,256]{3,2,1,0:T(8,128)(2,1)S(1)}, u32[]{:S(2)}, u32[]{:S(2)}) collective-permute-start(bf16[3,8,64,256]{3,2,1,0:T(8,128)(2,1)S(1)} %collective-permute-done.5), channel_id=1, source_target_pairs={{0,224},{32,0},{64,32},{96,64},{128,96},{160,128},{192,160},{224,1... | collective-permute-start | bytes 2359304 | tf_op jit(solution)/shard_map/ppermute | solution.py:105
  77.6 0.6 fusion.44
  78.2 0.6 fusion.45
  78.8 8.1 %collective-permute-done.19 = bf16[3,16,64,256]{3,2,1,0:T(8,128)(2,1)S(1)} collective-permute-done((bf16[3,16,64,256]{3,2,1,0:T(8,128)(2,1)S(1)}, bf16[3,16,64,256]{3,2,1,0:T(8,128)(2,1)S(1)}, u32[]{:S(2)}, u32[]{:S(2)}) %collective-permute-start.19) | collective-permute-done | bytes 1572896 | tf_op jit(solution)/shard_map/ppermute | solution.py:104
  86.9 1.1 collective-permute-start.21
  88.1 2.2 %collective-permute-start.22 = (bf16[3,16,32,256]{3,2,1,0:T(8,128)(2,1)S(1)}, bf16[3,16,32,256]{3,2,1,0:T(8,128)(2,1)S(1)}, u32[]{:S(2)}, u32[]{:S(2)}) collective-permute-start(bf16[3,16,32,256]{3,2,1,0:T(8,128)(2,1)S(1)} %slice.137), channel_id=1, source_target_pairs={{0,12},{4,0},{8,4},{12,8},{1,13},{5,1},{9,5},{13,9},{2,14},{6,2},{... | collective-permute-start | bytes 2359304 | tf_op jit(solution)/shard_map/ppermute | solution.py:109
  90.4 1.0 fusion.50
  91.4 3.3 %collective-permute-start.9 = (bf16[3,8,64,256]{3,2,1,0:T(8,128)(2,1)S(1)}, bf16[3,8,64,256]{3,2,1,0:T(8,128)(2,1)S(1)}, u32[]{:S(2)}, u32[]{:S(2)}) collective-permute-start(bf16[3,8,64,256]{3,2,1,0:T(8,128)(2,1)S(1)} %collective-permute-done.7), channel_id=1, source_target_pairs={{0,224},{32,0},{64,32},{96,64},{128,96},{160,128},{192,160},{224,1... | collective-permute-start | bytes 2359304 | tf_op jit(solution)/shard_map/ppermute | solution.py:105
  94.7 1.0 fusion.51
  95.7 0.6 fusion.46
  96.3 0.6 fusion.47
  96.9 10.8 %collective-permute-done.8 = bf16[3,8,64,256]{3,2,1,0:T(8,128)(2,1)S(1)} collective-permute-done((bf16[3,8,64,256]{3,2,1,0:T(8,128)(2,1)S(1)}, bf16[3,8,64,256]{3,2,1,0:T(8,128)(2,1)S(1)}, u32[]{:S(2)}, u32[]{:S(2)}) %collective-permute-start.8) | collective-permute-done | bytes 786464 | tf_op jit(solution)/shard_map/ppermute | solution.py:104
  107.8 0.3 collective-permute-start.10
  108.2 3.3 %collective-permute-start.11 = (bf16[3,8,32,256]{3,2,1,0:T(8,128)(2,1)S(1)}, bf16[3,8,32,256]{3,2,1,0:T(8,128)(2,1)S(1)}, u32[]{:S(2)}, u32[]{:S(2)}) collective-permute-start(bf16[3,8,32,256]{3,2,1,0:T(8,128)(2,1)S(1)} %slice.128), channel_id=1, source_target_pairs={{0,224},{32,0},{64,32},{96,64},{128,96},{160,128},{192,160},{224,1... | collective-permute-start | bytes 1179656 | tf_op jit(solution)/shard_map/ppermute | solution.py:109
  111.5 0.6 fusion.10
  112.1 0.7 fusion.7
  112.8 0.6 fusion.48
  113.4 3.7 %collective-permute-done.10 = bf16[3,8,32,256]{3,2,1,0:T(8,128)(2,1)S(1)} collective-permute-done((bf16[3,8,32,256]{3,2,1,0:T(8,128)(2,1)S(1)}, bf16[3,8,32,256]{3,2,1,0:T(8,128)(2,1)S(1)}, u32[]{:S(2)}, u32[]{:S(2)}) %collective-permute-start.10) | collective-permute-done | bytes 393248 | tf_op jit(solution)/shard_map/ppermute | solution.py:108
  117.1 0.4 fusion.15
  117.5 0.4 fusion.14
  117.9 0.9 fusion.6
  119.2 0.6 collective-permute-start.23
  119.9 3.2 %collective-permute-start.24 = (f32[4,128,128]{2,1,0:T(8,128)S(1)}, f32[4,128,128]{2,1,0:T(8,128)S(1)}, u32[]{:S(2)}, u32[]{:S(2)}) collective-permute-start(f32[4,128,128]{2,1,0:T(8,128)S(1)} %fusion.52), channel_id=1, source_target_pairs={{0,8},{4,12},{8,0},{12,4},{1,9},{5,13},{9,1},{13,5},{2,10},{6,14},... | collective-permute-start | bytes 786440 | tf_op jit(solution)/shard_map/ppermute | solution.py:49
  123.0 1.7 collective-permute-start.25
  124.7 2.2 %collective-permute-done.23 = f32[4,128,128]{2,1,0:T(8,128)S(1)} collective-permute-done((f32[4,128,128]{2,1,0:T(8,128)S(1)}, f32[4,128,128]{2,1,0:T(8,128)S(1)}, u32[]{:S(2)}, u32[]{:S(2)}) %collective-permute-start.23) | collective-permute-done | bytes 262176 | tf_op jit(solution)/shard_map/ppermute | solution.py:49
  126.9 3.3 %collective-permute-done.24 = f32[4,128,128]{2,1,0:T(8,128)S(1)} collective-permute-done((f32[4,128,128]{2,1,0:T(8,128)S(1)}, f32[4,128,128]{2,1,0:T(8,128)S(1)}, u32[]{:S(2)}, u32[]{:S(2)}) %collective-permute-start.24) | collective-permute-done | bytes 262176 | tf_op jit(solution)/shard_map/ppermute | solution.py:49
  130.2 0.4 collective-permute-done.25
  130.6 2.2 %collective-permute-start.26 = (f32[4,128,128]{2,1,0:T(8,128)S(1)}, f32[4,128,128]{2,1,0:T(8,128)S(1)}, u32[]{:S(2)}, u32[]{:S(2)}) collective-permute-start(f32[4,128,128]{2,1,0:T(8,128)S(1)} %add_add_fusion), channel_id=1, source_target_pairs={{0,16},{16,0},{1,17},{17,1},{2,18},{18,2},{3,19},{19,3},{4,20},{20... | collective-permute-start | bytes 786440 | tf_op jit(solution)/shard_map/ppermute | solution.py:49
  132.8 5.7 %collective-permute-done.26 = f32[4,128,128]{2,1,0:T(8,128)S(1)} collective-permute-done((f32[4,128,128]{2,1,0:T(8,128)S(1)}, f32[4,128,128]{2,1,0:T(8,128)S(1)}, u32[]{:S(2)}, u32[]{:S(2)}) %collective-permute-start.26) | collective-permute-done | bytes 262176 | tf_op jit(solution)/shard_map/ppermute | solution.py:49
  138.6 0.7 copy-done
  139.4 7.7 %collective-permute-done.27 = f32[4,128,128]{2,1,0:T(8,128)S(1)} collective-permute-done((f32[4,128,128]{2,1,0:T(8,128)S(1)}, f32[4,128,128]{2,1,0:T(8,128)S(1)}, u32[]{:S(2)}, u32[]{:S(2)}) %collective-permute-start.27) | collective-permute-done | bytes 262176 | tf_op jit(solution)/shard_map/ppermute | solution.py:72
  147.1 0.7 copy-done.1
  148.0 0.8 iota_compare_fusion
  148.8 12.9 %collective-permute-done.28 = f32[4,128,128]{2,1,0:T(8,128)S(1)} collective-permute-done((f32[4,128,128]{2,1,0:T(8,128)S(1)}, f32[4,128,128]{2,1,0:T(8,128)S(1)}, u32[]{:S(2)}, u32[]{:S(2)}) %collective-permute-start.28) | collective-permute-done | bytes 262176 | tf_op jit(solution)/shard_map/ppermute | solution.py:72
  161.8 0.8 add.180
  162.5 3.2 %collective-permute-start.29 = (f32[4,128,128]{2,1,0:T(8,128)}, f32[4,128,128]{2,1,0:T(8,128)}, u32[]{:S(2)}, u32[]{:S(2)}) collective-permute-start(f32[4,128,128]{2,1,0:T(8,128)} %add.180), channel_id=1, source_target_pairs={{0,128},{32,160},{64,192},{96,224},{128,0},{160,32},{192,64},{224,... | collective-permute-start | bytes 786440 | tf_op jit(solution)/shard_map/ppermute | solution.py:72
  165.7 2.3 %fusion.2 = f32[4,128,512]{2,1,0:T(8,128)S(1)} fusion(bf16[512,4,128]{0,2,1:T(8,128)(2,1)S(1)} %bitcast.236, bf16[512,4,128]{0,2,1:T(8,128)(2,1)S(1)} %bitcast.231, bf16[512,4,128]{0,2,1:T(8,128)(2,1)S(1)} %bitcast.234, pred[512,512]{1,0:T(8,128)(4,1)} %iota_compare_fusion), kind=kOutput, calls=%fused_computation.11 | convolution fusion | flops 538968064 | bytes 2883584 | tf_op jit(solution)/shard_map/hqk,khd->qhd/dot_general | solution.py:134
  168.1 7.7 %collective-permute-done.29 = f32[4,128,128]{2,1,0:T(8,128)} collective-permute-done((f32[4,128,128]{2,1,0:T(8,128)}, f32[4,128,128]{2,1,0:T(8,128)}, u32[]{:S(2)}, u32[]{:S(2)}) %collective-permute-start.29) | collective-permute-done | bytes 262176 | tf_op jit(solution)/shard_map/ppermute | solution.py:72
  175.7 1.6 multiply_reduce_fusion
  177.5 1.0 copy.27
  (75 shorter events, 2.6 us)
Async XLA Ops:
  1.6 15.5 %collective-permute-start = (bf16[3,64,512]{2,1,0:T(8,128)(2,1)}, bf16[3,64,512]{2,1,0:T(8,128)(2,1)S(1)}, u32[]{:S(2)}, u32[]{:S(2)}) collective-permute-start(bf16[3,64,512]{2,1,0:T(8,128)(2,1)} %get-tuple-element.26), channel_id=1, source_target_pairs={{0,16},{16,0},{1,17},{17,1},{2,18},{18,2},{3,19},{19,3},{4,20},{20... | collective-permute-start | bytes 589832 | tf_op jit(solution)/shard_map/ppermute | solution.py:81
  17.5 9.8 %collective-permute-start.12 = (bf16[3,2,64,256]{3,2,0,1:T(8,128)(2,1)S(1)}, bf16[3,2,64,256]{3,2,0,1:T(8,128)(2,1)S(1)}, u32[]{:S(2)}, u32[]{:S(2)}) collective-permute-start(bf16[3,2,64,256]{3,2,0,1:T(8,128)(2,1)S(1)} %get-tuple-element.22), channel_id=1, source_target_pairs={{0,224},{32,0},{64,32},{96,64},{128,96},{160,128},{192,160},{224,1... | collective-permute-start | bytes 589832 | tf_op jit(solution)/shard_map/ppermute | solution.py:30
  23.4 7.6 %collective-permute-start.15 = (bf16[3,2,64,256]{3,2,0,1:T(8,128)(2,1)S(1)}, bf16[3,2,64,256]{3,2,0,1:T(8,128)(2,1)S(1)}, u32[]{:S(2)}, u32[]{:S(2)}) collective-permute-start(bf16[3,2,64,256]{3,2,0,1:T(8,128)(2,1)S(1)} %get-tuple-element.22), channel_id=1, source_target_pairs={{0,32},{32,64},{64,96},{96,128},{128,160},{160,192},{192,224},{224... | collective-permute-start | bytes 589832 | tf_op jit(solution)/shard_map/ppermute | solution.py:27
  23.4 10.0 %collective-permute-start.1 = (bf16[3,2,64,256]{3,2,0,1:T(8,128)(2,1)S(1)}, bf16[3,2,64,256]{3,2,0,1:T(8,128)(2,1)S(1)}, u32[]{:S(2)}, u32[]{:S(2)}) collective-permute-start(bf16[3,2,64,256]{3,2,0,1:T(8,128)(2,1)S(1)} %get-tuple-element.23), channel_id=1, source_target_pairs={{0,12},{4,0},{8,4},{12,8},{1,13},{5,1},{9,5},{13,9},{2,14},{6,2},{... | collective-permute-start | bytes 589832 | tf_op jit(solution)/shard_map/ppermute | solution.py:30
  26.4 7.0 %collective-permute-start.2 = (bf16[3,2,64,256]{3,2,0,1:T(8,128)(2,1)S(1)}, bf16[3,2,64,256]{3,2,0,1:T(8,128)(2,1)S(1)}, u32[]{:S(2)}, u32[]{:S(2)}) collective-permute-start(bf16[3,2,64,256]{3,2,0,1:T(8,128)(2,1)S(1)} %get-tuple-element.23), channel_id=1, source_target_pairs={{0,4},{4,8},{8,12},{12,0},{1,5},{5,9},{9,13},{13,1},{2,6},{6,10},{... | collective-permute-start | bytes 589832 | tf_op jit(solution)/shard_map/ppermute | solution.py:27
  27.3 6.9 %collective-permute-start.13 = (bf16[3,2,64,256]{3,2,0,1:T(8,128)(2,1)S(1)}, bf16[3,2,64,256]{3,2,0,1:T(8,128)(2,1)S(1)}, u32[]{:S(2)}, u32[]{:S(2)}) collective-permute-start(bf16[3,2,64,256]{3,2,0,1:T(8,128)(2,1)S(1)} %collective-permute-done.12), channel_id=1, source_target_pairs={{0,224},{32,0},{64,32},{96,64},{128,96},{160,128},{192,160},{224,1... | collective-permute-start | bytes 589832 | tf_op jit(solution)/shard_map/ppermute | solution.py:30
  31.0 6.9 %collective-permute-start.16 = (bf16[3,2,64,256]{3,2,0,1:T(8,128)(2,1)S(1)}, bf16[3,2,64,256]{3,2,0,1:T(8,128)(2,1)S(1)}, u32[]{:S(2)}, u32[]{:S(2)}) collective-permute-start(bf16[3,2,64,256]{3,2,0,1:T(8,128)(2,1)S(1)} %collective-permute-done.15), channel_id=1, source_target_pairs={{0,32},{32,64},{64,96},{96,128},{128,160},{160,192},{192,224},{224... | collective-permute-start | bytes 589832 | tf_op jit(solution)/shard_map/ppermute | solution.py:27
  33.4 6.9 %collective-permute-start.3 = (bf16[3,2,64,256]{3,2,0,1:T(8,128)(2,1)S(1)}, bf16[3,2,64,256]{3,2,0,1:T(8,128)(2,1)S(1)}, u32[]{:S(2)}, u32[]{:S(2)}) collective-permute-start(bf16[3,2,64,256]{3,2,0,1:T(8,128)(2,1)S(1)} %collective-permute-done.2), channel_id=1, source_target_pairs={{0,4},{4,8},{8,12},{12,0},{1,5},{5,9},{9,13},{13,1},{2,6},{6,10},{... | collective-permute-start | bytes 589832 | tf_op jit(solution)/shard_map/ppermute | solution.py:27
  34.1 10.6 %collective-permute-start.14 = (bf16[3,2,64,256]{3,2,0,1:T(8,128)(2,1)S(1)}, bf16[3,2,64,256]{3,2,0,1:T(8,128)(2,1)S(1)}, u32[]{:S(2)}, u32[]{:S(2)}) collective-permute-start(bf16[3,2,64,256]{3,2,0,1:T(8,128)(2,1)S(1)} %collective-permute-done.13), channel_id=1, source_target_pairs={{0,224},{32,0},{64,32},{96,64},{128,96},{160,128},{192,160},{224,1... | collective-permute-start | bytes 589832 | tf_op jit(solution)/shard_map/ppermute | solution.py:30
  37.8 6.9 %collective-permute-start.17 = (bf16[3,2,64,256]{3,2,0,1:T(8,128)(2,1)S(1)}, bf16[3,2,64,256]{3,2,0,1:T(8,128)(2,1)S(1)}, u32[]{:S(2)}, u32[]{:S(2)}) collective-permute-start(bf16[3,2,64,256]{3,2,0,1:T(8,128)(2,1)S(1)} %collective-permute-done.16), channel_id=1, source_target_pairs={{0,32},{32,64},{64,96},{96,128},{128,160},{160,192},{192,224},{224... | collective-permute-start | bytes 589832 | tf_op jit(solution)/shard_map/ppermute | solution.py:27
  44.7 6.9 %collective-permute-start.18 = (bf16[3,2,64,256]{3,2,0,1:T(8,128)(2,1)S(1)}, bf16[3,2,64,256]{3,2,0,1:T(8,128)(2,1)S(1)}, u32[]{:S(2)}, u32[]{:S(2)}) collective-permute-start(bf16[3,2,64,256]{3,2,0,1:T(8,128)(2,1)S(1)} %collective-permute-done.17), channel_id=1, source_target_pairs={{0,32},{32,64},{64,96},{96,128},{128,160},{160,192},{192,224},{224... | collective-permute-start | bytes 589832 | tf_op jit(solution)/shard_map/ppermute | solution.py:27
  52.2 34.7 %collective-permute-start.19 = (bf16[3,16,64,256]{3,2,1,0:T(8,128)(2,1)S(1)}, bf16[3,16,64,256]{3,2,1,0:T(8,128)(2,1)S(1)}, u32[]{:S(2)}, u32[]{:S(2)}) collective-permute-start(bf16[3,16,64,256]{3,2,1,0:T(8,128)(2,1)S(1)} %bitcast.237), channel_id=1, source_target_pairs={{0,4},{4,8},{8,12},{12,0},{1,5},{5,9},{9,13},{13,1},{2,6},{6,10},{... | collective-permute-start | bytes 4718600 | tf_op jit(solution)/shard_map/ppermute | solution.py:104
  54.0 34.1 %collective-permute-start.20 = (bf16[3,16,64,256]{3,2,1,0:T(8,128)(2,1)S(1)}, bf16[3,16,64,256]{3,2,1,0:T(8,128)(2,1)S(1)}, u32[]{:S(2)}, u32[]{:S(2)}) collective-permute-start(bf16[3,16,64,256]{3,2,1,0:T(8,128)(2,1)S(1)} %bitcast.238), channel_id=1, source_target_pairs={{0,12},{4,0},{8,4},{12,8},{1,13},{5,1},{9,5},{13,9},{2,14},{6,2},{... | collective-permute-start | bytes 4718600 | tf_op jit(solution)/shard_map/ppermute | solution.py:105
  55.9 17.8 %collective-permute-start.4 = (bf16[3,8,64,256]{3,2,1,0:T(8,128)(2,1)S(1)}, bf16[3,8,64,256]{3,2,1,0:T(8,128)(2,1)S(1)}, u32[]{:S(2)}, u32[]{:S(2)}) collective-permute-start(bf16[3,8,64,256]{3,2,1,0:T(8,128)(2,1)S(1)} %bitcast.245), channel_id=1, source_target_pairs={{0,32},{32,64},{64,96},{96,128},{128,160},{160,192},{192,224},{224... | collective-permute-start | bytes 2359304 | tf_op jit(solution)/shard_map/ppermute | solution.py:104
  56.0 18.3 %collective-permute-start.5 = (bf16[3,8,64,256]{3,2,1,0:T(8,128)(2,1)S(1)}, bf16[3,8,64,256]{3,2,1,0:T(8,128)(2,1)S(1)}, u32[]{:S(2)}, u32[]{:S(2)}) collective-permute-start(bf16[3,8,64,256]{3,2,1,0:T(8,128)(2,1)S(1)} %bitcast.246), channel_id=1, source_target_pairs={{0,224},{32,0},{64,32},{96,64},{128,96},{160,128},{192,160},{224,1... | collective-permute-start | bytes 2359304 | tf_op jit(solution)/shard_map/ppermute | solution.py:105
  59.9 1.2 copy-start.3
  73.7 16.7 %collective-permute-start.6 = (bf16[3,8,64,256]{3,2,1,0:T(8,128)(2,1)S(1)}, bf16[3,8,64,256]{3,2,1,0:T(8,128)(2,1)S(1)}, u32[]{:S(2)}, u32[]{:S(2)}) collective-permute-start(bf16[3,8,64,256]{3,2,1,0:T(8,128)(2,1)S(1)} %collective-permute-done.4), channel_id=1, source_target_pairs={{0,32},{32,64},{64,96},{96,128},{128,160},{160,192},{192,224},{224... | collective-permute-start | bytes 2359304 | tf_op jit(solution)/shard_map/ppermute | solution.py:104
  74.3 17.1 %collective-permute-start.7 = (bf16[3,8,64,256]{3,2,1,0:T(8,128)(2,1)S(1)}, bf16[3,8,64,256]{3,2,1,0:T(8,128)(2,1)S(1)}, u32[]{:S(2)}, u32[]{:S(2)}) collective-permute-start(bf16[3,8,64,256]{3,2,1,0:T(8,128)(2,1)S(1)} %collective-permute-done.5), channel_id=1, source_target_pairs={{0,224},{32,0},{64,32},{96,64},{128,96},{160,128},{192,160},{224,1... | collective-permute-start | bytes 2359304 | tf_op jit(solution)/shard_map/ppermute | solution.py:105
  86.9 24.5 %collective-permute-start.21 = (bf16[3,16,32,256]{3,2,1,0:T(8,128)(2,1)S(1)}, bf16[3,16,32,256]{3,2,1,0:T(8,128)(2,1)S(1)}, u32[]{:S(2)}, u32[]{:S(2)}) collective-permute-start(bf16[3,16,32,256]{3,2,1,0:T(8,128)(2,1)S(1)} %slice.134), channel_id=1, source_target_pairs={{0,4},{4,8},{8,12},{12,0},{1,5},{5,9},{9,13},{13,1},{2,6},{6,10},{... | collective-permute-start | bytes 2359304 | tf_op jit(solution)/shard_map/ppermute | solution.py:108
  88.1 23.9 %collective-permute-start.22 = (bf16[3,16,32,256]{3,2,1,0:T(8,128)(2,1)S(1)}, bf16[3,16,32,256]{3,2,1,0:T(8,128)(2,1)S(1)}, u32[]{:S(2)}, u32[]{:S(2)}) collective-permute-start(bf16[3,16,32,256]{3,2,1,0:T(8,128)(2,1)S(1)} %slice.137), channel_id=1, source_target_pairs={{0,12},{4,0},{8,4},{12,8},{1,13},{5,1},{9,5},{13,9},{2,14},{6,2},{... | collective-permute-start | bytes 2359304 | tf_op jit(solution)/shard_map/ppermute | solution.py:109
  90.4 17.4 %collective-permute-start.8 = (bf16[3,8,64,256]{3,2,1,0:T(8,128)(2,1)S(1)}, bf16[3,8,64,256]{3,2,1,0:T(8,128)(2,1)S(1)}, u32[]{:S(2)}, u32[]{:S(2)}) collective-permute-start(bf16[3,8,64,256]{3,2,1,0:T(8,128)(2,1)S(1)} %collective-permute-done.6), channel_id=1, source_target_pairs={{0,32},{32,64},{64,96},{96,128},{128,160},{160,192},{192,224},{224... | collective-permute-start | bytes 2359304 | tf_op jit(solution)/shard_map/ppermute | solution.py:104
  91.4 16.7 %collective-permute-start.9 = (bf16[3,8,64,256]{3,2,1,0:T(8,128)(2,1)S(1)}, bf16[3,8,64,256]{3,2,1,0:T(8,128)(2,1)S(1)}, u32[]{:S(2)}, u32[]{:S(2)}) collective-permute-start(bf16[3,8,64,256]{3,2,1,0:T(8,128)(2,1)S(1)} %collective-permute-done.7), channel_id=1, source_target_pairs={{0,224},{32,0},{64,32},{96,64},{128,96},{160,128},{192,160},{224,1... | collective-permute-start | bytes 2359304 | tf_op jit(solution)/shard_map/ppermute | solution.py:105
  107.8 9.3 %collective-permute-start.10 = (bf16[3,8,32,256]{3,2,1,0:T(8,128)(2,1)S(1)}, bf16[3,8,32,256]{3,2,1,0:T(8,128)(2,1)S(1)}, u32[]{:S(2)}, u32[]{:S(2)}) collective-permute-start(bf16[3,8,32,256]{3,2,1,0:T(8,128)(2,1)S(1)} %slice.125), channel_id=1, source_target_pairs={{0,32},{32,64},{64,96},{96,128},{128,160},{160,192},{192,224},{224... | collective-permute-start | bytes 1179656 | tf_op jit(solution)/shard_map/ppermute | solution.py:108
  108.2 9.3 %collective-permute-start.11 = (bf16[3,8,32,256]{3,2,1,0:T(8,128)(2,1)S(1)}, bf16[3,8,32,256]{3,2,1,0:T(8,128)(2,1)S(1)}, u32[]{:S(2)}, u32[]{:S(2)}) collective-permute-start(bf16[3,8,32,256]{3,2,1,0:T(8,128)(2,1)S(1)} %slice.128), channel_id=1, source_target_pairs={{0,224},{32,0},{64,32},{96,64},{128,96},{160,128},{192,160},{224,1... | collective-permute-start | bytes 1179656 | tf_op jit(solution)/shard_map/ppermute | solution.py:109
  119.2 7.7 %collective-permute-start.23 = (f32[4,128,128]{2,1,0:T(8,128)S(1)}, f32[4,128,128]{2,1,0:T(8,128)S(1)}, u32[]{:S(2)}, u32[]{:S(2)}) collective-permute-start(f32[4,128,128]{2,1,0:T(8,128)S(1)} %fusion.52), channel_id=1, source_target_pairs={{0,4},{4,8},{8,12},{12,0},{1,5},{5,9},{9,13},{13,1},{2,6},{6,10},{... | collective-permute-start | bytes 786440 | tf_op jit(solution)/shard_map/ppermute | solution.py:49
  119.9 10.3 %collective-permute-start.24 = (f32[4,128,128]{2,1,0:T(8,128)S(1)}, f32[4,128,128]{2,1,0:T(8,128)S(1)}, u32[]{:S(2)}, u32[]{:S(2)}) collective-permute-start(f32[4,128,128]{2,1,0:T(8,128)S(1)} %fusion.52), channel_id=1, source_target_pairs={{0,8},{4,12},{8,0},{12,4},{1,9},{5,13},{9,1},{13,5},{2,10},{6,14},... | collective-permute-start | bytes 786440 | tf_op jit(solution)/shard_map/ppermute | solution.py:49
  123.0 7.5 %collective-permute-start.25 = (f32[4,128,128]{2,1,0:T(8,128)S(1)}, f32[4,128,128]{2,1,0:T(8,128)S(1)}, u32[]{:S(2)}, u32[]{:S(2)}) collective-permute-start(f32[4,128,128]{2,1,0:T(8,128)S(1)} %fusion.52), channel_id=1, source_target_pairs={{0,12},{4,0},{8,4},{12,8},{1,13},{5,1},{9,5},{13,9},{2,14},{6,2},{... | collective-permute-start | bytes 786440 | tf_op jit(solution)/shard_map/ppermute | solution.py:49
  130.6 8.0 %collective-permute-start.26 = (f32[4,128,128]{2,1,0:T(8,128)S(1)}, f32[4,128,128]{2,1,0:T(8,128)S(1)}, u32[]{:S(2)}, u32[]{:S(2)}) collective-permute-start(f32[4,128,128]{2,1,0:T(8,128)S(1)} %add_add_fusion), channel_id=1, source_target_pairs={{0,16},{16,0},{1,17},{17,1},{2,18},{18,2},{3,19},{19,3},{4,20},{20... | collective-permute-start | bytes 786440 | tf_op jit(solution)/shard_map/ppermute | solution.py:49
  138.6 0.7 copy-start
  139.3 7.8 %collective-permute-start.27 = (f32[4,128,128]{2,1,0:T(8,128)S(1)}, f32[4,128,128]{2,1,0:T(8,128)S(1)}, u32[]{:S(2)}, u32[]{:S(2)}) collective-permute-start(f32[4,128,128]{2,1,0:T(8,128)S(1)} %add.177), channel_id=1, source_target_pairs={{0,32},{32,0},{64,96},{96,64},{128,160},{160,128},{192,224},{224,1... | collective-permute-start | bytes 786440 | tf_op jit(solution)/shard_map/ppermute | solution.py:72
  147.1 0.7 copy-start.1
  147.9 13.9 %collective-permute-start.28 = (f32[4,128,128]{2,1,0:T(8,128)S(1)}, f32[4,128,128]{2,1,0:T(8,128)S(1)}, u32[]{:S(2)}, u32[]{:S(2)}) collective-permute-start(f32[4,128,128]{2,1,0:T(8,128)S(1)} %add.178), channel_id=1, source_target_pairs={{0,64},{32,96},{64,0},{96,32},{128,192},{160,224},{192,128},{224,1... | collective-permute-start | bytes 786440 | tf_op jit(solution)/shard_map/ppermute | solution.py:72
  161.8 4.0 %copy-start.2 = (f32[4,128,128]{2,1,0:T(8,128)}, f32[4,128,128]{2,1,0:T(8,128)S(1)}, u32[]{:S(2)}) copy-start(f32[4,128,128]{2,1,0:T(8,128)S(1)} %collective-permute-done.28) | copy-start | bytes 786436
  162.5 13.2 %collective-permute-start.29 = (f32[4,128,128]{2,1,0:T(8,128)}, f32[4,128,128]{2,1,0:T(8,128)}, u32[]{:S(2)}, u32[]{:S(2)}) collective-permute-start(f32[4,128,128]{2,1,0:T(8,128)} %add.180), channel_id=1, source_target_pairs={{0,128},{32,160},{64,192},{96,224},{128,0},{160,32},{192,64},{224,... | collective-permute-start | bytes 786440 | tf_op jit(solution)/shard_map/ppermute | solution.py:72
